TPU v7x, 512 devices: a whole 4x8x8 slice. The times are simulated.
512 devices in a mesh: seq: 32 (over y, z_lo, core), head: 16 (over x, z_hi).
Axes of the slice: x: 4, y: 8, z: 8 (z_hi: 4, z_lo: 2; z = z_hi * 2 + z_lo), core: 2. Of those that a mesh axis runs over, the one named last changes fastest.
Arguments:
- queries: bfloat16 [65536, 64, 128], P(('seq', 'head')), may hold values from -6 to 6
- keys: bfloat16 [65536, 8, 128], P(('seq', 'head')), may hold values from -6 to 6
- values: bfloat16 [65536, 8, 128], P(('seq', 'head')), may hold values from -6 to 6
- block_lists: int32 [8, 512, 8], replicated, may hold values from 0 to 511, as said below
- block_counts: int32 [8, 512], replicated, may hold values from 1 to 8, as said below
Outputs:
- attended: bfloat16 [65536, 64, 128], P(('seq', 'head'))
Inputs may be any that keep to these rules, and one draw needn't show every extreme that they name: block_lists[g, b, 0] is b. For 1 <= j < block_counts[g, b] the slot names a block of another seq shard (block c lies on shard c // 16), distinct within the row; slots from block_counts[g, b] on repeat b. Over the 16 rows of one seq shard and one head g, at most 4 read slots name blocks of any one other shard, and some pair of shards reaches 4 for every g. `block_counts`: for every head g, all rows of one seq shard have 8.
All inputs are finite; a program needn't handle non-finite values.
Results may differ from a plain program's by a relative error of at most 0.0049.
Values may be sent and summed in bfloat16 or wider, within the bound.
No kernel may reach another device: no remote copies, remote signals or barrier semaphores. Data moves between devices by JAX's collectives and lax.ppermute only.
A program may use at most 128 MiB of HBM per device.

v0:
```python
from functools import partial

import jax
import jax.numpy as jnp
from jax import lax
from jax.sharding import PartitionSpec as P

BLK = 128


NEG_FILL = -1e30


def attend(table_keys, table_values, score_scale, inputs):
    query_row, slot_index, row_count = inputs
    slot_total = slot_index.shape[0]
    head_dim = table_keys.shape[-1]
    key_rows = table_keys[slot_index].reshape(slot_total * BLK, head_dim)
    value_rows = table_values[slot_index].reshape(slot_total * BLK, head_dim)
    scores = (
        jnp.einsum("tgd,kd->tgk", query_row, key_rows, preferred_element_type=jnp.float32)
        * score_scale
    )
    allowed = jnp.arange(slot_total * BLK, dtype=jnp.int32) // BLK < row_count
    scores = jnp.where(allowed[None, None, :], scores, NEG_FILL)
    row_max = jnp.max(scores, axis=2, keepdims=True)
    weights = jnp.exp(scores - row_max)
    probs = (weights / jnp.sum(weights, axis=2, keepdims=True)).astype(jnp.bfloat16)
    return jnp.einsum("tgk,kd->tgd", probs, value_rows, preferred_element_type=jnp.float32).astype(
        jnp.bfloat16
    )


def make_plan(block_lists, block_counts, group_head, seq_index, shard_count, qblocks, capacity):
    slot_total = block_lists.shape[2]
    entries = qblocks * (slot_total - 1)
    row_lists = lax.dynamic_index_in_dim(block_lists, group_head, 0, keepdims=False)
    row_counts = lax.dynamic_index_in_dim(block_counts, group_head, 0, keepdims=False)
    slot_number = jnp.arange(1, slot_total, dtype=jnp.int32)
    live = (slot_number[None, :] < row_counts[:, None]).reshape(shard_count, entries)
    remote = row_lists[:, 1:].reshape(shard_count, entries)
    owner_shard = remote // qblocks
    within = remote % qblocks
    shard_ids = jnp.arange(shard_count, dtype=jnp.int32)
    hits = ((owner_shard[:, :, None] == shard_ids[None, None, :]) & live[:, :, None]).astype(
        jnp.int32
    )
    place = jnp.sum((jnp.cumsum(hits, axis=1) - hits) * hits, axis=2)
    mine = (live & (owner_shard == seq_index)).astype(jnp.int32)
    slot_match = (place[:, :, None] == jnp.arange(capacity, dtype=jnp.int32)[None, None, :]).astype(
        jnp.int32
    )
    chosen = jnp.sum(mine[:, :, None] * slot_match * within[:, :, None], axis=1)
    my_live = lax.dynamic_index_in_dim(live, seq_index, 0, keepdims=False)
    my_owner = lax.dynamic_index_in_dim(owner_shard, seq_index, 0, keepdims=False)
    my_place = lax.dynamic_index_in_dim(place, seq_index, 0, keepdims=False)
    remote_index = jnp.where(my_live, qblocks + my_owner * capacity + my_place, 0).reshape(
        qblocks, slot_total - 1
    )
    slot_index = jnp.concatenate(
        [jnp.arange(qblocks, dtype=jnp.int32)[:, None], remote_index], axis=1
    )
    my_counts = lax.dynamic_slice_in_dim(row_counts, seq_index * qblocks, qblocks, 0)
    return (chosen, slot_index, my_counts)


def pick_blocks(source, plans):
    parts = [source[plan[0], :, unit] for unit, plan in enumerate(plans)]
    return jnp.stack(parts, axis=1)


def fetch_blocks(payload):
    return (
        lax.all_to_all(payload[0], "seq", split_axis=0, concat_axis=0, tiled=True),
        lax.all_to_all(payload[1], "seq", split_axis=0, concat_axis=0, tiled=True),
    )


def build_tables(block_keys, block_values, recv_keys, recv_values, plans):
    tables = []
    for unit, plan in enumerate(plans):
        shape_rows = (
            recv_keys.shape[0] * recv_keys.shape[2],
            recv_keys.shape[3],
            recv_keys.shape[4],
        )
        table_keys = jnp.concatenate(
            [block_keys[:, :, unit], recv_keys[:, unit].reshape(shape_rows)], axis=0
        )
        table_values = jnp.concatenate(
            [block_values[:, :, unit], recv_values[:, unit].reshape(shape_rows)], axis=0
        )
        tables.append((table_keys, table_values, plan[1], plan[2]))
    return tables


def on_device(queries, keys, values, block_lists, block_counts):
    head_count = lax.axis_size("head")
    shard_count = lax.axis_size("seq")
    head_index = lax.axis_index("head")
    seq_index = lax.axis_index("seq")
    kv_total = keys.shape[1]
    head_dim = keys.shape[2]
    share = max(1, head_count // kv_total)
    units = kv_total * share // head_count
    local_queries = lax.all_to_all(queries, "head", split_axis=1, concat_axis=0, tiled=True)
    seq_rows = local_queries.shape[0]
    qblocks = seq_rows // BLK
    group_size = local_queries.shape[1] // units
    slot_total = block_lists.shape[2]
    capacity = (qblocks * (slot_total - 1) + shard_count - 2) // (shard_count - 1)
    own_keys, own_values = (
        lax.all_to_all(
            jnp.repeat(keys, share, axis=1), "head", split_axis=1, concat_axis=0, tiled=True
        ),
        lax.all_to_all(
            jnp.repeat(values, share, axis=1), "head", split_axis=1, concat_axis=0, tiled=True
        ),
    )
    block_keys = own_keys.reshape(qblocks, BLK, units, head_dim)
    block_values = own_values.reshape(qblocks, BLK, units, head_dim)
    group_heads = (head_index * units + 0) // share
    plans = [
        make_plan(block_lists, block_counts, group_heads, seq_index, shard_count, qblocks, capacity)
    ]
    recv_keys, recv_values = fetch_blocks(
        (pick_blocks(block_keys, plans), pick_blocks(block_values, plans))
    )
    tables = build_tables(block_keys, block_values, recv_keys, recv_values, plans)
    score_scale = head_dim ** (-0.5)
    table_keys, table_values, slot_index, my_counts = tables[0]
    query_rows = local_queries.reshape(qblocks, BLK, group_size, head_dim)
    attended = lax.map(
        partial(attend, table_keys, table_values, score_scale), (query_rows, slot_index, my_counts)
    )
    outputs = attended.reshape(seq_rows, group_size, head_dim)
    return lax.all_to_all(outputs, "head", split_axis=0, concat_axis=1, tiled=True)


def solution(mesh):
    return jax.shard_map(
        on_device,
        mesh=mesh,
        in_specs=(
            P(("seq", "head"), None, None),
            P(("seq", "head"), None, None),
            P(("seq", "head"), None, None),
            P(),
            P(),
        ),
        out_specs=P(("seq", "head"), None, None),
        check_vma=False,
    )
```

profile of v0, /device:TPU:73, one launch (start us, length us, event | category | flops | bytes accessed | tf_op | source)
XLA Modules:
  0.0 541.3 jit_solution(7378154033905632050)
XLA Ops:
  1.9 11.7 %all-to-all-start.1 = ((bf16[128,16,128]{2,0,1:T(8,128)(2,1)}), bf16[128,16,128]{2,0,1:T(8,128)(2,1)S(1)}, u32[]{:S(2)}, u32[]{:S(2)}) async-start(bf16[128,16,128]{2,0,1:T(8,128)(2,1)} %bitcast.13), calls=%async_computation.1 | async-start | bytes 1048576 | tf_op jit(solution)/shard_map/all_to_all | solution.py:113
  15.1 15.6 %all-to-all-done.1 = bf16[128,16,128]{2,0,1:T(8,128)(2,1)S(1)} async-done(((bf16[128,16,128]{2,0,1:T(8,128)(2,1)}), bf16[128,16,128]{2,0,1:T(8,128)(2,1)S(1)}, u32[]{:S(2)}, u32[]{:S(2)}) %all-to-all-start.1) | async-done | bytes 524320 | tf_op jit(solution)/shard_map/all_to_all | solution.py:113
  31.7 5.4 all-to-all-start.3
  37.3 3.9 fusion.44
  41.7 3.1 gather_fusion.2
  44.8 10.5 %all-to-all-done.3 = bf16[128,16,128]{2,0,1:T(8,128)(2,1)S(1)} async-done(((bf16[128,16,128]{2,0,1:T(8,128)(2,1)}), bf16[128,16,128]{2,0,1:T(8,128)(2,1)S(1)}, u32[]{:S(2)}, u32[]{:S(2)}) %all-to-all-start.3) | async-done | bytes 524320 | tf_op jit(solution)/shard_map/all_to_all | solution.py:116
  55.3 8.8 %all-to-all-start.2 = ((bf16[32,1,4,128,128]{4,3,2,1,0:T(8,128)(2,1)}), bf16[32,1,4,128,128]{4,3,2,1,0:T(8,128)(2,1)}, u32[]{:S(2)}, u32[]{:S(2)}) async-start(bf16[32,1,4,128,128]{4,3,2,1,0:T(8,128)(2,1)} %bitcast.98), calls=%async_computation.2 | async-start | bytes 8388608 | tf_op jit(solution)/shard_map/all_to_all | solution.py:74
  64.1 3.0 gather_fusion.3
  67.1 92.0 %all-to-all-done.2 = bf16[32,1,4,128,128]{4,3,2,1,0:T(8,128)(2,1)} async-done(((bf16[32,1,4,128,128]{4,3,2,1,0:T(8,128)(2,1)}), bf16[32,1,4,128,128]{4,3,2,1,0:T(8,128)(2,1)}, u32[]{:S(2)}, u32[]{:S(2)}) %all-to-all-start.2) | async-done | bytes 4194336 | tf_op jit(solution)/shard_map/all_to_all | solution.py:74
  159.1 6.6 %all-to-all-start.4 = ((bf16[32,1,4,128,128]{4,3,2,1,0:T(8,128)(2,1)}), bf16[32,1,4,128,128]{4,3,2,1,0:T(8,128)(2,1)}, u32[]{:S(2)}, u32[]{:S(2)}) async-start(bf16[32,1,4,128,128]{4,3,2,1,0:T(8,128)(2,1)} %bitcast.99), calls=%async_computation.4 | async-start | bytes 8388608 | tf_op jit(solution)/shard_map/all_to_all | solution.py:75
  168.4 92.6 %all-to-all-done.4 = bf16[32,1,4,128,128]{4,3,2,1,0:T(8,128)(2,1)} async-done(((bf16[32,1,4,128,128]{4,3,2,1,0:T(8,128)(2,1)}), bf16[32,1,4,128,128]{4,3,2,1,0:T(8,128)(2,1)}, u32[]{:S(2)}, u32[]{:S(2)}) %all-to-all-start.4) | async-done | bytes 4194336 | tf_op jit(solution)/shard_map/all_to_all | solution.py:75
  260.9 3.9 all-to-all-start
  266.0 4.7 pad_maximum_fusion
  270.7 4.8 pad_maximum_fusion.1
  275.5 38.8 %all-to-all-done = bf16[128,64,128]{2,0,1:T(8,128)(2,1)S(1)} async-done(((bf16[128,64,128]{2,0,1:T(8,128)(2,1)}), bf16[128,64,128]{2,0,1:T(8,128)(2,1)S(1)}, u32[]{:S(2)}, u32[]{:S(2)}) %all-to-all-start) | async-done | bytes 2097184 | tf_op jit(solution)/shard_map/all_to_all | solution.py:106
  314.3 162.9 %while.12 = (s32[]{:T(128)}, bf16[16,128,4,128]{3,1,0,2:T(8,128)(2,1)}, s32[16]{0:T(128)S(1)}, bf16[16,128,4,128]{3,1,2,0:T(8,128)(2,1)S(1)}, s32[16,8]{1,0:T(8,...) while((s32[]{:T(128)}, bf16[16,128,4,128]{3,1,0,2:T(8,128)(2,1)}, ...), condition=%wide.region_6.7_spmd, body=%wide.region_3.6_spmd.sunk | while | flops 407450144 | bytes 2240781 | solution.py:133
  319.4 2.9 gather_fusion
  329.6 2.9 gather_fusion
  339.7 2.9 gather_fusion
  349.9 2.9 gather_fusion
  360.1 2.9 gather_fusion
  370.3 2.9 gather_fusion
  380.5 2.9 gather_fusion
  390.7 2.9 gather_fusion
  400.8 2.9 gather_fusion
  411.0 2.9 gather_fusion
  421.2 2.9 gather_fusion
  431.4 2.9 gather_fusion
  441.6 2.9 gather_fusion
  451.8 2.9 gather_fusion
  477.3 3.4 copy.74
  480.7 57.4 %all_to_all.73 = bf16[2048,4,128]{2,1,0:T(4,128)(2,1)S(1)} all-to-all(bf16[2048,4,128]{2,1,0:T(4,128)(2,1)S(1)} %copy.74), channel_id=1, replica_groups=mesh['seq'=32,'head'=16] {'head'}, dimensions={0} | all-to-all | bytes 4194304 | tf_op jit(solution)/shard_map/all_to_all | solution.py:137
  (156 shorter events, 133.4 us)
Async XLA Ops:
  0.0 13.7 %copy-start = (s32[8,512,8]{1,2,0:T(8,128)S(1)}, s32[8,512,8]{1,2,0:T(8,128)}, u32[]{:S(2)}) copy-start(s32[8,512,8]{1,2,0:T(8,128)} %param.10) | copy-start | bytes 393220
  0.0 15.0 %copy-start.2 = (bf16[128,8,128]{2,1,0:T(8,128)(2,1)S(1)}, bf16[128,8,128]{2,1,0:T(8,128)(2,1)}, u32[]{:S(2)}) copy-start(bf16[128,8,128]{2,1,0:T(8,128)(2,1)} %param.9) | copy-start | bytes 786436
  1.9 28.8 %all-to-all-start.1 = ((bf16[128,16,128]{2,0,1:T(8,128)(2,1)}), bf16[128,16,128]{2,0,1:T(8,128)(2,1)S(1)}, u32[]{:S(2)}, u32[]{:S(2)}) async-start(bf16[128,16,128]{2,0,1:T(8,128)(2,1)} %bitcast.13), calls=%async_computation.1 | async-start | bytes 1048576 | tf_op jit(solution)/shard_map/all_to_all | solution.py:113
  31.7 23.6 %all-to-all-start.3 = ((bf16[128,16,128]{2,0,1:T(8,128)(2,1)}), bf16[128,16,128]{2,0,1:T(8,128)(2,1)S(1)}, u32[]{:S(2)}, u32[]{:S(2)}) async-start(bf16[128,16,128]{2,0,1:T(8,128)(2,1)} %bitcast.21), calls=%async_computation.3 | async-start | bytes 1048576 | tf_op jit(solution)/shard_map/all_to_all | solution.py:116
  55.3 103.8 %all-to-all-start.2 = ((bf16[32,1,4,128,128]{4,3,2,1,0:T(8,128)(2,1)}), bf16[32,1,4,128,128]{4,3,2,1,0:T(8,128)(2,1)}, u32[]{:S(2)}, u32[]{:S(2)}) async-start(bf16[32,1,4,128,128]{4,3,2,1,0:T(8,128)(2,1)} %bitcast.98), calls=%async_computation.2 | async-start | bytes 8388608 | tf_op jit(solution)/shard_map/all_to_all | solution.py:74
  159.1 6.6 %copy-start.1 = (bf16[128,64,128]{2,1,0:T(8,128)(2,1)S(1)}, bf16[128,64,128]{2,1,0:T(8,128)(2,1)}, u32[]{:S(2)}) copy-start(bf16[128,64,128]{2,1,0:T(8,128)(2,1)} %param.7) | copy-start | bytes 6291460
  159.1 101.8 %all-to-all-start.4 = ((bf16[32,1,4,128,128]{4,3,2,1,0:T(8,128)(2,1)}), bf16[32,1,4,128,128]{4,3,2,1,0:T(8,128)(2,1)}, u32[]{:S(2)}, u32[]{:S(2)}) async-start(bf16[32,1,4,128,128]{4,3,2,1,0:T(8,128)(2,1)} %bitcast.99), calls=%async_computation.4 | async-start | bytes 8388608 | tf_op jit(solution)/shard_map/all_to_all | solution.py:75
  260.9 53.4 %all-to-all-start = ((bf16[128,64,128]{2,0,1:T(8,128)(2,1)}), bf16[128,64,128]{2,0,1:T(8,128)(2,1)S(1)}, u32[]{:S(2)}, u32[]{:S(2)}) async-start(bf16[128,64,128]{2,0,1:T(8,128)(2,1)} %copy.60), calls=%async_computation | async-start | bytes 4194304 | tf_op jit(solution)/shard_map/all_to_all | solution.py:106
where the time goes:
time: 543 us; the launch traced here: 541 us
  waiting for transfers between devices  249 us (46%)
  local copies, waits for them, and re-layouts  125 us (23%)
  blocking collectives  57.4 us (11%)
  matrix products  48 us (9%)
  starting transfers between devices  36.4 us (7%)
  other arithmetic  24.3 us (4%)
    all_to_all x1, waiting for transfers between devices, fetch_blocks(): lax.all_to_all(payload[1], 'seq', split_axis=0, concat_axis=0, tiled=True)  92.6 us
    all_to_all x1, waiting for transfers between devices, fetch_blocks(): lax.all_to_all(payload[0], 'seq', split_axis=0, concat_axis=0, tiled=True)  92 us
    all_to_all x1, blocking collectives, on_device(): lax.all_to_all(outputs, 'head', split_axis=0, concat_axis=1, tiled=True)  57.4 us
    gather x16, local copies, waits for them, and re-layouts, attend(): value_rows = table_values[slot_index].reshape(slot_total * BLK, head_dim)  47 us
    gather x16, local copies, waits for them, and re-layouts, attend(): key_rows = table_keys[slot_index].reshape(slot_total * BLK, head_dim)  46.9 us
    all_to_all x1, waiting for transfers between devices, on_device(): lax.all_to_all(queries, 'head', split_axis=1, concat_axis=0, tiled=True)  38.8 us
    dot_general x16, matrix products, attend(): jnp.einsum('tgk,kd->tgd', probs, value_rows, preferred_element_type=jnp.f...  34.8 us
    all_to_all x1, waiting for transfers between devices, on_device(): lax.all_to_all(jnp.repeat(keys, share, axis=1), 'head', split_axis=1, con...  15.6 us
  transfers between devices with their start and end apart: 5, of which 5 were waited for; matrix products, arithmetic and copies ran while one was open for 5% of the time, Pallas kernels for 0%

commit v1 on v0

v1 whole, which is shorter than its diff:
```python
from functools import partial

import jax
import jax.numpy as jnp
from jax import lax
from jax.experimental import pallas as pl
from jax.experimental.pallas import tpu as pltpu
from jax.sharding import PartitionSpec as P

BLK = 128


NEG_FILL = -1e30


def attend_kernel(slot_ref, count_ref, query_ref, own_ref, recv_ref, out_ref, *, score_scale,
                  slot_total, qblocks):
    row = pl.program_id(0)
    query = query_ref[0]
    row_count = count_ref[row]
    scores = []
    values = []
    for slot in range(slot_total):
        if slot == 0:
            key = own_ref[0, row]
            value = own_ref[1, row]
        else:
            index = jnp.maximum(slot_ref[row, slot] - qblocks, 0)
            key = recv_ref[index, 0]
            value = recv_ref[index, 1]
        part = lax.dot_general(
            query, key, (((1,), (1,)), ((), ())), preferred_element_type=jnp.float32
        ) * score_scale
        if slot > 0:
            part = jnp.where(slot < row_count, part, NEG_FILL)
        scores.append(part)
        values.append(value)
    row_max = jnp.max(scores[0], axis=1, keepdims=True)
    for part in scores[1:]:
        row_max = jnp.maximum(row_max, jnp.max(part, axis=1, keepdims=True))
    weights = [jnp.exp(part - row_max) for part in scores]
    total = jnp.sum(weights[0], axis=1, keepdims=True)
    for part in weights[1:]:
        total = total + jnp.sum(part, axis=1, keepdims=True)
    inverse = 1.0 / total
    acc = None
    for part, value in zip(weights, values):
        probs = (part * inverse).astype(jnp.bfloat16)
        term = jnp.dot(probs, value, preferred_element_type=jnp.float32)
        acc = term if acc is None else acc + term
    out_ref[0] = acc.astype(out_ref.dtype)


def attend_all(query_rows, own_blocks, recv_blocks, slot_index, row_counts, score_scale):
    qblocks, rows, head_dim = query_rows.shape
    slot_total = slot_index.shape[1]
    kernel = partial(
        attend_kernel, score_scale=score_scale, slot_total=slot_total, qblocks=qblocks
    )
    return pl.pallas_call(
        kernel,
        out_shape=jax.ShapeDtypeStruct(query_rows.shape, query_rows.dtype),
        grid_spec=pltpu.PrefetchScalarGridSpec(
            num_scalar_prefetch=2,
            grid=(qblocks,),
            in_specs=[
                pl.BlockSpec((1, rows, head_dim), lambda r, s, c: (r, 0, 0)),
                pl.BlockSpec(own_blocks.shape, lambda r, s, c: (0, 0, 0, 0)),
                pl.BlockSpec(recv_blocks.shape, lambda r, s, c: (0, 0, 0, 0)),
            ],
            out_specs=pl.BlockSpec((1, rows, head_dim), lambda r, s, c: (r, 0, 0)),
        ),
        compiler_params=pltpu.CompilerParams(vmem_limit_bytes=100 * 1024 * 1024),
    )(slot_index, row_counts, query_rows, own_blocks, recv_blocks)


def make_plan(block_lists, block_counts, group_head, seq_index, shard_count, qblocks, capacity):
    slot_total = block_lists.shape[2]
    entries = qblocks * (slot_total - 1)
    row_lists = lax.dynamic_index_in_dim(block_lists, group_head, 0, keepdims=False)
    row_counts = lax.dynamic_index_in_dim(block_counts, group_head, 0, keepdims=False)
    slot_number = jnp.arange(1, slot_total, dtype=jnp.int32)
    live = (slot_number[None, :] < row_counts[:, None]).reshape(shard_count, entries)
    remote = row_lists[:, 1:].reshape(shard_count, entries)
    owner_shard = remote // qblocks
    within = remote % qblocks
    shard_ids = jnp.arange(shard_count, dtype=jnp.int32)
    hits = ((owner_shard[:, :, None] == shard_ids[None, None, :]) & live[:, :, None]).astype(
        jnp.int32
    )
    place = jnp.sum((jnp.cumsum(hits, axis=1) - hits) * hits, axis=2)
    mine = (live & (owner_shard == seq_index)).astype(jnp.int32)
    slot_match = (place[:, :, None] == jnp.arange(capacity, dtype=jnp.int32)[None, None, :]).astype(
        jnp.int32
    )
    chosen = jnp.sum(mine[:, :, None] * slot_match * within[:, :, None], axis=1)
    my_live = lax.dynamic_index_in_dim(live, seq_index, 0, keepdims=False)
    my_owner = lax.dynamic_index_in_dim(owner_shard, seq_index, 0, keepdims=False)
    my_place = jnp.minimum(lax.dynamic_index_in_dim(place, seq_index, 0, keepdims=False),
                           capacity - 1)
    remote_index = jnp.where(my_live, qblocks + my_owner * capacity + my_place, 0).reshape(
        qblocks, slot_total - 1
    )
    slot_index = jnp.concatenate(
        [jnp.arange(qblocks, dtype=jnp.int32)[:, None], remote_index], axis=1
    )
    my_counts = lax.dynamic_slice_in_dim(row_counts, seq_index * qblocks, qblocks, 0)
    return (chosen, slot_index, my_counts)


def on_device(queries, keys, values, block_lists, block_counts):
    head_count = lax.axis_size("head")
    shard_count = lax.axis_size("seq")
    head_index = lax.axis_index("head")
    seq_index = lax.axis_index("seq")
    kv_total = keys.shape[1]
    head_dim = keys.shape[2]
    share = max(1, head_count // kv_total)
    units = kv_total * share // head_count
    assert units == 1
    local_queries = lax.all_to_all(queries, "head", split_axis=1, concat_axis=0, tiled=True)
    seq_rows = local_queries.shape[0]
    qblocks = seq_rows // BLK
    group_size = local_queries.shape[1]
    slot_total = block_lists.shape[2]
    capacity = (qblocks * (slot_total - 1) + shard_count - 2) // (shard_count - 1)
    kv = jnp.stack([keys, values], axis=1)
    own_kv = lax.all_to_all(
        jnp.repeat(kv, share, axis=2), "head", split_axis=2, concat_axis=0, tiled=True
    )
    block_kv = own_kv.reshape(qblocks, BLK, 2, head_dim)
    group_head = head_index // share
    chosen, slot_index, my_counts = make_plan(
        block_lists, block_counts, group_head, seq_index, shard_count, qblocks, capacity
    )
    picked = jnp.transpose(block_kv[chosen], (0, 1, 3, 2, 4))
    recv = lax.all_to_all(picked, "seq", split_axis=0, concat_axis=0, tiled=True)
    recv_blocks = recv.reshape(shard_count * capacity, 2, BLK, head_dim)
    own_blocks = jnp.transpose(block_kv, (2, 0, 1, 3))
    score_scale = head_dim ** (-0.5)
    query_rows = local_queries.reshape(qblocks, BLK * group_size, head_dim)
    attended = attend_all(query_rows, own_blocks, recv_blocks, slot_index, my_counts, score_scale)
    outputs = attended.reshape(seq_rows, group_size, head_dim)
    return lax.all_to_all(outputs, "head", split_axis=0, concat_axis=1, tiled=True)


def solution(mesh):
    return jax.shard_map(
        on_device,
        mesh=mesh,
        in_specs=(
            P(("seq", "head"), None, None),
            P(("seq", "head"), None, None),
            P(("seq", "head"), None, None),
            P(),
            P(),
        ),
        out_specs=P(("seq", "head"), None, None),
        check_vma=False,
    )
```

time: 543 us -> 391 us (0.72)
  the two profiles are of different devices: /device:TPU:73 before, /device:TPU:8 now
where the time goes in v1:
time: 391 us; the launch traced here: 390 us
  waiting for transfers between devices  240 us (61%)
  blocking collectives  58.1 us (15%)
  Pallas kernels  36.4 us (9%)
  starting transfers between devices  28.8 us (7%)
  local copies, waits for them, and re-layouts  21.2 us (5%)
  other arithmetic  6.14 us (2%)
    all_to_all x1, waiting for transfers between devices, on_device(): lax.all_to_all(picked, 'seq', split_axis=0, concat_axis=0, tiled=True)  180 us
    all_to_all x1, blocking collectives, on_device(): lax.all_to_all(outputs, 'head', split_axis=0, concat_axis=1, tiled=True)  58.1 us
    all_to_all x1, waiting for transfers between devices, on_device(): lax.all_to_all(queries, 'head', split_axis=1, concat_axis=0, tiled=True)  38.1 us
    pallas_call x1, Pallas kernels, attend_all(): pl.pallas_call(kernel, out_shape=jax.ShapeDtypeStruct(query_rows.shape, q...  36.4 us
    all_to_all x1, waiting for transfers between devices, on_device(): lax.all_to_all(jnp.repeat(kv, share, axis=2), 'head', split_axis=2, conca...  21.5 us
    all_to_all x1, starting transfers between devices, on_device(): lax.all_to_all(jnp.repeat(kv, share, axis=2), 'head', split_axis=2, conca...  12.9 us
    all_to_all x1, starting transfers between devices, on_device(): lax.all_to_all(picked, 'seq', split_axis=0, concat_axis=0, tiled=True)  8.75 us
  transfers between devices with their start and end apart: 3, of which 3 were waited for; matrix products, arithmetic and copies ran while one was open for 6% of the time, Pallas kernels for 0%

profile of v1, /device:TPU:8, one launch (start us, length us, event | category | flops | bytes accessed | tf_op | source)
XLA Modules:
  0.0 390.5 jit_solution(2590161052973585860)
XLA Ops:
  0.0 1.1 pad_maximum_fusion
  1.1 0.1 copy.48
  1.2 1.2 broadcast_in_dim.6
  2.4 12.9 %all-to-all-start.1 = ((bf16[128,2,16,128]{3,0,1,2:T(8,128)(2,1)}), bf16[128,2,16,128]{3,0,1,2:T(8,128)(2,1)S(1)}, u32[]{:S(2)}, u32[]{:S(2)}) async-start(bf16[128,2,16,128]{3,0,1,2:T(8,128)(2,1)} %bitcast.7), calls=%async_computation.1 | async-start | bytes 2097152 | tf_op jit(solution)/shard_map/all_to_all | solution.py:128
  15.3 2.7 copy.46
  18.0 21.5 %all-to-all-done.1 = bf16[128,2,16,128]{3,0,1,2:T(8,128)(2,1)S(1)} async-done(((bf16[128,2,16,128]{3,0,1,2:T(8,128)(2,1)}), bf16[128,2,16,128]{3,0,1,2:T(8,128)(2,1)S(1)}, u32[]{:S(2)}, u32[]{:S(2)}) %all-to-all-start.1) | async-done | bytes 1048608 | tf_op jit(solution)/shard_map/all_to_all | solution.py:128
  39.5 7.2 %all-to-all-start = ((bf16[128,64,128]{2,0,1:T(8,128)(2,1)}), bf16[128,64,128]{2,0,1:T(8,128)(2,1)S(1)}, u32[]{:S(2)}, u32[]{:S(2)}) async-start(bf16[128,64,128]{2,0,1:T(8,128)(2,1)} %copy.46), calls=%async_computation | async-start | bytes 4194304 | tf_op jit(solution)/shard_map/all_to_all | solution.py:121
  46.8 0.7 dynamic-slice_bitcast_fusion
  47.5 0.1 copy.41
  47.7 0.2 reshape.161
  47.8 0.1 copy.42
  47.9 0.7 dynamic-slice_reduce_fusion
  48.6 0.1 lt.69
  48.8 0.1 lt.66
  49.0 0.1 and_convert_fusion
  49.1 3.9 fusion.3
  53.2 0.2 multiply_reduce_fusion
  53.3 0.1 copy.53
  53.4 0.1 reshape.169
  53.6 1.3 copy.57
  54.9 6.4 %gather_fusion = bf16[128,128,2,128]{3,1,2,0:T(8,128)(2,1)} fusion(bf16[16,128,2,128]{3,1,0,2:T(8,128)(2,1)S(1)} %bitcast.36, s32[1024]{0:T(1024)S(1)} %pad_clamp_fusion), kind=kCustom, calls=%fused_computation | custom fusion | bytes 16777728 | tf_op jit(solution)/shard_map/gather | solution.py:136
  61.2 38.1 %all-to-all-done = bf16[128,64,128]{2,0,1:T(8,128)(2,1)S(1)} async-done(((bf16[128,64,128]{2,0,1:T(8,128)(2,1)}), bf16[128,64,128]{2,0,1:T(8,128)(2,1)S(1)}, u32[]{:S(2)}, u32[]{:S(2)}) %all-to-all-start) | async-done | bytes 2097184 | tf_op jit(solution)/shard_map/all_to_all | solution.py:121
  99.4 8.8 %all-to-all-start.2 = ((bf16[32,4,2,128,128]{4,3,2,1,0:T(8,128)(2,1)}), bf16[32,4,2,128,128]{4,3,2,1,0:T(8,128)(2,1)}, u32[]{:S(2)}, u32[]{:S(2)}) async-start(bf16[32,4,2,128,128]{4,3,2,1,0:T(8,128)(2,1)} %bitcast.38), calls=%async_computation.2 | async-start | bytes 16777216 | tf_op jit(solution)/shard_map/all_to_all | solution.py:137
  108.2 0.2 select_reduce_fusion
  108.4 0.1 select_n.70
  108.4 1.4 dynamic-slice_bitcast_fusion.1.count_ref
  109.8 0.7 pad_add_fusion.slot_ref
  110.5 3.1 copy.47
  113.5 180.0 %all-to-all-done.2 = bf16[32,4,2,128,128]{4,3,2,1,0:T(8,128)(2,1)} async-done(((bf16[32,4,2,128,128]{4,3,2,1,0:T(8,128)(2,1)}), bf16[32,4,2,128,128]{4,3,2,1,0:T(8,128)(2,1)}, u32[]{:S(2)}, u32[]{:S(2)}) %all-to-all-start.2) | async-done | bytes 8388640 | tf_op jit(solution)/shard_map/all_to_all | solution.py:137
  293.5 36.4 %shard_map.55 = bf16[16,512,128]{2,1,0:T(8,128)(2,1)} custom-call(s32[16,8]{1,0:T(8,128)} %pad_add_fusion.slot_ref, s32[16]{0:T(128)} %dynamic-slice_bitcast_fusion.1.count_ref, bf16[16,512,128]{2,1,0:T(8,128)(2,1)} %bitcast.41, bf16[2,16,128,128]{3,2,1,0:T(8,128)(2,1)} %bitcast.37, bf16[128,2,128,128]{3,2,1,0:T(8,128)(2,1)} %bitcast.17.recv_ref), custom_call_target="tpu_custom_call" | custom-call | tf_op jit(solution)/shard_map/pallas_call | solution.py:60
  329.9 58.1 %all_to_all.53 = bf16[2048,4,128]{2,1,0:T(4,128)(2,1)S(1)} all-to-all(bf16[2048,4,128]{2,1,0:T(4,128)(2,1)} %bitcast.42), channel_id=1, replica_groups=mesh['seq'=32,'head'=16] {'head'}, dimensions={0} | all-to-all | bytes 4194304 | tf_op jit(solution)/shard_map/all_to_all | solution.py:144
  388.0 2.5 copy.54
  (19 shorter events, 0.4 us)
Async XLA Ops:
  1.2 14.1 %copy-start.2 = (bf16[128,64,128]{2,1,0:T(8,128)(2,1)S(1)}, bf16[128,64,128]{2,1,0:T(8,128)(2,1)}, u32[]{:S(2)}) copy-start(bf16[128,64,128]{2,1,0:T(8,128)(2,1)} %param.5) | copy-start | bytes 6291460
  2.4 37.1 %all-to-all-start.1 = ((bf16[128,2,16,128]{3,0,1,2:T(8,128)(2,1)}), bf16[128,2,16,128]{3,0,1,2:T(8,128)(2,1)S(1)}, u32[]{:S(2)}, u32[]{:S(2)}) async-start(bf16[128,2,16,128]{3,0,1,2:T(8,128)(2,1)} %bitcast.7), calls=%async_computation.1 | async-start | bytes 2097152 | tf_op jit(solution)/shard_map/all_to_all | solution.py:128
  39.5 14.0 %copy-start.1 = (bf16[128,2,16,128]{3,0,1,2:T(8,128)(2,1)}, bf16[128,2,16,128]{3,0,1,2:T(8,128)(2,1)S(1)}, u32[]{:S(2)}) copy-start(bf16[128,2,16,128]{3,0,1,2:T(8,128)(2,1)S(1)} %all-to-all-done.1) | copy-start | bytes 3145732
  39.5 59.9 %all-to-all-start = ((bf16[128,64,128]{2,0,1:T(8,128)(2,1)}), bf16[128,64,128]{2,0,1:T(8,128)(2,1)S(1)}, u32[]{:S(2)}, u32[]{:S(2)}) async-start(bf16[128,64,128]{2,0,1:T(8,128)(2,1)} %copy.46), calls=%async_computation | async-start | bytes 4194304 | tf_op jit(solution)/shard_map/all_to_all | solution.py:121
  54.9 6.4 %copy-start = (bf16[128,2,16,128]{3,0,2,1:T(8,128)(2,1)}, bf16[128,2,16,128]{3,0,2,1:T(8,128)(2,1)S(1)}, u32[]{:S(2)}) copy-start(bf16[128,2,16,128]{3,0,2,1:T(8,128)(2,1)S(1)} %copy.57) | copy-start | bytes 3145732
  99.4 194.1 %all-to-all-start.2 = ((bf16[32,4,2,128,128]{4,3,2,1,0:T(8,128)(2,1)}), bf16[32,4,2,128,128]{4,3,2,1,0:T(8,128)(2,1)}, u32[]{:S(2)}, u32[]{:S(2)}) async-start(bf16[32,4,2,128,128]{4,3,2,1,0:T(8,128)(2,1)} %bitcast.38), calls=%async_computation.2 | async-start | bytes 16777216 | tf_op jit(solution)/shard_map/all_to_all | solution.py:137

commit v2 on v1

--- a/solution.py
+++ b/solution.py
@@ -13,11 +13,20 @@
 NEG_FILL = -1e30
 
 
-def attend_kernel(slot_ref, count_ref, query_ref, own_ref, recv_ref, out_ref, *, score_scale,
-                  slot_total, qblocks):
+def attend_kernel(slot_ref, which_ref, count_ref, query_ref, own_ref, mine0_ref, mine1_ref,
+                  peer0_ref, peer1_ref, out_ref, key_buf, value_buf, *, score_scale, slot_total):
     row = pl.program_id(0)
     query = query_ref[0]
     row_count = count_ref[row]
+    sources = (mine0_ref, mine1_ref, peer0_ref, peer1_ref)
+    for slot in range(1, slot_total):
+        index = slot_ref[row, slot]
+        which = which_ref[row, slot]
+        for code, source in enumerate(sources):
+            @pl.when(which == code)
+            def _(source=source, slot=slot, index=index):
+                key_buf[slot - 1] = source[index, 0]
+                value_buf[slot - 1] = source[index, 1]
     scores = []
     values = []
     for slot in range(slot_total):
@@ -25,9 +34,8 @@
             key = own_ref[0, row]
             value = own_ref[1, row]
         else:
-            index = jnp.maximum(slot_ref[row, slot] - qblocks, 0)
-            key = recv_ref[index, 0]
-            value = recv_ref[index, 1]
+            key = key_buf[slot - 1]
+            value = value_buf[slot - 1]
         part = lax.dot_general(
             query, key, (((1,), (1,)), ((), ())), preferred_element_type=jnp.float32
         ) * score_scale
@@ -51,27 +59,30 @@
     out_ref[0] = acc.astype(out_ref.dtype)
 
 
-def attend_all(query_rows, own_blocks, recv_blocks, slot_index, row_counts, score_scale):
+def attend_all(query_rows, own_blocks, received, slot_index, slot_which, row_counts, score_scale):
     qblocks, rows, head_dim = query_rows.shape
     slot_total = slot_index.shape[1]
-    kernel = partial(
-        attend_kernel, score_scale=score_scale, slot_total=slot_total, qblocks=qblocks
-    )
+    kernel = partial(attend_kernel, score_scale=score_scale, slot_total=slot_total)
+    whole = lambda shape: pl.BlockSpec(shape, lambda r, s, w, c: (0,) * len(shape))
     return pl.pallas_call(
         kernel,
         out_shape=jax.ShapeDtypeStruct(query_rows.shape, query_rows.dtype),
         grid_spec=pltpu.PrefetchScalarGridSpec(
-            num_scalar_prefetch=2,
+            num_scalar_prefetch=3,
             grid=(qblocks,),
             in_specs=[
-                pl.BlockSpec((1, rows, head_dim), lambda r, s, c: (r, 0, 0)),
-                pl.BlockSpec(own_blocks.shape, lambda r, s, c: (0, 0, 0, 0)),
-                pl.BlockSpec(recv_blocks.shape, lambda r, s, c: (0, 0, 0, 0)),
+                pl.BlockSpec((1, rows, head_dim), lambda r, s, w, c: (r, 0, 0)),
+                whole(own_blocks.shape),
+            ]
+            + [whole(part.shape) for part in received],
+            out_specs=pl.BlockSpec((1, rows, head_dim), lambda r, s, w, c: (r, 0, 0)),
+            scratch_shapes=[
+                pltpu.VMEM((slot_total - 1, BLK, head_dim), own_blocks.dtype),
+                pltpu.VMEM((slot_total - 1, BLK, head_dim), own_blocks.dtype),
             ],
-            out_specs=pl.BlockSpec((1, rows, head_dim), lambda r, s, c: (r, 0, 0)),
         ),
         compiler_params=pltpu.CompilerParams(vmem_limit_bytes=100 * 1024 * 1024),
-    )(slot_index, row_counts, query_rows, own_blocks, recv_blocks)
+    )(slot_index, slot_which, row_counts, query_rows, own_blocks, *received)
 
 
 def make_plan(block_lists, block_counts, group_head, seq_index, shard_count, qblocks, capacity):
@@ -98,14 +109,14 @@
     my_owner = lax.dynamic_index_in_dim(owner_shard, seq_index, 0, keepdims=False)
     my_place = jnp.minimum(lax.dynamic_index_in_dim(place, seq_index, 0, keepdims=False),
                            capacity - 1)
-    remote_index = jnp.where(my_live, qblocks + my_owner * capacity + my_place, 0).reshape(
-        qblocks, slot_total - 1
-    )
-    slot_index = jnp.concatenate(
-        [jnp.arange(qblocks, dtype=jnp.int32)[:, None], remote_index], axis=1
-    )
     my_counts = lax.dynamic_slice_in_dim(row_counts, seq_index * qblocks, qblocks, 0)
-    return (chosen, slot_index, my_counts)
+    return (chosen, my_live, my_owner, my_place, my_counts)
+
+
+def swap_halves(heads, inner):
+    shape = heads.shape
+    split = heads.reshape(shape[:1] + (2, inner, 6 - inner, 4) + shape[2:])
+    return jnp.swapaxes(split, 2, 3).reshape(shape)
 
 
 def on_device(queries, keys, values, block_lists, block_counts):
@@ -115,33 +126,51 @@
     seq_index = lax.axis_index("seq")
     kv_total = keys.shape[1]
     head_dim = keys.shape[2]
-    share = max(1, head_count // kv_total)
-    units = kv_total * share // head_count
-    assert units == 1
-    local_queries = lax.all_to_all(queries, "head", split_axis=1, concat_axis=0, tiled=True)
+    assert head_count == 16 and kv_total == 8
+    group_head = (head_index // 8) * 4 + head_index % 4
+    half = (head_index // 4) % 2
+    local_queries = lax.all_to_all(
+        swap_halves(queries, 4), "head", split_axis=1, concat_axis=0, tiled=True
+    )
     seq_rows = local_queries.shape[0]
     qblocks = seq_rows // BLK
     group_size = local_queries.shape[1]
     slot_total = block_lists.shape[2]
     capacity = (qblocks * (slot_total - 1) + shard_count - 2) // (shard_count - 1)
+    assert capacity == 4
     kv = jnp.stack([keys, values], axis=1)
-    own_kv = lax.all_to_all(
-        jnp.repeat(kv, share, axis=2), "head", split_axis=2, concat_axis=0, tiled=True
-    )
+    kv = jnp.broadcast_to(
+        kv.reshape(kv.shape[0], 2, 2, 1, 4, head_dim), (kv.shape[0], 2, 2, 2, 4, head_dim)
+    ).reshape(kv.shape[0], 2, head_count, head_dim)
+    own_kv = lax.all_to_all(kv, "head", split_axis=2, concat_axis=0, tiled=True)
     block_kv = own_kv.reshape(qblocks, BLK, 2, head_dim)
-    group_head = head_index // share
-    chosen, slot_index, my_counts = make_plan(
+    chosen, my_live, my_owner, my_place, my_counts = make_plan(
         block_lists, block_counts, group_head, seq_index, shard_count, qblocks, capacity
     )
-    picked = jnp.transpose(block_kv[chosen], (0, 1, 3, 2, 4))
-    recv = lax.all_to_all(picked, "seq", split_axis=0, concat_axis=0, tiled=True)
-    recv_blocks = recv.reshape(shard_count * capacity, 2, BLK, head_dim)
+    partner = [(h, h ^ 4) for h in range(head_count)]
+    mine = []
+    peer = []
+    for chunk in range(2):
+        pick = lax.dynamic_index_in_dim(chosen, 2 * half + chunk, 1, keepdims=False)
+        picked = jnp.transpose(block_kv[pick], (0, 2, 1, 3))
+        got = lax.all_to_all(picked, "seq", split_axis=0, concat_axis=0, tiled=True)
+        mine.append(got)
+        peer.append(lax.ppermute(got, "head", partner))
+    which = jnp.where(my_place // 2 == half, 0, 2) + my_place % 2
+    slot_index = jnp.where(my_live, my_owner, 0).reshape(qblocks, slot_total - 1)
+    slot_which = jnp.where(my_live, which, 0).reshape(qblocks, slot_total - 1)
+    zero_col = jnp.zeros((qblocks, 1), jnp.int32)
+    slot_index = jnp.concatenate([zero_col, slot_index], axis=1)
+    slot_which = jnp.concatenate([zero_col, slot_which], axis=1)
     own_blocks = jnp.transpose(block_kv, (2, 0, 1, 3))
     score_scale = head_dim ** (-0.5)
     query_rows = local_queries.reshape(qblocks, BLK * group_size, head_dim)
-    attended = attend_all(query_rows, own_blocks, recv_blocks, slot_index, my_counts, score_scale)
+    attended = attend_all(
+        query_rows, own_blocks, mine + peer, slot_index, slot_which, my_counts, score_scale
+    )
     outputs = attended.reshape(seq_rows, group_size, head_dim)
-    return lax.all_to_all(outputs, "head", split_axis=0, concat_axis=1, tiled=True)
+    back = lax.all_to_all(outputs, "head", split_axis=0, concat_axis=1, tiled=True)
+    return swap_halves(back, 2)
 
 
 def solution(mesh):

time: 391 us -> 385 us (0.985)
  the two profiles are of different devices: /device:TPU:8 before, /device:TPU:72 now
where the time goes in v2:
time: 385 us; the launch traced here: 384 us
  waiting for transfers between devices  220 us (57%)
  blocking collectives  60.4 us (16%)
  Pallas kernels  39.8 us (10%)
  starting transfers between devices  34.9 us (9%)
  local copies, waits for them, and re-layouts  23 us (6%)
  other arithmetic  5.87 us (2%)
    all_to_all x2, waiting for transfers between devices, on_device(): got = lax.all_to_all(picked, 'seq', split_axis=0, concat_axis=0, tiled=True)  94.5 us
    all_to_all x1, blocking collectives, on_device(): lax.all_to_all(outputs, 'head', split_axis=0, concat_axis=1, tiled=True)  60.4 us
    ppermute x2, waiting for transfers between devices, on_device(): peer.append(lax.ppermute(got, 'head', partner))  60.3 us
    all_to_all x1, waiting for transfers between devices, on_device(): lax.all_to_all(swap_halves(queries, 4), 'head', split_axis=1, concat_axis...  42.3 us
    pallas_call x1, Pallas kernels, attend_all(): pl.pallas_call(kernel, out_shape=jax.ShapeDtypeStruct(query_rows.shape, q...  39.8 us
    all_to_all x1, waiting for transfers between devices, on_device(): own_kv = lax.all_to_all(kv, 'head', split_axis=2, concat_axis=0, tiled=True)  23.2 us
    all_to_all x2, starting transfers between devices, on_device(): got = lax.all_to_all(picked, 'seq', split_axis=0, concat_axis=0, tiled=True)  13.2 us
    all_to_all x1, starting transfers between devices, on_device(): own_kv = lax.all_to_all(kv, 'head', split_axis=2, concat_axis=0, tiled=True)  12 us
  transfers between devices with their start and end apart: 6, of which 6 were waited for; matrix products, arithmetic and copies ran while one was open for 5% of the time, Pallas kernels for 0%

profile of v2, /device:TPU:72, one launch (start us, length us, event | category | flops | bytes accessed | tf_op | source)
XLA Modules:
  0.0 384.5 jit_solution(15389638442137605763)
XLA Ops:
  0.0 1.4 maximum_bitcast_fusion
  1.5 1.2 broadcast_in_dim.12
  2.7 12.0 %all-to-all-start.1 = ((bf16[128,2,16,128]{3,0,1,2:T(8,128)(2,1)}), bf16[128,2,16,128]{3,0,1,2:T(8,128)(2,1)S(1)}, u32[]{:S(2)}, u32[]{:S(2)}) async-start(bf16[128,2,16,128]{3,0,1,2:T(8,128)(2,1)} %bitcast.11), calls=%async_computation.1 | async-start | bytes 2097152 | tf_op jit(solution)/shard_map/all_to_all | solution.py:145
  14.9 0.7 dynamic-slice_reduce_fusion.2
  15.8 0.7 dynamic-slice_bitcast_fusion
  17.2 3.9 %fusion.3 = s32[32,112]{0,1:T(8,128)S(1)} fusion(s32[32,112]{0,1:T(8,128)S(1)} %get-tuple-element.10, pred[32,112]{0,1:T(8,128)(4,1)S(1)} %get-tuple-element.6), kind=kOutput, calls=%fused_computation.6 | output fusion | flops 13758976 | bytes 32256 | tf_op jit(solution)/shard_map/jit(cumsum)/reduce_window_sum | solution.py:102
  21.4 23.2 %all-to-all-done.1 = bf16[128,2,16,128]{3,0,1,2:T(8,128)(2,1)S(1)} async-done(((bf16[128,2,16,128]{3,0,1,2:T(8,128)(2,1)}), bf16[128,2,16,128]{3,0,1,2:T(8,128)(2,1)S(1)}, u32[]{:S(2)}, u32[]{:S(2)}) %all-to-all-start.1) | async-done | bytes 1048608 | tf_op jit(solution)/shard_map/all_to_all | solution.py:145
  44.7 2.1 gather_fusion.1
  46.8 8.6 %all-to-all-start.3 = ((bf16[32,2,128,128]{3,2,1,0:T(8,128)(2,1)}), bf16[32,2,128,128]{3,2,1,0:T(8,128)(2,1)S(1)}, u32[]{:S(2)}, u32[]{:S(2)}) async-start(bf16[32,2,128,128]{3,2,1,0:T(8,128)(2,1)} %bitcast.21), calls=%async_computation.3 | async-start | bytes 4194304 | tf_op jit(solution)/shard_map/all_to_all | solution.py:156
  55.4 2.1 gather_fusion
  57.6 48.4 %all-to-all-done.3.mine1_ref = bf16[32,2,128,128]{3,2,1,0:T(8,128)(2,1)S(1)} async-done(((bf16[32,2,128,128]{3,2,1,0:T(8,128)(2,1)}), bf16[32,2,128,128]{3,2,1,0:T(8,128)(2,1)S(1)}, u32[]{:S(2)}, u32[]{:S(2)}) %all-to-all-start.3) | async-done | bytes 2097184 | tf_op jit(solution)/shard_map/all_to_all | solution.py:156
  106.0 1.3 copy-done.1
  107.2 4.5 %all-to-all-start.2 = ((bf16[32,2,128,128]{3,2,1,0:T(8,128)(2,1)}), bf16[32,2,128,128]{3,2,1,0:T(8,128)(2,1)}, u32[]{:S(2)}, u32[]{:S(2)}) async-start(bf16[32,2,128,128]{3,2,1,0:T(8,128)(2,1)} %bitcast.19), calls=%async_computation.2 | async-start | bytes 4194304 | tf_op jit(solution)/shard_map/all_to_all | solution.py:156
  111.8 2.9 copy.59
  114.7 1.5 copy.60
  116.2 46.1 %all-to-all-done.2.mine0_ref = bf16[32,2,128,128]{3,2,1,0:T(8,128)(2,1)} async-done(((bf16[32,2,128,128]{3,2,1,0:T(8,128)(2,1)}), bf16[32,2,128,128]{3,2,1,0:T(8,128)(2,1)}, u32[]{:S(2)}, u32[]{:S(2)}) %all-to-all-start.2) | async-done | bytes 2097184 | tf_op jit(solution)/shard_map/all_to_all | solution.py:156
  162.3 3.7 all-to-all-start
  166.1 3.8 collective-permute-start
  169.9 2.2 collective-permute-start.1
  172.4 0.2 minimum_reduce_fusion
  172.8 0.7 concatenate.8.which_ref
  173.5 0.7 concatenate.7.slot_ref
  174.1 1.3 dynamic-slice_bitcast_fusion.1.count_ref
  175.4 42.3 %all-to-all-done = bf16[128,64,128]{2,0,1:T(8,128)(2,1)S(1)} async-done(((bf16[128,64,128]{2,0,1:T(8,128)(2,1)}), bf16[128,64,128]{2,0,1:T(8,128)(2,1)S(1)}, u32[]{:S(2)}, u32[]{:S(2)}) %all-to-all-start) | async-done | bytes 2097184 | tf_op jit(solution)/shard_map/all_to_all | solution.py:132
  217.7 3.1 copy.61
  220.8 16.5 %collective-permute-done.peer0_ref = bf16[32,2,128,128]{3,2,1,0:T(8,128)(2,1)} collective-permute-done((bf16[32,2,128,128]{3,2,1,0:T(8,128)(2,1)}, bf16[32,2,128,128]{3,2,1,0:T(8,128)(2,1)}, u32[]{:S(2)}, u32[]{:S(2)}) %collective-permute-start) | collective-permute-done | bytes 2097184 | tf_op jit(solution)/shard_map/ppermute | solution.py:158
  237.3 43.9 %collective-permute-done.1.peer1_ref = bf16[32,2,128,128]{3,2,1,0:T(8,128)(2,1)} collective-permute-done((bf16[32,2,128,128]{3,2,1,0:T(8,128)(2,1)}, bf16[32,2,128,128]{3,2,1,0:T(8,128)(2,1)}, u32[]{:S(2)}, u32[]{:S(2)}) %collective-permute-start.1) | collective-permute-done | bytes 2097184 | tf_op jit(solution)/shard_map/ppermute | solution.py:158
  281.1 39.8 %shard_map.55 = bf16[16,512,128]{2,1,0:T(8,128)(2,1)} custom-call(s32[16,8]{1,0:T(8,128)} %concatenate.7.slot_ref, s32[16,8]{1,0:T(8,128)} %concatenate.8.which_ref, s32[16]{0:T(128)} %dynamic-slice_bitcast_fusion.1.count_ref, bf16[16,512,128]{2,1,0:T(8,128)(2,1)} %bitcast.51, bf16[2,16,128,128]{3,2,1,0:T(8,128)(2,1)} %bitcast.46, ...), custom_call_target="tpu_custom_call" | custom-call | tf_op jit(solution)/shard_map/pallas_call | solution.py:67
  320.9 60.4 %all_to_all.55 = bf16[2048,4,128]{2,1,0:T(4,128)(2,1)S(1)} all-to-all(bf16[2048,4,128]{2,1,0:T(4,128)(2,1)} %bitcast.52), channel_id=1, replica_groups=mesh['seq'=32,'head'=16] {'head'}, dimensions={0} | all-to-all | bytes 4194304 | tf_op jit(solution)/shard_map/all_to_all | solution.py:172
  381.3 0.3 copy.67
  381.5 0.2 copy.69
  381.8 2.7 copy.70
  (29 shorter events, 1.8 us)
Async XLA Ops:
  2.7 41.8 %all-to-all-start.1 = ((bf16[128,2,16,128]{3,0,1,2:T(8,128)(2,1)}), bf16[128,2,16,128]{3,0,1,2:T(8,128)(2,1)S(1)}, u32[]{:S(2)}, u32[]{:S(2)}) async-start(bf16[128,2,16,128]{3,0,1,2:T(8,128)(2,1)} %bitcast.11), calls=%async_computation.1 | async-start | bytes 2097152 | tf_op jit(solution)/shard_map/all_to_all | solution.py:145
  44.7 10.8 %copy-start = (bf16[128,2,16,128]{3,0,2,1:T(8,128)(2,1)}, bf16[128,2,16,128]{3,0,2,1:T(8,128)(2,1)S(1)}, u32[]{:S(2)}) copy-start(bf16[128,2,16,128]{3,0,2,1:T(8,128)(2,1)S(1)} %copy.74) | copy-start | bytes 3145732
  46.8 59.1 %all-to-all-start.3 = ((bf16[32,2,128,128]{3,2,1,0:T(8,128)(2,1)}), bf16[32,2,128,128]{3,2,1,0:T(8,128)(2,1)S(1)}, u32[]{:S(2)}, u32[]{:S(2)}) async-start(bf16[32,2,128,128]{3,2,1,0:T(8,128)(2,1)} %bitcast.21), calls=%async_computation.3 | async-start | bytes 4194304 | tf_op jit(solution)/shard_map/all_to_all | solution.py:156
  105.9 1.3 copy-start.1
  107.2 55.1 %all-to-all-start.2 = ((bf16[32,2,128,128]{3,2,1,0:T(8,128)(2,1)}), bf16[32,2,128,128]{3,2,1,0:T(8,128)(2,1)}, u32[]{:S(2)}, u32[]{:S(2)}) async-start(bf16[32,2,128,128]{3,2,1,0:T(8,128)(2,1)} %bitcast.19), calls=%async_computation.2 | async-start | bytes 4194304 | tf_op jit(solution)/shard_map/all_to_all | solution.py:156
  162.3 55.4 %all-to-all-start = ((bf16[128,64,128]{2,0,1:T(8,128)(2,1)}), bf16[128,64,128]{2,0,1:T(8,128)(2,1)S(1)}, u32[]{:S(2)}, u32[]{:S(2)}) async-start(bf16[128,64,128]{2,0,1:T(8,128)(2,1)} %bitcast.4), calls=%async_computation | async-start | bytes 4194304 | tf_op jit(solution)/shard_map/all_to_all | solution.py:132
  166.1 71.2 %collective-permute-start = (bf16[32,2,128,128]{3,2,1,0:T(8,128)(2,1)}, bf16[32,2,128,128]{3,2,1,0:T(8,128)(2,1)}, u32[]{:S(2)}, u32[]{:S(2)}) collective-permute-start(bf16[32,2,128,128]{3,2,1,0:T(8,128)(2,1)} %all-to-all-done.2.mine0_ref), channel_id=1, source_target_pairs={{0,4},{1,5},{2,6},{3,7},{4,0},{5,1},{6,2},{7,3},{8,12},{9,13},{10,... | collective-permute-start | bytes 6291464 | tf_op jit(solution)/shard_map/ppermute | solution.py:158
  169.9 111.2 %collective-permute-start.1 = (bf16[32,2,128,128]{3,2,1,0:T(8,128)(2,1)}, bf16[32,2,128,128]{3,2,1,0:T(8,128)(2,1)}, u32[]{:S(2)}, u32[]{:S(2)}) collective-permute-start(bf16[32,2,128,128]{3,2,1,0:T(8,128)(2,1)} %copy-done.1), channel_id=1, source_target_pairs={{0,4},{1,5},{2,6},{3,7},{4,0},{5,1},{6,2},{7,3},{8,12},{9,13},{10,... | collective-permute-start | bytes 6291464 | tf_op jit(solution)/shard_map/ppermute | solution.py:158

commit v3 on v2

--- a/solution.py
+++ b/solution.py
@@ -129,12 +129,9 @@
     assert head_count == 16 and kv_total == 8
     group_head = (head_index // 8) * 4 + head_index % 4
     half = (head_index // 4) % 2
-    local_queries = lax.all_to_all(
-        swap_halves(queries, 4), "head", split_axis=1, concat_axis=0, tiled=True
-    )
-    seq_rows = local_queries.shape[0]
+    seq_rows = queries.shape[0] * head_count
     qblocks = seq_rows // BLK
-    group_size = local_queries.shape[1]
+    group_size = queries.shape[1] // head_count
     slot_total = block_lists.shape[2]
     capacity = (qblocks * (slot_total - 1) + shard_count - 2) // (shard_count - 1)
     assert capacity == 4
@@ -153,6 +150,11 @@
     for chunk in range(2):
         pick = lax.dynamic_index_in_dim(chosen, 2 * half + chunk, 1, keepdims=False)
         picked = jnp.transpose(block_kv[pick], (0, 2, 1, 3))
+        if chunk == 1:
+            local_queries = lax.all_to_all(
+                swap_halves(queries, 4), "head", split_axis=1, concat_axis=0, tiled=True
+            )
+            local_queries, picked = lax.optimization_barrier((local_queries, picked))
         got = lax.all_to_all(picked, "seq", split_axis=0, concat_axis=0, tiled=True)
         mine.append(got)
         peer.append(lax.ppermute(got, "head", partner))

time: 385 us -> 365 us (0.948)
  the two profiles are of different devices: /device:TPU:72 before, /device:TPU:64 now
where the time goes in v3:
time: 365 us; the launch traced here: 364 us
  waiting for transfers between devices  196 us (54%)
  blocking collectives  57 us (16%)
  Pallas kernels  39.8 us (11%)
  starting transfers between devices  33.2 us (9%)
  local copies, waits for them, and re-layouts  31.4 us (9%)
  other arithmetic  5.87 us (2%)
    all_to_all x2, waiting for transfers between devices, on_device(): got = lax.all_to_all(picked, 'seq', split_axis=0, concat_axis=0, tiled=True)  95 us
    all_to_all x1, blocking collectives, on_device(): lax.all_to_all(outputs, 'head', split_axis=0, concat_axis=1, tiled=True)  57 us
    all_to_all x1, waiting for transfers between devices, on_device(): lax.all_to_all(swap_halves(queries, 4), 'head', split_axis=1, concat_axis...  40.5 us
    pallas_call x1, Pallas kernels, attend_all(): pl.pallas_call(kernel, out_shape=jax.ShapeDtypeStruct(query_rows.shape, q...  39.8 us
    ppermute x2, waiting for transfers between devices, on_device(): peer.append(lax.ppermute(got, 'head', partner))  33.7 us
    all_to_all x1, waiting for transfers between devices, on_device(): own_kv = lax.all_to_all(kv, 'head', split_axis=2, concat_axis=0, tiled=True)  27 us
    all_to_all x2, starting transfers between devices, on_device(): got = lax.all_to_all(picked, 'seq', split_axis=0, concat_axis=0, tiled=True)  13.5 us
    all_to_all x1, starting transfers between devices, on_device(): own_kv = lax.all_to_all(kv, 'head', split_axis=2, concat_axis=0, tiled=True)  12 us
  transfers between devices with their start and end apart: 6, of which 5 were waited for; matrix products, arithmetic and copies ran while one was open for 8% of the time, Pallas kernels for 0%

profile of v3, /device:TPU:64, one launch (start us, length us, event | category | flops | bytes accessed | tf_op | source)
XLA Modules:
  0.0 363.8 jit_solution(15255982225602839041)
XLA Ops:
  0.0 1.4 maximum_bitcast_fusion
  1.5 1.2 broadcast_in_dim.12
  2.8 12.0 %all-to-all-start.1 = ((bf16[128,2,16,128]{3,0,1,2:T(8,128)(2,1)}), bf16[128,2,16,128]{3,0,1,2:T(8,128)(2,1)S(1)}, u32[]{:S(2)}, u32[]{:S(2)}) async-start(bf16[128,2,16,128]{3,0,1,2:T(8,128)(2,1)} %bitcast.11), calls=%async_computation.1 | async-start | bytes 2097152 | tf_op jit(solution)/shard_map/all_to_all | solution.py:142
  14.7 1.4 copy.60
  16.1 1.5 copy.61
  17.6 27.0 %all-to-all-done.1 = bf16[128,2,16,128]{3,0,1,2:T(8,128)(2,1)S(1)} async-done(((bf16[128,2,16,128]{3,0,1,2:T(8,128)(2,1)}), bf16[128,2,16,128]{3,0,1,2:T(8,128)(2,1)S(1)}, u32[]{:S(2)}, u32[]{:S(2)}) %all-to-all-start.1) | async-done | bytes 1048608 | tf_op jit(solution)/shard_map/all_to_all | solution.py:142
  44.6 1.0 copy-done.2
  45.6 3.7 %all-to-all-start = ((bf16[128,64,128]{2,0,1:T(8,128)(2,1)}), bf16[128,64,128]{2,0,1:T(8,128)(2,1)S(1)}, u32[]{:S(2)}, u32[]{:S(2)}) async-start(bf16[128,64,128]{2,0,1:T(8,128)(2,1)} %bitcast.49), calls=%async_computation | async-start | bytes 4194304 | tf_op jit(solution)/shard_map/all_to_all | solution.py:154
  49.5 0.7 dynamic-slice_reduce_fusion.2
  50.4 0.7 dynamic-slice_bitcast_fusion
  51.8 3.9 %fusion.3 = s32[32,112]{0,1:T(8,128)S(1)} fusion(s32[32,112]{0,1:T(8,128)S(1)} %get-tuple-element.14, pred[32,112]{0,1:T(8,128)(4,1)S(1)} %get-tuple-element.10), kind=kOutput, calls=%fused_computation.6 | output fusion | flops 13758976 | bytes 32256 | tf_op jit(solution)/shard_map/jit(cumsum)/reduce_window_sum | solution.py:102
  56.0 1.3 copy.76
  57.3 2.1 gather_fusion.1
  59.4 40.5 %all-to-all-done = bf16[128,64,128]{2,0,1:T(8,128)(2,1)S(1)} async-done(((bf16[128,64,128]{2,0,1:T(8,128)(2,1)}), bf16[128,64,128]{2,0,1:T(8,128)(2,1)S(1)}, u32[]{:S(2)}, u32[]{:S(2)}) %all-to-all-start) | async-done | bytes 2097184 | tf_op jit(solution)/shard_map/all_to_all | solution.py:154
  99.9 8.8 %all-to-all-start.2 = ((bf16[32,2,128,128]{3,2,1,0:T(8,128)(2,1)}), bf16[32,2,128,128]{3,2,1,0:T(8,128)(2,1)}, u32[]{:S(2)}, u32[]{:S(2)}) async-start(bf16[32,2,128,128]{3,2,1,0:T(8,128)(2,1)} %bitcast.52), calls=%async_computation.2 | async-start | bytes 4194304 | tf_op jit(solution)/shard_map/all_to_all | solution.py:158
  108.7 2.2 gather_fusion
  110.8 1.5 copy.62
  112.3 46.7 %all-to-all-done.2.mine0_ref = bf16[32,2,128,128]{3,2,1,0:T(8,128)(2,1)} async-done(((bf16[32,2,128,128]{3,2,1,0:T(8,128)(2,1)}), bf16[32,2,128,128]{3,2,1,0:T(8,128)(2,1)}, u32[]{:S(2)}, u32[]{:S(2)}) %all-to-all-start.2) | async-done | bytes 2097184 | tf_op jit(solution)/shard_map/all_to_all | solution.py:158
  159.0 4.7 %all-to-all-start.3 = ((bf16[32,2,128,128]{3,2,1,0:T(8,128)(2,1)}), bf16[32,2,128,128]{3,2,1,0:T(8,128)(2,1)}, u32[]{:S(2)}, u32[]{:S(2)}) async-start(bf16[32,2,128,128]{3,2,1,0:T(8,128)(2,1)} %bitcast.51), calls=%async_computation.3 | async-start | bytes 4194304 | tf_op jit(solution)/shard_map/all_to_all | solution.py:158
  163.7 1.9 collective-permute-start
  165.6 48.4 %all-to-all-done.3.mine1_ref = bf16[32,2,128,128]{3,2,1,0:T(8,128)(2,1)} async-done(((bf16[32,2,128,128]{3,2,1,0:T(8,128)(2,1)}), bf16[32,2,128,128]{3,2,1,0:T(8,128)(2,1)}, u32[]{:S(2)}, u32[]{:S(2)}) %all-to-all-start.3) | async-done | bytes 2097184 | tf_op jit(solution)/shard_map/all_to_all | solution.py:158
  214.0 2.1 collective-permute-start.1
  216.8 0.7 concatenate.8.which_ref
  217.5 0.7 concatenate.7.slot_ref
  218.1 1.3 dynamic-slice_bitcast_fusion.1.count_ref
  219.4 10.7 %copy.68 = bf16[2048,4,128]{2,1,0:T(4,128)(2,1)} copy(bf16[2048,4,128]{2,0,1:T(8,128)(2,1)S(1)} %bitcast.50) | data formatting | bytes 4194304 | tf_op jit(solution)/shard_map/optimization_barrier | solution.py:157
  230.1 33.7 %collective-permute-done.1.peer1_ref = bf16[32,2,128,128]{3,2,1,0:T(8,128)(2,1)} collective-permute-done((bf16[32,2,128,128]{3,2,1,0:T(8,128)(2,1)}, bf16[32,2,128,128]{3,2,1,0:T(8,128)(2,1)}, u32[]{:S(2)}, u32[]{:S(2)}) %collective-permute-start.1) | collective-permute-done | bytes 2097184 | tf_op jit(solution)/shard_map/ppermute | solution.py:160
  263.8 39.8 %shard_map.55 = bf16[16,512,128]{2,1,0:T(8,128)(2,1)} custom-call(s32[16,8]{1,0:T(8,128)} %concatenate.7.slot_ref, s32[16,8]{1,0:T(8,128)} %concatenate.8.which_ref, s32[16]{0:T(128)} %dynamic-slice_bitcast_fusion.1.count_ref, bf16[16,512,128]{2,1,0:T(8,128)(2,1)} %bitcast.56, bf16[2,16,128,128]{3,2,1,0:T(8,128)(2,1)} %bitcast.47, ...), custom_call_target="tpu_custom_call" | custom-call | tf_op jit(solution)/shard_map/pallas_call | solution.py:67
  303.5 57.0 %all_to_all.58 = bf16[2048,4,128]{2,1,0:T(4,128)(2,1)S(1)} all-to-all(bf16[2048,4,128]{2,1,0:T(4,128)(2,1)} %bitcast.57), channel_id=1, replica_groups=mesh['seq'=32,'head'=16] {'head'}, dimensions={0} | all-to-all | bytes 4194304 | tf_op jit(solution)/shard_map/all_to_all | solution.py:174
  360.6 0.3 copy.69
  360.9 0.2 copy.71
  361.1 2.7 copy.72
  (34 shorter events, 1.9 us)
Async XLA Ops:
  1.5 13.2 %copy-start.3 = (bf16[128,64,128]{2,1,0:T(8,128)(2,1)S(1)}, bf16[128,64,128]{2,1,0:T(8,128)(2,1)}, u32[]{:S(2)}) copy-start(bf16[128,64,128]{2,1,0:T(8,128)(2,1)} %param.5) | copy-start | bytes 6291460
  2.8 41.8 %all-to-all-start.1 = ((bf16[128,2,16,128]{3,0,1,2:T(8,128)(2,1)}), bf16[128,2,16,128]{3,0,1,2:T(8,128)(2,1)S(1)}, u32[]{:S(2)}, u32[]{:S(2)}) async-start(bf16[128,2,16,128]{3,0,1,2:T(8,128)(2,1)} %bitcast.11), calls=%async_computation.1 | async-start | bytes 2097152 | tf_op jit(solution)/shard_map/all_to_all | solution.py:142
  44.6 1.0 copy-start.2
  45.6 54.3 %all-to-all-start = ((bf16[128,64,128]{2,0,1:T(8,128)(2,1)}), bf16[128,64,128]{2,0,1:T(8,128)(2,1)S(1)}, u32[]{:S(2)}, u32[]{:S(2)}) async-start(bf16[128,64,128]{2,0,1:T(8,128)(2,1)} %bitcast.49), calls=%async_computation | async-start | bytes 4194304 | tf_op jit(solution)/shard_map/all_to_all | solution.py:154
  57.3 51.4 %copy-start = (bf16[128,2,16,128]{3,0,2,1:T(8,128)(2,1)}, bf16[128,2,16,128]{3,0,2,1:T(8,128)(2,1)S(1)}, u32[]{:S(2)}) copy-start(bf16[128,2,16,128]{3,0,2,1:T(8,128)(2,1)S(1)} %copy.76) | copy-start | bytes 3145732
  99.9 59.1 %all-to-all-start.2 = ((bf16[32,2,128,128]{3,2,1,0:T(8,128)(2,1)}), bf16[32,2,128,128]{3,2,1,0:T(8,128)(2,1)}, u32[]{:S(2)}, u32[]{:S(2)}) async-start(bf16[32,2,128,128]{3,2,1,0:T(8,128)(2,1)} %bitcast.52), calls=%async_computation.2 | async-start | bytes 4194304 | tf_op jit(solution)/shard_map/all_to_all | solution.py:158
  112.3 107.1 %copy-start.1 = (bf16[16,128,4,128]{3,1,0,2:T(8,128)(2,1)S(1)}, bf16[16,128,4,128]{3,1,0,2:T(8,128)(2,1)}, u32[]{:S(2)}) copy-start(bf16[16,128,4,128]{3,1,0,2:T(8,128)(2,1)} %copy.62) | copy-start | bytes 6291460
  159.0 55.0 %all-to-all-start.3 = ((bf16[32,2,128,128]{3,2,1,0:T(8,128)(2,1)}), bf16[32,2,128,128]{3,2,1,0:T(8,128)(2,1)}, u32[]{:S(2)}, u32[]{:S(2)}) async-start(bf16[32,2,128,128]{3,2,1,0:T(8,128)(2,1)} %bitcast.51), calls=%async_computation.3 | async-start | bytes 4194304 | tf_op jit(solution)/shard_map/all_to_all | solution.py:158
  163.7 66.4 %collective-permute-start = (bf16[32,2,128,128]{3,2,1,0:T(8,128)(2,1)}, bf16[32,2,128,128]{3,2,1,0:T(8,128)(2,1)}, u32[]{:S(2)}, u32[]{:S(2)}) collective-permute-start(bf16[32,2,128,128]{3,2,1,0:T(8,128)(2,1)} %all-to-all-done.2.mine0_ref), channel_id=1, source_target_pairs={{0,4},{1,5},{2,6},{3,7},{4,0},{5,1},{6,2},{7,3},{8,12},{9,13},{10,... | collective-permute-start | bytes 6291464 | tf_op jit(solution)/shard_map/ppermute | solution.py:160
  214.0 49.8 %collective-permute-start.1 = (bf16[32,2,128,128]{3,2,1,0:T(8,128)(2,1)}, bf16[32,2,128,128]{3,2,1,0:T(8,128)(2,1)}, u32[]{:S(2)}, u32[]{:S(2)}) collective-permute-start(bf16[32,2,128,128]{3,2,1,0:T(8,128)(2,1)} %all-to-all-done.3.mine1_ref), channel_id=1, source_target_pairs={{0,4},{1,5},{2,6},{3,7},{4,0},{5,1},{6,2},{7,3},{8,12},{9,13},{10,... | collective-permute-start | bytes 6291464 | tf_op jit(solution)/shard_map/ppermute | solution.py:160

commit v4 on v3

--- a/solution.py
+++ b/solution.py
@@ -8,15 +8,20 @@
 from jax.sharding import PartitionSpec as P
 
 BLK = 128
+HEAD_SPLIT = 2
 
 
 NEG_FILL = -1e30
 
 
 def attend_kernel(slot_ref, which_ref, count_ref, query_ref, own_ref, mine0_ref, mine1_ref,
-                  peer0_ref, peer1_ref, out_ref, key_buf, value_buf, *, score_scale, slot_total):
+                  peer0_ref, peer1_ref, out_ref, block_buf, *, score_scale, slot_total, heads):
     row = pl.program_id(0)
-    query = query_ref[0]
+    head_dim = block_buf.shape[2] // 2
+    query = query_ref[...]
+    query = jnp.concatenate(
+        [query[:, h * head_dim:(h + 1) * head_dim] for h in range(heads)], axis=0
+    )
     row_count = count_ref[row]
     sources = (mine0_ref, mine1_ref, peer0_ref, peer1_ref)
     for slot in range(1, slot_total):
@@ -25,17 +30,13 @@
         for code, source in enumerate(sources):
             @pl.when(which == code)
             def _(source=source, slot=slot, index=index):
-                key_buf[slot - 1] = source[index, 0]
-                value_buf[slot - 1] = source[index, 1]
+                block_buf[slot - 1] = source[index]
     scores = []
     values = []
     for slot in range(slot_total):
-        if slot == 0:
-            key = own_ref[0, row]
-            value = own_ref[1, row]
-        else:
-            key = key_buf[slot - 1]
-            value = value_buf[slot - 1]
+        block = own_ref[row] if slot == 0 else block_buf[slot - 1]
+        key = block[:, :head_dim]
+        value = block[:, head_dim:]
         part = lax.dot_general(
             query, key, (((1,), (1,)), ((), ())), preferred_element_type=jnp.float32
         ) * score_scale
@@ -56,33 +57,39 @@
         probs = (part * inverse).astype(jnp.bfloat16)
         term = jnp.dot(probs, value, preferred_element_type=jnp.float32)
         acc = term if acc is None else acc + term
-    out_ref[0] = acc.astype(out_ref.dtype)
-
-
-def attend_all(query_rows, own_blocks, received, slot_index, slot_which, row_counts, score_scale):
-    qblocks, rows, head_dim = query_rows.shape
+    tokens = query_ref.shape[0]
+    for h in range(heads):
+        out_ref[:, h * head_dim:(h + 1) * head_dim] = acc[h * tokens:(h + 1) * tokens].astype(
+            out_ref.dtype
+        )
+
+
+def attend_all(local_queries, column, width, own_blocks, received, slot_index, slot_which,
+               row_counts, score_scale):
+    seq_rows = local_queries.shape[0]
+    qblocks, _, pair_dim = own_blocks.shape
+    head_dim = pair_dim // 2
     slot_total = slot_index.shape[1]
-    kernel = partial(attend_kernel, score_scale=score_scale, slot_total=slot_total)
+    kernel = partial(
+        attend_kernel, score_scale=score_scale, slot_total=slot_total, heads=width // head_dim
+    )
     whole = lambda shape: pl.BlockSpec(shape, lambda r, s, w, c: (0,) * len(shape))
     return pl.pallas_call(
         kernel,
-        out_shape=jax.ShapeDtypeStruct(query_rows.shape, query_rows.dtype),
+        out_shape=jax.ShapeDtypeStruct((seq_rows, width), local_queries.dtype),
         grid_spec=pltpu.PrefetchScalarGridSpec(
             num_scalar_prefetch=3,
             grid=(qblocks,),
             in_specs=[
-                pl.BlockSpec((1, rows, head_dim), lambda r, s, w, c: (r, 0, 0)),
+                pl.BlockSpec((BLK, width), lambda r, s, w, c: (r, column)),
                 whole(own_blocks.shape),
             ]
             + [whole(part.shape) for part in received],
-            out_specs=pl.BlockSpec((1, rows, head_dim), lambda r, s, w, c: (r, 0, 0)),
-            scratch_shapes=[
-                pltpu.VMEM((slot_total - 1, BLK, head_dim), own_blocks.dtype),
-                pltpu.VMEM((slot_total - 1, BLK, head_dim), own_blocks.dtype),
-            ],
+            out_specs=pl.BlockSpec((BLK, width), lambda r, s, w, c: (r, 0)),
+            scratch_shapes=[pltpu.VMEM((slot_total - 1, BLK, pair_dim), own_blocks.dtype)],
         ),
         compiler_params=pltpu.CompilerParams(vmem_limit_bytes=100 * 1024 * 1024),
-    )(slot_index, slot_which, row_counts, query_rows, own_blocks, *received)
+    )(slot_index, slot_which, row_counts, local_queries, own_blocks, *received)
 
 
 def make_plan(block_lists, block_counts, group_head, seq_index, shard_count, qblocks, capacity):
@@ -124,23 +131,23 @@
     shard_count = lax.axis_size("seq")
     head_index = lax.axis_index("head")
     seq_index = lax.axis_index("seq")
+    tokens, query_heads, head_dim = queries.shape
     kv_total = keys.shape[1]
-    head_dim = keys.shape[2]
     assert head_count == 16 and kv_total == 8
     group_head = (head_index // 8) * 4 + head_index % 4
     half = (head_index // 4) % 2
-    seq_rows = queries.shape[0] * head_count
+    seq_rows = tokens * head_count
     qblocks = seq_rows // BLK
-    group_size = queries.shape[1] // head_count
+    group_size = query_heads // head_count
     slot_total = block_lists.shape[2]
     capacity = (qblocks * (slot_total - 1) + shard_count - 2) // (shard_count - 1)
     assert capacity == 4
-    kv = jnp.stack([keys, values], axis=1)
+    kv = jnp.concatenate([keys, values], axis=2)
     kv = jnp.broadcast_to(
-        kv.reshape(kv.shape[0], 2, 2, 1, 4, head_dim), (kv.shape[0], 2, 2, 2, 4, head_dim)
-    ).reshape(kv.shape[0], 2, head_count, head_dim)
-    own_kv = lax.all_to_all(kv, "head", split_axis=2, concat_axis=0, tiled=True)
-    block_kv = own_kv.reshape(qblocks, BLK, 2, head_dim)
+        kv.reshape(tokens, 2, 1, 4, 2 * head_dim), (tokens, 2, 2, 4, 2 * head_dim)
+    ).reshape(tokens, head_count, 2 * head_dim)
+    own_kv = lax.all_to_all(kv, "head", split_axis=1, concat_axis=0, tiled=True)
+    own_blocks = own_kv.reshape(qblocks, BLK, 2 * head_dim)
     chosen, my_live, my_owner, my_place, my_counts = make_plan(
         block_lists, block_counts, group_head, seq_index, shard_count, qblocks, capacity
     )
@@ -149,29 +156,34 @@
     peer = []
     for chunk in range(2):
         pick = lax.dynamic_index_in_dim(chosen, 2 * half + chunk, 1, keepdims=False)
-        picked = jnp.transpose(block_kv[pick], (0, 2, 1, 3))
+        picked = own_blocks[pick]
         if chunk == 1:
-            local_queries = lax.all_to_all(
-                swap_halves(queries, 4), "head", split_axis=1, concat_axis=0, tiled=True
-            )
+            spread = swap_halves(queries, 4).reshape(tokens, head_count, group_size * head_dim)
+            local_queries = lax.all_to_all(spread, "head", split_axis=1, concat_axis=0, tiled=True)
             local_queries, picked = lax.optimization_barrier((local_queries, picked))
         got = lax.all_to_all(picked, "seq", split_axis=0, concat_axis=0, tiled=True)
         mine.append(got)
         peer.append(lax.ppermute(got, "head", partner))
+    local_queries = local_queries.reshape(seq_rows, group_size * head_dim)
     which = jnp.where(my_place // 2 == half, 0, 2) + my_place % 2
     slot_index = jnp.where(my_live, my_owner, 0).reshape(qblocks, slot_total - 1)
     slot_which = jnp.where(my_live, which, 0).reshape(qblocks, slot_total - 1)
     zero_col = jnp.zeros((qblocks, 1), jnp.int32)
     slot_index = jnp.concatenate([zero_col, slot_index], axis=1)
     slot_which = jnp.concatenate([zero_col, slot_which], axis=1)
-    own_blocks = jnp.transpose(block_kv, (2, 0, 1, 3))
     score_scale = head_dim ** (-0.5)
-    query_rows = local_queries.reshape(qblocks, BLK * group_size, head_dim)
-    attended = attend_all(
-        query_rows, own_blocks, mine + peer, slot_index, slot_which, my_counts, score_scale
-    )
-    outputs = attended.reshape(seq_rows, group_size, head_dim)
-    back = lax.all_to_all(outputs, "head", split_axis=0, concat_axis=1, tiled=True)
+    pieces = []
+    width = group_size * head_dim // HEAD_SPLIT
+    for column in range(HEAD_SPLIT):
+        attended = attend_all(
+            local_queries, column, width, own_blocks, mine + peer, slot_index, slot_which,
+            my_counts, score_scale
+        )
+        back = lax.all_to_all(
+            attended.reshape(seq_rows, 1, width), "head", split_axis=0, concat_axis=1, tiled=True
+        )
+        pieces.append(back)
+    back = jnp.concatenate(pieces, axis=2).reshape(tokens, query_heads, head_dim)
     return swap_halves(back, 2)
 
 

time: 365 us -> 382 us (1.047)
  blocking collectives: 57 us -> 0 us
  waiting for transfers between devices: 196 us -> 231 us
  Pallas kernels: 39.8 us -> 55.2 us
  starting transfers between devices: 33.2 us -> 48.3 us
  other arithmetic: 5.87 us -> 11.2 us
    all_to_all x1 -> x0, blocking collectives: 57 us -> none  [on_device(): lax.all_to_all(outputs, 'head', split_axis=0, concat_axis=1, tiled=True)]
    all_to_all x2 -> x4, waiting for transfers between devices: 67.5 us -> 89.9 us  [the longest x1 41.9 us: on_device(): lax.all_to_all(spread, 'head', split_axis=1, concat_axis=0, tiled=True)]
    pallas_call x1 -> x2, Pallas kernels: 39.8 us -> 55.2 us  [attend_all(): pl.pallas_call(kernel, out_shape=jax.ShapeDtypeStruct((seq_rows, width),...]
    all_to_all x2 -> x4, starting transfers between devices: 15.7 us -> 31 us  [the longest x2 15.3 us: on_device(): lax.all_to_all(attended.reshape(seq_rows, 1, width), 'head', split_axis=0...]
    optimization_barrier x1 -> x0, local copies, waits for them, and re-layouts: 10.7 us -> none  [on_device(): local_queries, picked = lax.optimization_barrier((local_queries, picked))]
    ppermute x2, waiting for transfers between devices: 33.7 us -> 44.3 us  [on_device(): peer.append(lax.ppermute(got, 'head', partner))]
    unnamed x9 -> x14, local copies, waits for them, and re-layouts: 2.36 us -> 12.6 us
    reshape x0 -> x2, other arithmetic: none -> 5.43 us  [on_device(): attended.reshape(seq_rows, 1, width)]
  transfers between devices with their start and end apart: 6 -> 8, of which waited for: 5 -> 6; matrix products, arithmetic and copies ran while one was open for 8% -> 7% of each run, Pallas kernels for 0% -> 7%
where the time goes in v4:
time: 382 us; the launch traced here: 381 us
  waiting for transfers between devices  231 us (60%)
  Pallas kernels  55.2 us (14%)
  starting transfers between devices  48.3 us (13%)
  local copies, waits for them, and re-layouts  34.7 us (9%)
  other arithmetic  11.2 us (3%)
    all_to_all x2, waiting for transfers between devices, on_device(): got = lax.all_to_all(picked, 'seq', split_axis=0, concat_axis=0, tiled=True)  96.6 us
    pallas_call x2, Pallas kernels, attend_all(): pl.pallas_call(kernel, out_shape=jax.ShapeDtypeStruct((seq_rows, width),...  55.2 us
    ppermute x2, waiting for transfers between devices, on_device(): peer.append(lax.ppermute(got, 'head', partner))  44.3 us
    all_to_all x1, waiting for transfers between devices, on_device(): lax.all_to_all(spread, 'head', split_axis=1, concat_axis=0, tiled=True)  41.9 us
    all_to_all x1, waiting for transfers between devices, on_device(): own_kv = lax.all_to_all(kv, 'head', split_axis=1, concat_axis=0, tiled=True)  25.1 us
    all_to_all x2, waiting for transfers between devices, on_device(): lax.all_to_all(attended.reshape(seq_rows, 1, width), 'head', split_axis=0...  22.9 us
    all_to_all x2, starting transfers between devices, on_device(): lax.all_to_all(attended.reshape(seq_rows, 1, width), 'head', split_axis=0...  15.3 us
    all_to_all x2, starting transfers between devices, on_device(): got = lax.all_to_all(picked, 'seq', split_axis=0, concat_axis=0, tiled=True)  13.4 us
  transfers between devices with their start and end apart: 8, of which 6 were waited for; matrix products, arithmetic and copies ran while one was open for 7% of the time, Pallas kernels for 7%

profile of v4, /device:TPU:64, one launch (start us, length us, event | category | flops | bytes accessed | tf_op | source)
XLA Modules:
  0.0 380.5 jit_solution(1602915732744857377)
XLA Ops:
  2.3 12.0 %all-to-all-start.1 = ((bf16[128,16,256]{2,0,1:T(8,128)(2,1)}), bf16[128,16,256]{2,0,1:T(8,128)(2,1)S(1)}, u32[]{:S(2)}, u32[]{:S(2)}) async-start(bf16[128,16,256]{2,0,1:T(8,128)(2,1)} %bitcast.8), calls=%async_computation.1 | async-start | bytes 2097152 | tf_op jit(solution)/shard_map/all_to_all | solution.py:149
  14.3 2.6 copy.56
  16.8 2.2 reshape_reshape.6
  19.0 25.1 %all-to-all-done.1 = bf16[128,16,256]{2,0,1:T(8,128)(2,1)S(1)} async-done(((bf16[128,16,256]{2,0,1:T(8,128)(2,1)}), bf16[128,16,256]{2,0,1:T(8,128)(2,1)S(1)}, u32[]{:S(2)}, u32[]{:S(2)}) %all-to-all-start.1) | async-done | bytes 1048608 | tf_op jit(solution)/shard_map/all_to_all | solution.py:149
  44.1 3.7 all-to-all-start
  50.4 3.9 %fusion.3 = s32[32,112]{0,1:T(8,128)S(1)} fusion(s32[32,112]{0,1:T(8,128)S(1)} %get-tuple-element.12, pred[32,112]{0,1:T(8,128)(4,1)S(1)} %get-tuple-element.10), kind=kOutput, calls=%fused_computation.7 | output fusion | flops 13758976 | bytes 32256 | tf_op jit(solution)/shard_map/jit(cumsum)/reduce_window_sum | solution.py:109
  54.5 2.0 gather_fusion.1
  56.5 41.9 %all-to-all-done = bf16[128,16,512]{2,0,1:T(8,128)(2,1)S(1)} async-done(((bf16[128,16,512]{2,0,1:T(8,128)(2,1)}), bf16[128,16,512]{2,0,1:T(8,128)(2,1)S(1)}, u32[]{:S(2)}, u32[]{:S(2)}) %all-to-all-start) | async-done | bytes 2097184 | tf_op jit(solution)/shard_map/all_to_all | solution.py:162
  98.4 1.3 copy-done.1
  99.8 8.8 %all-to-all-start.2 = ((bf16[32,128,256]{2,1,0:T(8,128)(2,1)}), bf16[32,128,256]{2,1,0:T(8,128)(2,1)}, u32[]{:S(2)}, u32[]{:S(2)}) async-start(bf16[32,128,256]{2,1,0:T(8,128)(2,1)} %gather_fusion.1), calls=%async_computation.2 | async-start | bytes 4194304 | tf_op jit(solution)/shard_map/all_to_all | solution.py:164
  108.6 2.0 gather_fusion
  110.6 48.3 %all-to-all-done.2.mine0_ref = bf16[32,128,256]{2,1,0:T(8,128)(2,1)} async-done(((bf16[32,128,256]{2,1,0:T(8,128)(2,1)}), bf16[32,128,256]{2,1,0:T(8,128)(2,1)}, u32[]{:S(2)}, u32[]{:S(2)}) %all-to-all-start.2) | async-done | bytes 2097184 | tf_op jit(solution)/shard_map/all_to_all | solution.py:164
  158.8 4.7 %all-to-all-start.3 = ((bf16[32,128,256]{2,1,0:T(8,128)(2,1)}), bf16[32,128,256]{2,1,0:T(8,128)(2,1)S(1)}, u32[]{:S(2)}, u32[]{:S(2)}) async-start(bf16[32,128,256]{2,1,0:T(8,128)(2,1)} %gather_fusion), calls=%async_computation.3 | async-start | bytes 4194304 | tf_op jit(solution)/shard_map/all_to_all | solution.py:164
  163.5 1.9 collective-permute-start
  165.4 48.3 %all-to-all-done.3.mine1_ref = bf16[32,128,256]{2,1,0:T(8,128)(2,1)S(1)} async-done(((bf16[32,128,256]{2,1,0:T(8,128)(2,1)}), bf16[32,128,256]{2,1,0:T(8,128)(2,1)S(1)}, u32[]{:S(2)}, u32[]{:S(2)}) %all-to-all-start.3) | async-done | bytes 2097184 | tf_op jit(solution)/shard_map/all_to_all | solution.py:164
  213.8 1.3 copy-done.2
  215.1 1.9 collective-permute-start.1
  219.0 1.3 dynamic-slice_bitcast_fusion.1.count_ref
  220.4 44.3 %collective-permute-done.1.peer1_ref = bf16[32,128,256]{2,1,0:T(8,128)(2,1)} collective-permute-done((bf16[32,128,256]{2,1,0:T(8,128)(2,1)S(1)}, bf16[32,128,256]{2,1,0:T(8,128)(2,1)}, u32[]{:S(2)}, u32[]{:S(2)}) %collective-permute-start.1) | collective-permute-done | bytes 2097184 | tf_op jit(solution)/shard_map/ppermute | solution.py:166
  264.7 27.6 %shard_map.55 = bf16[2048,256]{1,0:T(8,128)(2,1)} custom-call(s32[16,8]{1,0:T(8,128)} %concatenate.12.slot_ref, s32[16,8]{1,0:T(8,128)} %concatenate.13.which_ref, s32[16]{0:T(128)} %dynamic-slice_bitcast_fusion.1.count_ref, bf16[2048,512]{1,0:T(8,128)(2,1)} %bitcast.48, bf16[16,128,256]{2,1,0:T(8,128)(2,1)} %bitcast.46, ...), custom_call_target="tpu_custom_call" | custom-call | tf_op jit(solution)/shard_map/pallas_call | solution.py:77
  292.9 2.7 reduce.11
  295.6 1.1 reshape.186
  296.7 5.7 %all-to-all-start.4 = ((bf16[16,2,16384]{2,1,0:T(2,128)(2,1)}), bf16[16,2,16384]{2,1,0:T(2,128)(2,1)}, u32[]{:S(2)}, u32[]{:S(2)}) async-start(bf16[16,2,16384]{2,1,0:T(2,128)(2,1)} %reshape.186), calls=%async_computation.4 | async-start | bytes 2097152 | tf_op jit(solution)/shard_map/all_to_all | solution.py:182
  302.5 27.6 %shard_map.56 = bf16[2048,256]{1,0:T(8,128)(2,1)} custom-call(s32[16,8]{1,0:T(8,128)} %concatenate.12.slot_ref, s32[16,8]{1,0:T(8,128)} %concatenate.13.which_ref, s32[16]{0:T(128)} %dynamic-slice_bitcast_fusion.1.count_ref, bf16[2048,512]{1,0:T(8,128)(2,1)} %bitcast.49, bf16[16,128,256]{2,1,0:T(8,128)(2,1)} %bitcast.47, ...), custom_call_target="tpu_custom_call" | custom-call | tf_op jit(solution)/shard_map/pallas_call | solution.py:77
  330.1 2.7 reduce.10
  332.8 1.1 reshape.184
  333.9 9.6 %all-to-all-start.5 = ((bf16[16,2,16384]{2,1,0:T(2,128)(2,1)}), bf16[16,2,16384]{2,1,0:T(2,128)(2,1)S(1)}, u32[]{:S(2)}, u32[]{:S(2)}) async-start(bf16[16,2,16384]{2,1,0:T(2,128)(2,1)} %reshape.184), calls=%async_computation.5 | async-start | bytes 2097152 | tf_op jit(solution)/shard_map/all_to_all | solution.py:182
  343.5 4.3 %reshape.187 = bf16[2048,1,256]{2,1,0:T(2,128)(2,1)S(1)} reshape(bf16[16,2,16384]{2,1,0:T(2,128)(2,1)} %all-to-all-done.4) | data formatting | bytes 2097152
  347.8 1.2 copy.65
  349.0 22.9 %all-to-all-done.5 = bf16[16,2,16384]{2,1,0:T(2,128)(2,1)S(1)} async-done(((bf16[16,2,16384]{2,1,0:T(2,128)(2,1)}), bf16[16,2,16384]{2,1,0:T(2,128)(2,1)S(1)}, u32[]{:S(2)}, u32[]{:S(2)}) %all-to-all-start.5) | async-done | bytes 1048608 | tf_op jit(solution)/shard_map/all_to_all | solution.py:182
  374.3 2.1 reshape_reshape.7
  376.4 4.1 %copy.63 = bf16[128,2,4,2,4,128]{5,4,3,2,1,0:T(4,128)(2,1)} copy(bf16[128,2,4,2,4,128]{5,4,0,2,3,1:T(4,128)(2,1)} %bitcast.50) | data formatting | bytes 4194304 | tf_op jit(solution)/shard_map/transpose | solution.py:126
  (45 shorter events, 9.9 us)
Async XLA Ops:
  2.3 41.8 %all-to-all-start.1 = ((bf16[128,16,256]{2,0,1:T(8,128)(2,1)}), bf16[128,16,256]{2,0,1:T(8,128)(2,1)S(1)}, u32[]{:S(2)}, u32[]{:S(2)}) async-start(bf16[128,16,256]{2,0,1:T(8,128)(2,1)} %bitcast.8), calls=%async_computation.1 | async-start | bytes 2097152 | tf_op jit(solution)/shard_map/all_to_all | solution.py:149
  44.1 64.4 %copy-start = (bf16[128,16,256]{2,0,1:T(8,128)(2,1)}, bf16[128,16,256]{2,0,1:T(8,128)(2,1)S(1)}, u32[]{:S(2)}) copy-start(bf16[128,16,256]{2,0,1:T(8,128)(2,1)S(1)} %all-to-all-done.1) | copy-start | bytes 3145732
  44.1 54.3 %all-to-all-start = ((bf16[128,16,512]{2,0,1:T(8,128)(2,1)}), bf16[128,16,512]{2,0,1:T(8,128)(2,1)S(1)}, u32[]{:S(2)}, u32[]{:S(2)}) async-start(bf16[128,16,512]{2,0,1:T(8,128)(2,1)} %reshape_reshape.6), calls=%async_computation | async-start | bytes 4194304 | tf_op jit(solution)/shard_map/all_to_all | solution.py:162
  98.4 1.3 copy-start.1
  99.8 59.1 %all-to-all-start.2 = ((bf16[32,128,256]{2,1,0:T(8,128)(2,1)}), bf16[32,128,256]{2,1,0:T(8,128)(2,1)}, u32[]{:S(2)}, u32[]{:S(2)}) async-start(bf16[32,128,256]{2,1,0:T(8,128)(2,1)} %gather_fusion.1), calls=%async_computation.2 | async-start | bytes 4194304 | tf_op jit(solution)/shard_map/all_to_all | solution.py:164
  158.8 54.9 %all-to-all-start.3 = ((bf16[32,128,256]{2,1,0:T(8,128)(2,1)}), bf16[32,128,256]{2,1,0:T(8,128)(2,1)S(1)}, u32[]{:S(2)}, u32[]{:S(2)}) async-start(bf16[32,128,256]{2,1,0:T(8,128)(2,1)} %gather_fusion), calls=%async_computation.3 | async-start | bytes 4194304 | tf_op jit(solution)/shard_map/all_to_all | solution.py:164
  163.5 56.9 %collective-permute-start = (bf16[32,128,256]{2,1,0:T(8,128)(2,1)}, bf16[32,128,256]{2,1,0:T(8,128)(2,1)}, u32[]{:S(2)}, u32[]{:S(2)}) collective-permute-start(bf16[32,128,256]{2,1,0:T(8,128)(2,1)} %all-to-all-done.2.mine0_ref), channel_id=1, source_target_pairs={{0,4},{1,5},{2,6},{3,7},{4,0},{5,1},{6,2},{7,3},{8,12},{9,13},{10,... | collective-permute-start | bytes 6291464 | tf_op jit(solution)/shard_map/ppermute | solution.py:166
  213.8 1.3 copy-start.2
  215.1 49.6 %collective-permute-start.1 = (bf16[32,128,256]{2,1,0:T(8,128)(2,1)S(1)}, bf16[32,128,256]{2,1,0:T(8,128)(2,1)}, u32[]{:S(2)}, u32[]{:S(2)}) collective-permute-start(bf16[32,128,256]{2,1,0:T(8,128)(2,1)S(1)} %all-to-all-done.3.mine1_ref), channel_id=1, source_target_pairs={{0,4},{1,5},{2,6},{3,7},{4,0},{5,1},{6,2},{7,3},{8,12},{9,13},{10,... | collective-permute-start | bytes 6291464 | tf_op jit(solution)/shard_map/ppermute | solution.py:166
  296.7 37.2 %all-to-all-start.4 = ((bf16[16,2,16384]{2,1,0:T(2,128)(2,1)}), bf16[16,2,16384]{2,1,0:T(2,128)(2,1)}, u32[]{:S(2)}, u32[]{:S(2)}) async-start(bf16[16,2,16384]{2,1,0:T(2,128)(2,1)} %reshape.186), calls=%async_computation.4 | async-start | bytes 2097152 | tf_op jit(solution)/shard_map/all_to_all | solution.py:182
  333.9 37.9 %all-to-all-start.5 = ((bf16[16,2,16384]{2,1,0:T(2,128)(2,1)}), bf16[16,2,16384]{2,1,0:T(2,128)(2,1)S(1)}, u32[]{:S(2)}, u32[]{:S(2)}) async-start(bf16[16,2,16384]{2,1,0:T(2,128)(2,1)} %reshape.184), calls=%async_computation.5 | async-start | bytes 2097152 | tf_op jit(solution)/shard_map/all_to_all | solution.py:182
  372.9 1.2 copy-start.3

commit v5 on v4

--- a/solution.py
+++ b/solution.py
@@ -8,7 +8,6 @@
 from jax.sharding import PartitionSpec as P
 
 BLK = 128
-HEAD_SPLIT = 2
 
 
 NEG_FILL = -1e30
@@ -120,12 +119,6 @@
     return (chosen, my_live, my_owner, my_place, my_counts)
 
 
-def swap_halves(heads, inner):
-    shape = heads.shape
-    split = heads.reshape(shape[:1] + (2, inner, 6 - inner, 4) + shape[2:])
-    return jnp.swapaxes(split, 2, 3).reshape(shape)
-
-
 def on_device(queries, keys, values, block_lists, block_counts):
     head_count = lax.axis_size("head")
     shard_count = lax.axis_size("seq")
@@ -143,11 +136,10 @@
     capacity = (qblocks * (slot_total - 1) + shard_count - 2) // (shard_count - 1)
     assert capacity == 4
     kv = jnp.concatenate([keys, values], axis=2)
-    kv = jnp.broadcast_to(
-        kv.reshape(tokens, 2, 1, 4, 2 * head_dim), (tokens, 2, 2, 4, 2 * head_dim)
-    ).reshape(tokens, head_count, 2 * head_dim)
-    own_kv = lax.all_to_all(kv, "head", split_axis=1, concat_axis=0, tiled=True)
-    own_blocks = own_kv.reshape(qblocks, BLK, 2 * head_dim)
+    kv = jnp.transpose(kv.reshape(tokens, 2, 1, 4, 2 * head_dim), (1, 2, 3, 0, 4))
+    kv = jnp.broadcast_to(kv, (2, 2, 4, tokens, 2 * head_dim))
+    kv = kv.reshape(head_count, tokens, 2 * head_dim)
+    own_blocks = lax.all_to_all(kv, "head", split_axis=0, concat_axis=0, tiled=True)
     chosen, my_live, my_owner, my_place, my_counts = make_plan(
         block_lists, block_counts, group_head, seq_index, shard_count, qblocks, capacity
     )
@@ -158,8 +150,10 @@
         pick = lax.dynamic_index_in_dim(chosen, 2 * half + chunk, 1, keepdims=False)
         picked = own_blocks[pick]
         if chunk == 1:
-            spread = swap_halves(queries, 4).reshape(tokens, head_count, group_size * head_dim)
-            local_queries = lax.all_to_all(spread, "head", split_axis=1, concat_axis=0, tiled=True)
+            spread = jnp.transpose(
+                queries.reshape(tokens, 2, 4, 2, group_size, head_dim), (1, 3, 2, 0, 4, 5)
+            ).reshape(head_count, tokens, group_size * head_dim)
+            local_queries = lax.all_to_all(spread, "head", split_axis=0, concat_axis=0, tiled=True)
             local_queries, picked = lax.optimization_barrier((local_queries, picked))
         got = lax.all_to_all(picked, "seq", split_axis=0, concat_axis=0, tiled=True)
         mine.append(got)
@@ -172,19 +166,17 @@
     slot_index = jnp.concatenate([zero_col, slot_index], axis=1)
     slot_which = jnp.concatenate([zero_col, slot_which], axis=1)
     score_scale = head_dim ** (-0.5)
-    pieces = []
-    width = group_size * head_dim // HEAD_SPLIT
-    for column in range(HEAD_SPLIT):
-        attended = attend_all(
-            local_queries, column, width, own_blocks, mine + peer, slot_index, slot_which,
-            my_counts, score_scale
-        )
-        back = lax.all_to_all(
-            attended.reshape(seq_rows, 1, width), "head", split_axis=0, concat_axis=1, tiled=True
-        )
-        pieces.append(back)
-    back = jnp.concatenate(pieces, axis=2).reshape(tokens, query_heads, head_dim)
-    return swap_halves(back, 2)
+    width = group_size * head_dim
+    attended = attend_all(
+        local_queries, 0, width, own_blocks, mine + peer, slot_index, slot_which,
+        my_counts, score_scale
+    )
+    back = lax.all_to_all(
+        attended.reshape(head_count, tokens, width), "head", split_axis=0, concat_axis=0,
+        tiled=True
+    )
+    back = jnp.transpose(back.reshape(2, 2, 4, tokens, group_size, head_dim), (3, 0, 2, 1, 4, 5))
+    return back.reshape(tokens, query_heads, head_dim)
 
 
 def solution(mesh):

time: 382 us -> 368 us (0.963)
  blocking collectives: 0 us -> 57.1 us
  waiting for transfers between devices: 231 us -> 208 us
  Pallas kernels: 55.2 us -> 39.6 us
  starting transfers between devices: 48.3 us -> 33 us
  local copies, waits for them, and re-layouts: 34.7 us -> 24.3 us
  other arithmetic: 11.2 us -> 5.54 us
    all_to_all x0 -> x1, blocking collectives: none -> 57.1 us  [on_device(): lax.all_to_all(attended.reshape(head_count, tokens, width), 'head', split...]
    all_to_all x4 -> x2, waiting for transfers between devices: 89.9 us -> 67 us  [the longest x1 41.9 us: on_device(): lax.all_to_all(spread, 'head', split_axis=0, concat_axis=0, tiled=True)]
    pallas_call x2 -> x1, Pallas kernels: 55.2 us -> 39.6 us  [attend_all(): pl.pallas_call(kernel, out_shape=jax.ShapeDtypeStruct((seq_rows, width),...]
    all_to_all x4 -> x2, starting transfers between devices: 31 us -> 15.7 us  [the longest x1 12 us: on_device(): lax.all_to_all(kv, 'head', split_axis=0, concat_axis=0, tiled=True)]
    unnamed x14 -> x6, local copies, waits for them, and re-layouts: 12.6 us -> 2.65 us
    reshape x1 -> x4, local copies, waits for them, and re-layouts: 0.59 us -> 8.5 us  [the longest x2 6.16 us: on_device(): back.reshape(2, 2, 4, tokens, group_size, head_dim)]
    reshape x2 -> x0, other arithmetic: 5.43 us -> none  [on_device(): attended.reshape(seq_rows, 1, width)]
    another operation x2 -> x0, local copies, waits for them, and re-layouts: 4.3 us -> none  [the longest x1 2.21 us: on_device(): swap_halves(queries, 4).reshape(tokens, head_count, group_size * head_dim)]
  transfers between devices with their start and end apart: 8 -> 6, of which waited for: 6 -> 5; matrix products, arithmetic and copies ran while one was open for 7% -> 5% of each run, Pallas kernels for 7% -> 0%
where the time goes in v5:
time: 368 us
  waiting for transfers between devices  208 us (57%)
  blocking collectives  57.1 us (16%)
  Pallas kernels  39.6 us (11%)
  starting transfers between devices  33 us (9%)
  local copies, waits for them, and re-layouts  24.3 us (7%)
  other arithmetic  5.54 us (2%)
    all_to_all x2, waiting for transfers between devices, on_device(): got = lax.all_to_all(picked, 'seq', split_axis=0, concat_axis=0, tiled=True)  96.6 us
    all_to_all x1, blocking collectives, on_device(): lax.all_to_all(attended.reshape(head_count, tokens, width), 'head', split...  57.1 us
    ppermute x2, waiting for transfers between devices, on_device(): peer.append(lax.ppermute(got, 'head', partner))  44.3 us
    all_to_all x1, waiting for transfers between devices, on_device(): lax.all_to_all(spread, 'head', split_axis=0, concat_axis=0, tiled=True)  41.9 us
    pallas_call x1, Pallas kernels, attend_all(): pl.pallas_call(kernel, out_shape=jax.ShapeDtypeStruct((seq_rows, width),...  39.6 us
    all_to_all x1, waiting for transfers between devices, on_device(): lax.all_to_all(kv, 'head', split_axis=0, concat_axis=0, tiled=True)  25.1 us
    all_to_all x2, starting transfers between devices, on_device(): got = lax.all_to_all(picked, 'seq', split_axis=0, concat_axis=0, tiled=True)  13.4 us
    all_to_all x1, starting transfers between devices, on_device(): lax.all_to_all(kv, 'head', split_axis=0, concat_axis=0, tiled=True)  12 us
  transfers between devices with their start and end apart: 6, of which 5 were waited for; matrix products, arithmetic and copies ran while one was open for 5% of the time, Pallas kernels for 0%

profile of v5, /device:TPU:64, one launch (start us, length us, event | category | flops | bytes accessed | tf_op | source)
XLA Modules:
  0.0 367.7 jit_solution(17315859494238836587)
XLA Ops:
  0.0 1.1 pad_maximum_fusion
  1.3 1.1 broadcast_in_dim.12
  2.4 12.0 %all-to-all-start.1 = ((bf16[16,128,256]{2,1,0:T(8,128)(2,1)}), bf16[16,128,256]{2,1,0:T(8,128)(2,1)S(1)}, u32[]{:S(2)}, u32[]{:S(2)}) async-start(bf16[16,128,256]{2,1,0:T(8,128)(2,1)} %bitcast.6), calls=%async_computation.1 | async-start | bytes 2097152 | tf_op jit(solution)/shard_map/all_to_all | solution.py:142
  14.4 2.6 copy.40
  17.0 2.2 reshape.152
  19.2 25.1 %all-to-all-done.1.own_ref = bf16[16,128,256]{2,1,0:T(8,128)(2,1)S(1)} async-done(((bf16[16,128,256]{2,1,0:T(8,128)(2,1)}), bf16[16,128,256]{2,1,0:T(8,128)(2,1)S(1)}, u32[]{:S(2)}, u32[]{:S(2)}) %all-to-all-start.1) | async-done | bytes 1048608 | tf_op jit(solution)/shard_map/all_to_all | solution.py:142
  44.2 3.7 %all-to-all-start = ((bf16[16,128,512]{2,1,0:T(8,128)(2,1)}), bf16[16,128,512]{2,1,0:T(8,128)(2,1)S(1)}, u32[]{:S(2)}, u32[]{:S(2)}) async-start(bf16[16,128,512]{2,1,0:T(8,128)(2,1)} %reshape.152), calls=%async_computation | async-start | bytes 4194304 | tf_op jit(solution)/shard_map/all_to_all | solution.py:156
  48.2 0.7 dynamic-slice_reduce_fusion.2
  49.1 0.7 dynamic-slice_bitcast_fusion
  50.5 3.9 %fusion.3 = s32[32,112]{0,1:T(8,128)S(1)} fusion(s32[32,112]{0,1:T(8,128)S(1)} %get-tuple-element.12, pred[32,112]{0,1:T(8,128)(4,1)S(1)} %get-tuple-element.10), kind=kOutput, calls=%fused_computation.6 | output fusion | flops 13758976 | bytes 32256 | tf_op jit(solution)/shard_map/jit(cumsum)/reduce_window_sum | solution.py:108
  54.5 0.2 multiply_reduce_fusion
  54.6 2.0 gather_fusion.1
  56.6 41.9 %all-to-all-done = bf16[16,128,512]{2,1,0:T(8,128)(2,1)S(1)} async-done(((bf16[16,128,512]{2,1,0:T(8,128)(2,1)}), bf16[16,128,512]{2,1,0:T(8,128)(2,1)S(1)}, u32[]{:S(2)}, u32[]{:S(2)}) %all-to-all-start) | async-done | bytes 2097184 | tf_op jit(solution)/shard_map/all_to_all | solution.py:156
  98.6 1.3 copy-done.1
  99.9 8.8 %all-to-all-start.2 = ((bf16[32,128,256]{2,1,0:T(8,128)(2,1)}), bf16[32,128,256]{2,1,0:T(8,128)(2,1)}, u32[]{:S(2)}, u32[]{:S(2)}) async-start(bf16[32,128,256]{2,1,0:T(8,128)(2,1)} %gather_fusion.1), calls=%async_computation.2 | async-start | bytes 4194304 | tf_op jit(solution)/shard_map/all_to_all | solution.py:158
  108.7 2.0 gather_fusion
  110.7 48.3 %all-to-all-done.2.mine0_ref = bf16[32,128,256]{2,1,0:T(8,128)(2,1)} async-done(((bf16[32,128,256]{2,1,0:T(8,128)(2,1)}), bf16[32,128,256]{2,1,0:T(8,128)(2,1)}, u32[]{:S(2)}, u32[]{:S(2)}) %all-to-all-start.2) | async-done | bytes 2097184 | tf_op jit(solution)/shard_map/all_to_all | solution.py:158
  159.0 4.7 %all-to-all-start.3 = ((bf16[32,128,256]{2,1,0:T(8,128)(2,1)}), bf16[32,128,256]{2,1,0:T(8,128)(2,1)S(1)}, u32[]{:S(2)}, u32[]{:S(2)}) async-start(bf16[32,128,256]{2,1,0:T(8,128)(2,1)} %gather_fusion), calls=%async_computation.3 | async-start | bytes 4194304 | tf_op jit(solution)/shard_map/all_to_all | solution.py:158
  163.6 1.9 collective-permute-start
  165.6 48.3 %all-to-all-done.3.mine1_ref = bf16[32,128,256]{2,1,0:T(8,128)(2,1)S(1)} async-done(((bf16[32,128,256]{2,1,0:T(8,128)(2,1)}), bf16[32,128,256]{2,1,0:T(8,128)(2,1)S(1)}, u32[]{:S(2)}, u32[]{:S(2)}) %all-to-all-start.3) | async-done | bytes 2097184 | tf_op jit(solution)/shard_map/all_to_all | solution.py:158
  213.9 1.3 copy-done.2
  215.2 1.9 collective-permute-start.1
  217.2 0.2 dynamic-slice_reduce_fusion.1
  217.4 0.2 minimum_reduce_fusion
  217.8 0.7 concatenate.10.which_ref
  218.5 0.7 concatenate.9.slot_ref
  219.2 1.3 dynamic-slice_bitcast_fusion.1.count_ref
  220.5 44.3 %collective-permute-done.1.peer1_ref = bf16[32,128,256]{2,1,0:T(8,128)(2,1)} collective-permute-done((bf16[32,128,256]{2,1,0:T(8,128)(2,1)S(1)}, bf16[32,128,256]{2,1,0:T(8,128)(2,1)}, u32[]{:S(2)}, u32[]{:S(2)}) %collective-permute-start.1) | collective-permute-done | bytes 2097184 | tf_op jit(solution)/shard_map/ppermute | solution.py:160
  264.8 39.6 %shard_map.55 = bf16[2048,512]{1,0:T(8,128)(2,1)} custom-call(s32[16,8]{1,0:T(8,128)} %concatenate.9.slot_ref, s32[16,8]{1,0:T(8,128)} %concatenate.10.which_ref, s32[16]{0:T(128)} %dynamic-slice_bitcast_fusion.1.count_ref, bf16[2048,512]{1,0:T(8,128)(2,1)} %bitcast.22, bf16[16,128,256]{2,1,0:T(8,128)(2,1)} %copy-done, ...), custom_call_target="tpu_custom_call" | custom-call | tf_op jit(solution)/shard_map/pallas_call | solution.py:76
  304.4 57.1 %all_to_all.25 = bf16[16,128,512]{2,1,0:T(8,128)(2,1)S(1)} all-to-all(bf16[16,128,512]{2,1,0:T(8,128)(2,1)} %bitcast.23), channel_id=1, replica_groups=mesh['seq'=32,'head'=16] {'head'}, dimensions={0} | all-to-all | bytes 4194304 | tf_op jit(solution)/shard_map/all_to_all | solution.py:174
  361.5 2.1 reshape.157
  363.6 4.1 %copy.45 = bf16[2,2,4,128,4,128]{5,4,1,2,0,3:T(4,128)(2,1)} copy(bf16[2,2,4,128,4,128]{5,4,3,2,1,0:T(4,128)(2,1)} %reshape.157) | data formatting | bytes 4194304 | tf_op jit(solution)/shard_map/reshape | solution.py:178
  (30 shorter events, 1.5 us)
Async XLA Ops:
  2.4 41.8 %all-to-all-start.1 = ((bf16[16,128,256]{2,1,0:T(8,128)(2,1)}), bf16[16,128,256]{2,1,0:T(8,128)(2,1)S(1)}, u32[]{:S(2)}, u32[]{:S(2)}) async-start(bf16[16,128,256]{2,1,0:T(8,128)(2,1)} %bitcast.6), calls=%async_computation.1 | async-start | bytes 2097152 | tf_op jit(solution)/shard_map/all_to_all | solution.py:142
  44.2 64.4 %copy-start = (bf16[16,128,256]{2,1,0:T(8,128)(2,1)}, bf16[16,128,256]{2,1,0:T(8,128)(2,1)S(1)}, u32[]{:S(2)}) copy-start(bf16[16,128,256]{2,1,0:T(8,128)(2,1)S(1)} %all-to-all-done.1.own_ref) | copy-start | bytes 3145732
  44.2 54.3 %all-to-all-start = ((bf16[16,128,512]{2,1,0:T(8,128)(2,1)}), bf16[16,128,512]{2,1,0:T(8,128)(2,1)S(1)}, u32[]{:S(2)}, u32[]{:S(2)}) async-start(bf16[16,128,512]{2,1,0:T(8,128)(2,1)} %reshape.152), calls=%async_computation | async-start | bytes 4194304 | tf_op jit(solution)/shard_map/all_to_all | solution.py:156
  98.6 1.3 copy-start.1
  99.9 59.1 %all-to-all-start.2 = ((bf16[32,128,256]{2,1,0:T(8,128)(2,1)}), bf16[32,128,256]{2,1,0:T(8,128)(2,1)}, u32[]{:S(2)}, u32[]{:S(2)}) async-start(bf16[32,128,256]{2,1,0:T(8,128)(2,1)} %gather_fusion.1), calls=%async_computation.2 | async-start | bytes 4194304 | tf_op jit(solution)/shard_map/all_to_all | solution.py:158
  159.0 54.9 %all-to-all-start.3 = ((bf16[32,128,256]{2,1,0:T(8,128)(2,1)}), bf16[32,128,256]{2,1,0:T(8,128)(2,1)S(1)}, u32[]{:S(2)}, u32[]{:S(2)}) async-start(bf16[32,128,256]{2,1,0:T(8,128)(2,1)} %gather_fusion), calls=%async_computation.3 | async-start | bytes 4194304 | tf_op jit(solution)/shard_map/all_to_all | solution.py:158
  163.6 56.8 %collective-permute-start = (bf16[32,128,256]{2,1,0:T(8,128)(2,1)}, bf16[32,128,256]{2,1,0:T(8,128)(2,1)}, u32[]{:S(2)}, u32[]{:S(2)}) collective-permute-start(bf16[32,128,256]{2,1,0:T(8,128)(2,1)} %all-to-all-done.2.mine0_ref), channel_id=1, source_target_pairs={{0,4},{1,5},{2,6},{3,7},{4,0},{5,1},{6,2},{7,3},{8,12},{9,13},{10,... | collective-permute-start | bytes 6291464 | tf_op jit(solution)/shard_map/ppermute | solution.py:160
  213.9 1.3 copy-start.2
  215.2 49.6 %collective-permute-start.1 = (bf16[32,128,256]{2,1,0:T(8,128)(2,1)S(1)}, bf16[32,128,256]{2,1,0:T(8,128)(2,1)}, u32[]{:S(2)}, u32[]{:S(2)}) collective-permute-start(bf16[32,128,256]{2,1,0:T(8,128)(2,1)S(1)} %all-to-all-done.3.mine1_ref), channel_id=1, source_target_pairs={{0,4},{1,5},{2,6},{3,7},{4,0},{5,1},{6,2},{7,3},{8,12},{9,13},{10,... | collective-permute-start | bytes 6291464 | tf_op jit(solution)/shard_map/ppermute | solution.py:160

commit v6 on v5

--- a/solution.py
+++ b/solution.py
@@ -150,14 +150,15 @@
         pick = lax.dynamic_index_in_dim(chosen, 2 * half + chunk, 1, keepdims=False)
         picked = own_blocks[pick]
         if chunk == 1:
-            spread = jnp.transpose(
-                queries.reshape(tokens, 2, 4, 2, group_size, head_dim), (1, 3, 2, 0, 4, 5)
-            ).reshape(head_count, tokens, group_size * head_dim)
-            local_queries = lax.all_to_all(spread, "head", split_axis=0, concat_axis=0, tiled=True)
-            local_queries, picked = lax.optimization_barrier((local_queries, picked))
+            picked, _ = lax.optimization_barrier((picked, mine[0]))
         got = lax.all_to_all(picked, "seq", split_axis=0, concat_axis=0, tiled=True)
         mine.append(got)
         peer.append(lax.ppermute(got, "head", partner))
+    spread = jnp.transpose(
+        queries.reshape(tokens, 2, 4, 2, group_size, head_dim), (1, 3, 2, 0, 4, 5)
+    ).reshape(head_count, tokens, group_size * head_dim)
+    spread, _, _ = lax.optimization_barrier((spread, mine[1], peer[0]))
+    local_queries = lax.all_to_all(spread, "head", split_axis=0, concat_axis=0, tiled=True)
     local_queries = local_queries.reshape(seq_rows, group_size * head_dim)
     which = jnp.where(my_place // 2 == half, 0, 2) + my_place % 2
     slot_index = jnp.where(my_live, my_owner, 0).reshape(qblocks, slot_total - 1)

time: 368 us -> 342 us (0.929)
  the two profiles are of different devices: /device:TPU:64 before, /device:TPU:16 now
where the time goes in v6:
time: 342 us; the launch traced here: 341 us
  waiting for transfers between devices  171 us (50%)
  blocking collectives  61 us (18%)
  starting transfers between devices  42.6 us (12%)
  Pallas kernels  39.6 us (12%)
  local copies, waits for them, and re-layouts  21.7 us (6%)
  other arithmetic  5.5 us (2%)
    ppermute x2, waiting for transfers between devices, on_device(): peer.append(lax.ppermute(got, 'head', partner))  106 us
    all_to_all x1, blocking collectives, on_device(): lax.all_to_all(attended.reshape(head_count, tokens, width), 'head', split...  61 us
    all_to_all x2, waiting for transfers between devices, on_device(): got = lax.all_to_all(picked, 'seq', split_axis=0, concat_axis=0, tiled=True)  47.4 us
    pallas_call x1, Pallas kernels, attend_all(): pl.pallas_call(kernel, out_shape=jax.ShapeDtypeStruct((seq_rows, width),...  39.6 us
    all_to_all x2, starting transfers between devices, on_device(): got = lax.all_to_all(picked, 'seq', split_axis=0, concat_axis=0, tiled=True)  19.7 us
    all_to_all x1, waiting for transfers between devices, on_device(): lax.all_to_all(kv, 'head', split_axis=0, concat_axis=0, tiled=True)  17.6 us
    all_to_all x1, starting transfers between devices, on_device(): lax.all_to_all(kv, 'head', split_axis=0, concat_axis=0, tiled=True)  12.9 us
  transfers between devices with their start and end apart: 6, of which 4 were waited for; matrix products, arithmetic and copies ran while one was open for 5% of the time, Pallas kernels for 0%

profile of v6, /device:TPU:16, one launch (start us, length us, event | category | flops | bytes accessed | tf_op | source)
XLA Modules:
  0.0 341.3 jit_solution(8414609207507741567)
XLA Ops:
  0.0 1.1 pad_maximum_fusion
  1.1 0.1 reshape.153
  1.3 1.1 broadcast_in_dim.12
  2.4 12.9 %all-to-all-start = ((bf16[16,128,256]{2,1,0:T(8,128)(2,1)}), bf16[16,128,256]{2,1,0:T(8,128)(2,1)S(1)}, u32[]{:S(2)}, u32[]{:S(2)}) async-start(bf16[16,128,256]{2,1,0:T(8,128)(2,1)} %bitcast.6), calls=%async_computation | async-start | bytes 2097152 | tf_op jit(solution)/shard_map/all_to_all | solution.py:142
  15.3 0.7 dynamic-slice_bitcast_fusion
  16.1 0.1 copy.35
  16.2 0.2 reshape.150
  16.5 0.7 dynamic-slice_reduce_fusion.2
  17.7 3.9 %fusion.3 = s32[32,112]{0,1:T(8,128)S(1)} fusion(s32[32,112]{0,1:T(8,128)S(1)} %get-tuple-element.12, pred[32,112]{0,1:T(8,128)(4,1)S(1)} %get-tuple-element.10), kind=kOutput, calls=%fused_computation.6 | output fusion | flops 13758976 | bytes 32256 | tf_op jit(solution)/shard_map/jit(cumsum)/reduce_window_sum | solution.py:108
  21.7 0.2 multiply_reduce_fusion
  21.9 17.6 %all-to-all-done.own_ref = bf16[16,128,256]{2,1,0:T(8,128)(2,1)S(1)} async-done(((bf16[16,128,256]{2,1,0:T(8,128)(2,1)}), bf16[16,128,256]{2,1,0:T(8,128)(2,1)S(1)}, u32[]{:S(2)}, u32[]{:S(2)}) %all-to-all-start) | async-done | bytes 1048608 | tf_op jit(solution)/shard_map/all_to_all | solution.py:142
  39.5 2.0 gather_fusion.1
  41.5 14.2 %all-to-all-start.1 = ((bf16[32,128,256]{2,1,0:T(8,128)(2,1)}), bf16[32,128,256]{2,1,0:T(8,128)(2,1)}, u32[]{:S(2)}, u32[]{:S(2)}) async-start(bf16[32,128,256]{2,1,0:T(8,128)(2,1)} %gather_fusion.1), calls=%async_computation.1 | async-start | bytes 4194304 | tf_op jit(solution)/shard_map/all_to_all | solution.py:154
  55.7 2.0 gather_fusion
  57.7 47.4 %all-to-all-done.1.mine0_ref = bf16[32,128,256]{2,1,0:T(8,128)(2,1)} async-done(((bf16[32,128,256]{2,1,0:T(8,128)(2,1)}), bf16[32,128,256]{2,1,0:T(8,128)(2,1)}, u32[]{:S(2)}, u32[]{:S(2)}) %all-to-all-start.1) | async-done | bytes 2097184 | tf_op jit(solution)/shard_map/all_to_all | solution.py:154
  105.2 5.5 %all-to-all-start.2 = ((bf16[32,128,256]{2,1,0:T(8,128)(2,1)}), bf16[32,128,256]{2,1,0:T(8,128)(2,1)}, u32[]{:S(2)}, u32[]{:S(2)}) async-start(bf16[32,128,256]{2,1,0:T(8,128)(2,1)} %gather_fusion), calls=%async_computation.2 | async-start | bytes 4194304 | tf_op jit(solution)/shard_map/all_to_all | solution.py:154
  110.7 1.9 collective-permute-start
  112.7 2.6 copy.40
  115.2 2.2 reshape.152
  117.4 43.2 %collective-permute-done.peer0_ref = bf16[32,128,256]{2,1,0:T(8,128)(2,1)} collective-permute-done((bf16[32,128,256]{2,1,0:T(8,128)(2,1)}, bf16[32,128,256]{2,1,0:T(8,128)(2,1)}, u32[]{:S(2)}, u32[]{:S(2)}) %collective-permute-start) | collective-permute-done | bytes 2097184 | tf_op jit(solution)/shard_map/ppermute | solution.py:156
  160.6 4.4 %all-to-all-start.3 = ((bf16[16,128,512]{2,1,0:T(8,128)(2,1)}), bf16[16,128,512]{2,1,0:T(8,128)(2,1)}, u32[]{:S(2)}, u32[]{:S(2)}) async-start(bf16[16,128,512]{2,1,0:T(8,128)(2,1)} %reshape.152), calls=%async_computation.3 | async-start | bytes 4194304 | tf_op jit(solution)/shard_map/all_to_all | solution.py:161
  165.1 3.7 %collective-permute-start.1 = (bf16[32,128,256]{2,1,0:T(8,128)(2,1)}, bf16[32,128,256]{2,1,0:T(8,128)(2,1)}, u32[]{:S(2)}, u32[]{:S(2)}) collective-permute-start(bf16[32,128,256]{2,1,0:T(8,128)(2,1)} %all-to-all-done.2.mine1_ref), channel_id=1, source_target_pairs={{0,4},{1,5},{2,6},{3,7},{4,0},{5,1},{6,2},{7,3},{8,12},{9,13},{10,... | collective-permute-start | bytes 6291464 | tf_op jit(solution)/shard_map/ppermute | solution.py:156
  168.7 0.2 minimum_reduce_fusion
  169.1 0.2 dynamic-slice_reduce_fusion.1
  169.4 0.7 concatenate.10.which_ref
  170.1 0.7 concatenate.9.slot_ref
  170.8 1.3 dynamic-slice_bitcast_fusion.1.count_ref
  172.1 62.4 %collective-permute-done.1.peer1_ref = bf16[32,128,256]{2,1,0:T(8,128)(2,1)} collective-permute-done((bf16[32,128,256]{2,1,0:T(8,128)(2,1)}, bf16[32,128,256]{2,1,0:T(8,128)(2,1)}, u32[]{:S(2)}, u32[]{:S(2)}) %collective-permute-start.1) | collective-permute-done | bytes 2097184 | tf_op jit(solution)/shard_map/ppermute | solution.py:156
  234.5 39.6 %shard_map.55 = bf16[2048,512]{1,0:T(8,128)(2,1)} custom-call(s32[16,8]{1,0:T(8,128)} %concatenate.9.slot_ref, s32[16,8]{1,0:T(8,128)} %concatenate.10.which_ref, s32[16]{0:T(128)} %dynamic-slice_bitcast_fusion.1.count_ref, bf16[2048,512]{1,0:T(8,128)(2,1)} %bitcast.9.query_ref, bf16[16,128,256]{2,1,0:T(8,128)(2,1)} %copy-done, ...), custom_call_target="tpu_custom_call" | custom-call | tf_op jit(solution)/shard_map/pallas_call | solution.py:76
  274.1 61.0 %all_to_all.25 = bf16[16,128,512]{2,1,0:T(8,128)(2,1)S(1)} all-to-all(bf16[16,128,512]{2,1,0:T(8,128)(2,1)} %bitcast.22), channel_id=1, replica_groups=mesh['seq'=32,'head'=16] {'head'}, dimensions={0} | all-to-all | bytes 4194304 | tf_op jit(solution)/shard_map/all_to_all | solution.py:175
  335.2 2.1 reshape.157
  337.2 4.1 %copy.45 = bf16[2,2,4,128,4,128]{5,4,1,2,0,3:T(4,128)(2,1)} copy(bf16[2,2,4,128,4,128]{5,4,3,2,1,0:T(4,128)(2,1)} %reshape.157) | data formatting | bytes 4194304 | tf_op jit(solution)/shard_map/reshape | solution.py:179
  (26 shorter events, 1.1 us)
Async XLA Ops:
  2.4 37.1 %all-to-all-start = ((bf16[16,128,256]{2,1,0:T(8,128)(2,1)}), bf16[16,128,256]{2,1,0:T(8,128)(2,1)S(1)}, u32[]{:S(2)}, u32[]{:S(2)}) async-start(bf16[16,128,256]{2,1,0:T(8,128)(2,1)} %bitcast.6), calls=%async_computation | async-start | bytes 2097152 | tf_op jit(solution)/shard_map/all_to_all | solution.py:142
  39.5 16.2 %copy-start = (bf16[16,128,256]{2,1,0:T(8,128)(2,1)}, bf16[16,128,256]{2,1,0:T(8,128)(2,1)S(1)}, u32[]{:S(2)}) copy-start(bf16[16,128,256]{2,1,0:T(8,128)(2,1)S(1)} %all-to-all-done.own_ref) | copy-start | bytes 3145732
  41.5 63.7 %all-to-all-start.1 = ((bf16[32,128,256]{2,1,0:T(8,128)(2,1)}), bf16[32,128,256]{2,1,0:T(8,128)(2,1)}, u32[]{:S(2)}, u32[]{:S(2)}) async-start(bf16[32,128,256]{2,1,0:T(8,128)(2,1)} %gather_fusion.1), calls=%async_computation.1 | async-start | bytes 4194304 | tf_op jit(solution)/shard_map/all_to_all | solution.py:154
  105.2 55.5 %all-to-all-start.2 = ((bf16[32,128,256]{2,1,0:T(8,128)(2,1)}), bf16[32,128,256]{2,1,0:T(8,128)(2,1)}, u32[]{:S(2)}, u32[]{:S(2)}) async-start(bf16[32,128,256]{2,1,0:T(8,128)(2,1)} %gather_fusion), calls=%async_computation.2 | async-start | bytes 4194304 | tf_op jit(solution)/shard_map/all_to_all | solution.py:154
  110.7 49.9 %collective-permute-start = (bf16[32,128,256]{2,1,0:T(8,128)(2,1)}, bf16[32,128,256]{2,1,0:T(8,128)(2,1)}, u32[]{:S(2)}, u32[]{:S(2)}) collective-permute-start(bf16[32,128,256]{2,1,0:T(8,128)(2,1)} %all-to-all-done.1.mine0_ref), channel_id=1, source_target_pairs={{0,4},{1,5},{2,6},{3,7},{4,0},{5,1},{6,2},{7,3},{8,12},{9,13},{10,... | collective-permute-start | bytes 6291464 | tf_op jit(solution)/shard_map/ppermute | solution.py:156
  160.6 73.9 %all-to-all-start.3 = ((bf16[16,128,512]{2,1,0:T(8,128)(2,1)}), bf16[16,128,512]{2,1,0:T(8,128)(2,1)}, u32[]{:S(2)}, u32[]{:S(2)}) async-start(bf16[16,128,512]{2,1,0:T(8,128)(2,1)} %reshape.152), calls=%async_computation.3 | async-start | bytes 4194304 | tf_op jit(solution)/shard_map/all_to_all | solution.py:161
  165.1 69.4 %collective-permute-start.1 = (bf16[32,128,256]{2,1,0:T(8,128)(2,1)}, bf16[32,128,256]{2,1,0:T(8,128)(2,1)}, u32[]{:S(2)}, u32[]{:S(2)}) collective-permute-start(bf16[32,128,256]{2,1,0:T(8,128)(2,1)} %all-to-all-done.2.mine1_ref), channel_id=1, source_target_pairs={{0,4},{1,5},{2,6},{3,7},{4,0},{5,1},{6,2},{7,3},{8,12},{9,13},{10,... | collective-permute-start | bytes 6291464 | tf_op jit(solution)/shard_map/ppermute | solution.py:156

commit v7 on v6

--- a/solution.py
+++ b/solution.py
@@ -43,14 +43,15 @@
             part = jnp.where(slot < row_count, part, NEG_FILL)
         scores.append(part)
         values.append(value)
-    row_max = jnp.max(scores[0], axis=1, keepdims=True)
+    lane_max = scores[0]
     for part in scores[1:]:
-        row_max = jnp.maximum(row_max, jnp.max(part, axis=1, keepdims=True))
+        lane_max = jnp.maximum(lane_max, part)
+    row_max = jnp.max(lane_max, axis=1, keepdims=True)
     weights = [jnp.exp(part - row_max) for part in scores]
-    total = jnp.sum(weights[0], axis=1, keepdims=True)
+    lane_sum = weights[0]
     for part in weights[1:]:
-        total = total + jnp.sum(part, axis=1, keepdims=True)
-    inverse = 1.0 / total
+        lane_sum = lane_sum + part
+    inverse = 1.0 / jnp.sum(lane_sum, axis=1, keepdims=True)
     acc = None
     for part, value in zip(weights, values):
         probs = (part * inverse).astype(jnp.bfloat16)

time: 342 us -> 340 us (level)
  no operation moved by 1% of the time
where the time goes in v7:
time: 340 us; the launch traced here: 339 us
  waiting for transfers between devices  171 us (50%)
  blocking collectives  61 us (18%)
  starting transfers between devices  42.6 us (13%)
  Pallas kernels  37.5 us (11%)
  local copies, waits for them, and re-layouts  21.7 us (6%)
  other arithmetic  5.5 us (2%)
    ppermute x2, waiting for transfers between devices, on_device(): peer.append(lax.ppermute(got, 'head', partner))  106 us
    all_to_all x1, blocking collectives, on_device(): lax.all_to_all(attended.reshape(head_count, tokens, width), 'head', split...  61 us
    all_to_all x2, waiting for transfers between devices, on_device(): got = lax.all_to_all(picked, 'seq', split_axis=0, concat_axis=0, tiled=True)  47.4 us
    pallas_call x1, Pallas kernels, attend_all(): pl.pallas_call(kernel, out_shape=jax.ShapeDtypeStruct((seq_rows, width),...  37.5 us
    all_to_all x2, starting transfers between devices, on_device(): got = lax.all_to_all(picked, 'seq', split_axis=0, concat_axis=0, tiled=True)  19.7 us
    all_to_all x1, waiting for transfers between devices, on_device(): lax.all_to_all(kv, 'head', split_axis=0, concat_axis=0, tiled=True)  17.6 us
    all_to_all x1, starting transfers between devices, on_device(): lax.all_to_all(kv, 'head', split_axis=0, concat_axis=0, tiled=True)  12.9 us
  transfers between devices with their start and end apart: 6, of which 4 were waited for; matrix products, arithmetic and copies ran while one was open for 5% of the time, Pallas kernels for 0%

profile of v7, /device:TPU:16, one launch (start us, length us, event | category | flops | bytes accessed | tf_op | source)
XLA Modules:
  0.0 339.2 jit_solution(9459330867904035115)
XLA Ops:
  0.0 1.1 pad_maximum_fusion
  1.1 0.1 reshape.153
  1.3 1.1 broadcast_in_dim.12
  2.4 12.9 %all-to-all-start = ((bf16[16,128,256]{2,1,0:T(8,128)(2,1)}), bf16[16,128,256]{2,1,0:T(8,128)(2,1)S(1)}, u32[]{:S(2)}, u32[]{:S(2)}) async-start(bf16[16,128,256]{2,1,0:T(8,128)(2,1)} %bitcast.6), calls=%async_computation | async-start | bytes 2097152 | tf_op jit(solution)/shard_map/all_to_all | solution.py:143
  15.3 0.7 dynamic-slice_bitcast_fusion
  16.1 0.1 copy.35
  16.2 0.2 reshape.150
  16.5 0.7 dynamic-slice_reduce_fusion.2
  17.7 3.9 %fusion.3 = s32[32,112]{0,1:T(8,128)S(1)} fusion(s32[32,112]{0,1:T(8,128)S(1)} %get-tuple-element.12, pred[32,112]{0,1:T(8,128)(4,1)S(1)} %get-tuple-element.10), kind=kOutput, calls=%fused_computation.6 | output fusion | flops 13758976 | bytes 32256 | tf_op jit(solution)/shard_map/jit(cumsum)/reduce_window_sum | solution.py:109
  21.7 0.2 multiply_reduce_fusion
  21.9 17.6 %all-to-all-done.own_ref = bf16[16,128,256]{2,1,0:T(8,128)(2,1)S(1)} async-done(((bf16[16,128,256]{2,1,0:T(8,128)(2,1)}), bf16[16,128,256]{2,1,0:T(8,128)(2,1)S(1)}, u32[]{:S(2)}, u32[]{:S(2)}) %all-to-all-start) | async-done | bytes 1048608 | tf_op jit(solution)/shard_map/all_to_all | solution.py:143
  39.5 2.0 gather_fusion.1
  41.5 14.2 %all-to-all-start.1 = ((bf16[32,128,256]{2,1,0:T(8,128)(2,1)}), bf16[32,128,256]{2,1,0:T(8,128)(2,1)}, u32[]{:S(2)}, u32[]{:S(2)}) async-start(bf16[32,128,256]{2,1,0:T(8,128)(2,1)} %gather_fusion.1), calls=%async_computation.1 | async-start | bytes 4194304 | tf_op jit(solution)/shard_map/all_to_all | solution.py:155
  55.7 2.0 gather_fusion
  57.7 47.4 %all-to-all-done.1.mine0_ref = bf16[32,128,256]{2,1,0:T(8,128)(2,1)} async-done(((bf16[32,128,256]{2,1,0:T(8,128)(2,1)}), bf16[32,128,256]{2,1,0:T(8,128)(2,1)}, u32[]{:S(2)}, u32[]{:S(2)}) %all-to-all-start.1) | async-done | bytes 2097184 | tf_op jit(solution)/shard_map/all_to_all | solution.py:155
  105.2 5.5 %all-to-all-start.2 = ((bf16[32,128,256]{2,1,0:T(8,128)(2,1)}), bf16[32,128,256]{2,1,0:T(8,128)(2,1)}, u32[]{:S(2)}, u32[]{:S(2)}) async-start(bf16[32,128,256]{2,1,0:T(8,128)(2,1)} %gather_fusion), calls=%async_computation.2 | async-start | bytes 4194304 | tf_op jit(solution)/shard_map/all_to_all | solution.py:155
  110.7 1.9 collective-permute-start
  112.7 2.6 copy.40
  115.2 2.2 reshape.152
  117.4 43.2 %collective-permute-done.peer0_ref = bf16[32,128,256]{2,1,0:T(8,128)(2,1)} collective-permute-done((bf16[32,128,256]{2,1,0:T(8,128)(2,1)}, bf16[32,128,256]{2,1,0:T(8,128)(2,1)}, u32[]{:S(2)}, u32[]{:S(2)}) %collective-permute-start) | collective-permute-done | bytes 2097184 | tf_op jit(solution)/shard_map/ppermute | solution.py:157
  160.6 4.4 %all-to-all-start.3 = ((bf16[16,128,512]{2,1,0:T(8,128)(2,1)}), bf16[16,128,512]{2,1,0:T(8,128)(2,1)}, u32[]{:S(2)}, u32[]{:S(2)}) async-start(bf16[16,128,512]{2,1,0:T(8,128)(2,1)} %reshape.152), calls=%async_computation.3 | async-start | bytes 4194304 | tf_op jit(solution)/shard_map/all_to_all | solution.py:162
  165.1 3.7 %collective-permute-start.1 = (bf16[32,128,256]{2,1,0:T(8,128)(2,1)}, bf16[32,128,256]{2,1,0:T(8,128)(2,1)}, u32[]{:S(2)}, u32[]{:S(2)}) collective-permute-start(bf16[32,128,256]{2,1,0:T(8,128)(2,1)} %all-to-all-done.2.mine1_ref), channel_id=1, source_target_pairs={{0,4},{1,5},{2,6},{3,7},{4,0},{5,1},{6,2},{7,3},{8,12},{9,13},{10,... | collective-permute-start | bytes 6291464 | tf_op jit(solution)/shard_map/ppermute | solution.py:157
  168.7 0.2 minimum_reduce_fusion
  169.1 0.2 dynamic-slice_reduce_fusion.1
  169.4 0.7 concatenate.10.which_ref
  170.1 0.7 concatenate.9.slot_ref
  170.8 1.3 dynamic-slice_bitcast_fusion.1.count_ref
  172.1 62.4 %collective-permute-done.1.peer1_ref = bf16[32,128,256]{2,1,0:T(8,128)(2,1)} collective-permute-done((bf16[32,128,256]{2,1,0:T(8,128)(2,1)}, bf16[32,128,256]{2,1,0:T(8,128)(2,1)}, u32[]{:S(2)}, u32[]{:S(2)}) %collective-permute-start.1) | collective-permute-done | bytes 2097184 | tf_op jit(solution)/shard_map/ppermute | solution.py:157
  234.5 37.5 %shard_map.55 = bf16[2048,512]{1,0:T(8,128)(2,1)} custom-call(s32[16,8]{1,0:T(8,128)} %concatenate.9.slot_ref, s32[16,8]{1,0:T(8,128)} %concatenate.10.which_ref, s32[16]{0:T(128)} %dynamic-slice_bitcast_fusion.1.count_ref, bf16[2048,512]{1,0:T(8,128)(2,1)} %bitcast.9.query_ref, bf16[16,128,256]{2,1,0:T(8,128)(2,1)} %copy-done, ...), custom_call_target="tpu_custom_call" | custom-call | tf_op jit(solution)/shard_map/pallas_call | solution.py:77
  272.0 61.0 %all_to_all.25 = bf16[16,128,512]{2,1,0:T(8,128)(2,1)S(1)} all-to-all(bf16[16,128,512]{2,1,0:T(8,128)(2,1)} %bitcast.22), channel_id=1, replica_groups=mesh['seq'=32,'head'=16] {'head'}, dimensions={0} | all-to-all | bytes 4194304 | tf_op jit(solution)/shard_map/all_to_all | solution.py:176
  333.0 2.1 reshape.157
  335.1 4.1 %copy.45 = bf16[2,2,4,128,4,128]{5,4,1,2,0,3:T(4,128)(2,1)} copy(bf16[2,2,4,128,4,128]{5,4,3,2,1,0:T(4,128)(2,1)} %reshape.157) | data formatting | bytes 4194304 | tf_op jit(solution)/shard_map/reshape | solution.py:180
  (26 shorter events, 1.1 us)
Async XLA Ops:
  2.4 37.1 %all-to-all-start = ((bf16[16,128,256]{2,1,0:T(8,128)(2,1)}), bf16[16,128,256]{2,1,0:T(8,128)(2,1)S(1)}, u32[]{:S(2)}, u32[]{:S(2)}) async-start(bf16[16,128,256]{2,1,0:T(8,128)(2,1)} %bitcast.6), calls=%async_computation | async-start | bytes 2097152 | tf_op jit(solution)/shard_map/all_to_all | solution.py:143
  39.5 16.2 %copy-start = (bf16[16,128,256]{2,1,0:T(8,128)(2,1)}, bf16[16,128,256]{2,1,0:T(8,128)(2,1)S(1)}, u32[]{:S(2)}) copy-start(bf16[16,128,256]{2,1,0:T(8,128)(2,1)S(1)} %all-to-all-done.own_ref) | copy-start | bytes 3145732
  41.5 63.7 %all-to-all-start.1 = ((bf16[32,128,256]{2,1,0:T(8,128)(2,1)}), bf16[32,128,256]{2,1,0:T(8,128)(2,1)}, u32[]{:S(2)}, u32[]{:S(2)}) async-start(bf16[32,128,256]{2,1,0:T(8,128)(2,1)} %gather_fusion.1), calls=%async_computation.1 | async-start | bytes 4194304 | tf_op jit(solution)/shard_map/all_to_all | solution.py:155
  105.2 55.5 %all-to-all-start.2 = ((bf16[32,128,256]{2,1,0:T(8,128)(2,1)}), bf16[32,128,256]{2,1,0:T(8,128)(2,1)}, u32[]{:S(2)}, u32[]{:S(2)}) async-start(bf16[32,128,256]{2,1,0:T(8,128)(2,1)} %gather_fusion), calls=%async_computation.2 | async-start | bytes 4194304 | tf_op jit(solution)/shard_map/all_to_all | solution.py:155
  110.7 49.9 %collective-permute-start = (bf16[32,128,256]{2,1,0:T(8,128)(2,1)}, bf16[32,128,256]{2,1,0:T(8,128)(2,1)}, u32[]{:S(2)}, u32[]{:S(2)}) collective-permute-start(bf16[32,128,256]{2,1,0:T(8,128)(2,1)} %all-to-all-done.1.mine0_ref), channel_id=1, source_target_pairs={{0,4},{1,5},{2,6},{3,7},{4,0},{5,1},{6,2},{7,3},{8,12},{9,13},{10,... | collective-permute-start | bytes 6291464 | tf_op jit(solution)/shard_map/ppermute | solution.py:157
  160.6 73.9 %all-to-all-start.3 = ((bf16[16,128,512]{2,1,0:T(8,128)(2,1)}), bf16[16,128,512]{2,1,0:T(8,128)(2,1)}, u32[]{:S(2)}, u32[]{:S(2)}) async-start(bf16[16,128,512]{2,1,0:T(8,128)(2,1)} %reshape.152), calls=%async_computation.3 | async-start | bytes 4194304 | tf_op jit(solution)/shard_map/all_to_all | solution.py:162
  165.1 69.4 %collective-permute-start.1 = (bf16[32,128,256]{2,1,0:T(8,128)(2,1)}, bf16[32,128,256]{2,1,0:T(8,128)(2,1)}, u32[]{:S(2)}, u32[]{:S(2)}) collective-permute-start(bf16[32,128,256]{2,1,0:T(8,128)(2,1)} %all-to-all-done.2.mine1_ref), channel_id=1, source_target_pairs={{0,4},{1,5},{2,6},{3,7},{4,0},{5,1},{6,2},{7,3},{8,12},{9,13},{10,... | collective-permute-start | bytes 6291464 | tf_op jit(solution)/shard_map/ppermute | solution.py:157

commit v8 on v7

--- a/solution.py
+++ b/solution.py
@@ -13,7 +13,7 @@
 NEG_FILL = -1e30
 
 
-def attend_kernel(slot_ref, which_ref, count_ref, query_ref, own_ref, mine0_ref, mine1_ref,
+def attend_kernel(slot_ref, which_ref, count_ref, qrow_ref, query_ref, own_ref, mine0_ref, mine1_ref,
                   peer0_ref, peer1_ref, out_ref, block_buf, *, score_scale, slot_total, heads):
     row = pl.program_id(0)
     head_dim = block_buf.shape[2] // 2
@@ -64,32 +64,32 @@
         )
 
 
-def attend_all(local_queries, column, width, own_blocks, received, slot_index, slot_which,
+def attend_all(local_queries, query_row, width, own_blocks, received, slot_index, slot_which,
                row_counts, score_scale):
-    seq_rows = local_queries.shape[0]
+    seq_rows = local_queries.shape[0] * local_queries.shape[1]
     qblocks, _, pair_dim = own_blocks.shape
     head_dim = pair_dim // 2
     slot_total = slot_index.shape[1]
     kernel = partial(
         attend_kernel, score_scale=score_scale, slot_total=slot_total, heads=width // head_dim
     )
-    whole = lambda shape: pl.BlockSpec(shape, lambda r, s, w, c: (0,) * len(shape))
+    whole = lambda shape: pl.BlockSpec(shape, lambda r, s, w, c, q: (0,) * len(shape))
     return pl.pallas_call(
         kernel,
         out_shape=jax.ShapeDtypeStruct((seq_rows, width), local_queries.dtype),
         grid_spec=pltpu.PrefetchScalarGridSpec(
-            num_scalar_prefetch=3,
+            num_scalar_prefetch=4,
             grid=(qblocks,),
             in_specs=[
-                pl.BlockSpec((BLK, width), lambda r, s, w, c: (r, column)),
+                pl.BlockSpec((None, BLK, width), lambda r, s, w, c, q: (q[r], 0, 0)),
                 whole(own_blocks.shape),
             ]
             + [whole(part.shape) for part in received],
-            out_specs=pl.BlockSpec((BLK, width), lambda r, s, w, c: (r, 0)),
+            out_specs=pl.BlockSpec((BLK, width), lambda r, s, w, c, q: (r, 0)),
             scratch_shapes=[pltpu.VMEM((slot_total - 1, BLK, pair_dim), own_blocks.dtype)],
         ),
         compiler_params=pltpu.CompilerParams(vmem_limit_bytes=100 * 1024 * 1024),
-    )(slot_index, slot_which, row_counts, local_queries, own_blocks, *received)
+    )(slot_index, slot_which, row_counts, query_row, local_queries, own_blocks, *received)
 
 
 def make_plan(block_lists, block_counts, group_head, seq_index, shard_count, qblocks, capacity):
@@ -158,9 +158,15 @@
     spread = jnp.transpose(
         queries.reshape(tokens, 2, 4, 2, group_size, head_dim), (1, 3, 2, 0, 4, 5)
     ).reshape(head_count, tokens, group_size * head_dim)
-    spread, _, _ = lax.optimization_barrier((spread, mine[1], peer[0]))
-    local_queries = lax.all_to_all(spread, "head", split_axis=0, concat_axis=0, tiled=True)
-    local_queries = local_queries.reshape(seq_rows, group_size * head_dim)
+    pieces = [lax.dynamic_index_in_dim(spread, head_index, 0, keepdims=False)]
+    for shift in range(1, head_count):
+        piece = lax.dynamic_index_in_dim(spread, (head_index + shift) % head_count, 0,
+                                         keepdims=False)
+        pieces.append(lax.ppermute(
+            piece, "head", [(h, (h + shift) % head_count) for h in range(head_count)]
+        ))
+    local_queries = jnp.stack(pieces)
+    query_row = (head_index - jnp.arange(qblocks, dtype=jnp.int32)) % head_count
     which = jnp.where(my_place // 2 == half, 0, 2) + my_place % 2
     slot_index = jnp.where(my_live, my_owner, 0).reshape(qblocks, slot_total - 1)
     slot_which = jnp.where(my_live, which, 0).reshape(qblocks, slot_total - 1)
@@ -170,7 +176,7 @@
     score_scale = head_dim ** (-0.5)
     width = group_size * head_dim
     attended = attend_all(
-        local_queries, 0, width, own_blocks, mine + peer, slot_index, slot_which,
+        local_queries, query_row, width, own_blocks, mine + peer, slot_index, slot_which,
         my_counts, score_scale
     )
     back = lax.all_to_all(

time: 340 us -> 448 us (1.32)
  the two profiles are of different devices: /device:TPU:16 before, /device:TPU:88 now
where the time goes in v8:
time: 448 us; the launch traced here: 447 us
  waiting for transfers between devices  212 us (47%)
  starting transfers between devices  103 us (23%)
  blocking collectives  52 us (12%)
  Pallas kernels  37.7 us (8%)
  local copies, waits for them, and re-layouts  34.5 us (8%)
  other arithmetic  6.12 us (1%)
    ppermute x15, waiting for transfers between devices, on_device(): lax.ppermute(piece, 'head', [(h, (h + shift) % head_count) for h in range...  143 us
    ppermute x15, starting transfers between devices, on_device(): lax.ppermute(piece, 'head', [(h, (h + shift) % head_count) for h in range...  69.7 us
    all_to_all x1, blocking collectives, on_device(): lax.all_to_all(attended.reshape(head_count, tokens, width), 'head', split...  52 us
    all_to_all x2, waiting for transfers between devices, on_device(): got = lax.all_to_all(picked, 'seq', split_axis=0, concat_axis=0, tiled=True)  45.6 us
    pallas_call x1, Pallas kernels, attend_all(): pl.pallas_call(kernel, out_shape=jax.ShapeDtypeStruct((seq_rows, width),...  37.7 us
    all_to_all x1, waiting for transfers between devices, on_device(): lax.all_to_all(kv, 'head', split_axis=0, concat_axis=0, tiled=True)  23.2 us
    all_to_all x2, starting transfers between devices, on_device(): got = lax.all_to_all(picked, 'seq', split_axis=0, concat_axis=0, tiled=True)  15.8 us
    all_to_all x1, starting transfers between devices, on_device(): lax.all_to_all(kv, 'head', split_axis=0, concat_axis=0, tiled=True)  12 us
  transfers between devices with their start and end apart: 20, of which 13 were waited for; matrix products, arithmetic and copies ran while one was open for 7% of the time, Pallas kernels for 0%

profile of v8, /device:TPU:88, one launch (start us, length us, event | category | flops | bytes accessed | tf_op | source)
XLA Modules:
  0.0 446.5 jit_solution(17020861355041261383)
XLA Ops:
  2.4 12.0 %all-to-all-start = ((bf16[16,128,256]{2,1,0:T(8,128)(2,1)}), bf16[16,128,256]{2,1,0:T(8,128)(2,1)S(1)}, u32[]{:S(2)}, u32[]{:S(2)}) async-start(bf16[16,128,256]{2,1,0:T(8,128)(2,1)} %bitcast.36), calls=%async_computation | async-start | bytes 2097152 | tf_op jit(solution)/shard_map/all_to_all | solution.py:143
  16.9 3.9 fusion.3
  21.0 23.2 %all-to-all-done.own_ref = bf16[16,128,256]{2,1,0:T(8,128)(2,1)S(1)} async-done(((bf16[16,128,256]{2,1,0:T(8,128)(2,1)}), bf16[16,128,256]{2,1,0:T(8,128)(2,1)S(1)}, u32[]{:S(2)}, u32[]{:S(2)}) %all-to-all-start) | async-done | bytes 1048608 | tf_op jit(solution)/shard_map/all_to_all | solution.py:143
  46.2 8.4 %all-to-all-start.1 = ((bf16[32,128,256]{2,1,0:T(8,128)(2,1)}), bf16[32,128,256]{2,1,0:T(8,128)(2,1)S(1)}, u32[]{:S(2)}, u32[]{:S(2)}) async-start(bf16[32,128,256]{2,1,0:T(8,128)(2,1)} %gather_fusion), calls=%async_computation.1 | async-start | bytes 4194304 | tf_op jit(solution)/shard_map/all_to_all | solution.py:155
  56.7 45.6 %all-to-all-done.1.mine0_ref = bf16[32,128,256]{2,1,0:T(8,128)(2,1)S(1)} async-done(((bf16[32,128,256]{2,1,0:T(8,128)(2,1)}), bf16[32,128,256]{2,1,0:T(8,128)(2,1)S(1)}, u32[]{:S(2)}, u32[]{:S(2)}) %all-to-all-start.1) | async-done | bytes 2097184 | tf_op jit(solution)/shard_map/all_to_all | solution.py:155
  102.2 7.4 %all-to-all-start.2 = ((bf16[32,128,256]{2,1,0:T(8,128)(2,1)}), bf16[32,128,256]{2,1,0:T(8,128)(2,1)}, u32[]{:S(2)}, u32[]{:S(2)}) async-start(bf16[32,128,256]{2,1,0:T(8,128)(2,1)} %gather_fusion.1), calls=%async_computation.2 | async-start | bytes 4194304 | tf_op jit(solution)/shard_map/all_to_all | solution.py:155
  109.8 3.9 copy.47
  113.7 2.7 reshape.149
  117.6 4.2 collective-permute-start.14
  121.8 4.4 collective-permute-start.13
  128.6 5.8 %collective-permute-start.5 = (bf16[128,512]{1,0:T(8,128)(2,1)S(1)}, bf16[128,512]{1,0:T(8,128)(2,1)S(1)}, u32[]{:S(2)}, u32[]{:S(2)}) collective-permute-start(bf16[128,512]{1,0:T(8,128)(2,1)S(1)} %get-tuple-element.18), channel_id=1, source_target_pairs={{0,6},{1,7},{2,8},{3,9},{4,10},{5,11},{6,12},{7,13},{8,14},{9,15},... | collective-permute-start | bytes 393224 | tf_op jit(solution)/shard_map/ppermute | solution.py:165
  134.4 4.3 collective-permute-start
  142.6 4.4 collective-permute-done
  147.0 4.2 collective-permute-start.1
  152.0 15.9 %collective-permute-done.1 = bf16[128,512]{1,0:T(8,128)(2,1)S(1)} collective-permute-done((bf16[128,512]{1,0:T(8,128)(2,1)}, bf16[128,512]{1,0:T(8,128)(2,1)S(1)}, u32[]{:S(2)}, u32[]{:S(2)}) %collective-permute-start.1) | collective-permute-done | bytes 131104 | tf_op jit(solution)/shard_map/ppermute | solution.py:165
  167.9 4.1 collective-permute-start.2
  172.6 5.9 %collective-permute-done.2 = bf16[128,512]{1,0:T(8,128)(2,1)S(1)} collective-permute-done((bf16[128,512]{1,0:T(8,128)(2,1)}, bf16[128,512]{1,0:T(8,128)(2,1)S(1)}, u32[]{:S(2)}, u32[]{:S(2)}) %collective-permute-start.2) | collective-permute-done | bytes 131104 | tf_op jit(solution)/shard_map/ppermute | solution.py:165
  181.1 5.7 %collective-permute-done.3 = bf16[128,512]{1,0:T(8,128)(2,1)S(1)} collective-permute-done((bf16[128,512]{1,0:T(8,128)(2,1)}, bf16[128,512]{1,0:T(8,128)(2,1)S(1)}, u32[]{:S(2)}, u32[]{:S(2)}) %collective-permute-start.3) | collective-permute-done | bytes 131104 | tf_op jit(solution)/shard_map/ppermute | solution.py:165
  189.3 9.6 %collective-permute-done.4 = bf16[128,512]{1,0:T(8,128)(2,1)S(1)} collective-permute-done((bf16[128,512]{1,0:T(8,128)(2,1)}, bf16[128,512]{1,0:T(8,128)(2,1)S(1)}, u32[]{:S(2)}, u32[]{:S(2)}) %collective-permute-start.4) | collective-permute-done | bytes 131104 | tf_op jit(solution)/shard_map/ppermute | solution.py:165
  201.6 3.9 collective-permute-start.16
  209.4 83.3 %collective-permute-done.7 = bf16[128,512]{1,0:T(8,128)(2,1)S(1)} collective-permute-done((bf16[128,512]{1,0:T(8,128)(2,1)S(1)}, bf16[128,512]{1,0:T(8,128)(2,1)S(1)}, u32[]{:S(2)}, u32[]{:S(2)}) %collective-permute-start.7) | collective-permute-done | bytes 131104 | tf_op jit(solution)/shard_map/ppermute | solution.py:165
  292.7 4.2 collective-permute-start.8
  297.6 6.1 %collective-permute-done.8 = bf16[128,512]{1,0:T(8,128)(2,1)S(1)} collective-permute-done((bf16[128,512]{1,0:T(8,128)(2,1)S(1)}, bf16[128,512]{1,0:T(8,128)(2,1)S(1)}, u32[]{:S(2)}, u32[]{:S(2)}) %collective-permute-start.8) | collective-permute-done | bytes 131104 | tf_op jit(solution)/shard_map/ppermute | solution.py:165
  303.7 11.8 %collective-permute-start.9 = (bf16[128,512]{1,0:T(8,128)(2,1)S(1)}, bf16[128,512]{1,0:T(8,128)(2,1)S(1)}, u32[]{:S(2)}, u32[]{:S(2)}) collective-permute-start(bf16[128,512]{1,0:T(8,128)(2,1)S(1)} %get-tuple-element.14), channel_id=1, source_target_pairs={{0,10},{1,11},{2,12},{3,13},{4,14},{5,15},{6,0},{7,1},{8,2},{9,3},... | collective-permute-start | bytes 393224 | tf_op jit(solution)/shard_map/ppermute | solution.py:165
  318.0 5.0 %collective-permute-start.10 = (bf16[128,512]{1,0:T(8,128)(2,1)S(1)}, bf16[128,512]{1,0:T(8,128)(2,1)S(1)}, u32[]{:S(2)}, u32[]{:S(2)}) collective-permute-start(bf16[128,512]{1,0:T(8,128)(2,1)S(1)} %get-tuple-element.13), channel_id=1, source_target_pairs={{0,11},{1,12},{2,13},{3,14},{4,15},{5,0},{6,1},{7,2},{8,3},{9,4},{... | collective-permute-start | bytes 393224 | tf_op jit(solution)/shard_map/ppermute | solution.py:165
  323.7 3.0 collective-permute-done.10
  326.8 6.4 %collective-permute-start.11 = (bf16[128,512]{1,0:T(8,128)(2,1)S(1)}, bf16[128,512]{1,0:T(8,128)(2,1)S(1)}, u32[]{:S(2)}, u32[]{:S(2)}) collective-permute-start(bf16[128,512]{1,0:T(8,128)(2,1)S(1)} %get-tuple-element.12), channel_id=1, source_target_pairs={{0,12},{1,13},{2,14},{3,15},{4,0},{5,1},{6,2},{7,3},{8,4},{9,5},{1... | collective-permute-start | bytes 393224 | tf_op jit(solution)/shard_map/ppermute | solution.py:165
  335.7 6.6 %collective-permute-start.12 = (bf16[128,512]{1,0:T(8,128)(2,1)S(1)}, bf16[128,512]{1,0:T(8,128)(2,1)S(1)}, u32[]{:S(2)}, u32[]{:S(2)}) collective-permute-start(bf16[128,512]{1,0:T(8,128)(2,1)S(1)} %get-tuple-element.11), channel_id=1, source_target_pairs={{0,13},{1,14},{2,15},{3,0},{4,1},{5,2},{6,3},{7,4},{8,5},{9,6},{10... | collective-permute-start | bytes 393224 | tf_op jit(solution)/shard_map/ppermute | solution.py:165
  343.0 5.7 %collective-permute-done.12 = bf16[128,512]{1,0:T(8,128)(2,1)S(1)} collective-permute-done((bf16[128,512]{1,0:T(8,128)(2,1)S(1)}, bf16[128,512]{1,0:T(8,128)(2,1)S(1)}, u32[]{:S(2)}, u32[]{:S(2)}) %collective-permute-start.12) | collective-permute-done | bytes 131104 | tf_op jit(solution)/shard_map/ppermute | solution.py:165
  350.7 37.7 %shard_map.55 = bf16[2048,512]{1,0:T(8,128)(2,1)} custom-call(s32[16,8]{1,0:T(8,128)} %concatenate.9.slot_ref, s32[16,8]{1,0:T(8,128)} %concatenate.10.which_ref, s32[16]{0:T(128)} %dynamic-slice_bitcast_fusion.16.count_ref, s32[16]{0:T(128)} %and_select_fusion.qrow_ref, bf16[16,128,512]{2,1,0:T(8,128)(2,1)} %bitcast_dynamic-update-slice_fusion.query_ref, ...), custom_call_target="tpu_custom_call" | custom-call | tf_op jit(solution)/shard_map/pallas_call | solution.py:77
  388.4 52.0 %all_to_all.20 = bf16[16,128,512]{2,1,0:T(8,128)(2,1)S(1)} all-to-all(bf16[16,128,512]{2,1,0:T(8,128)(2,1)} %bitcast.83), channel_id=1, replica_groups=mesh['seq'=32,'head'=16] {'head'}, dimensions={0} | all-to-all | bytes 4194304 | tf_op jit(solution)/shard_map/all_to_all | solution.py:182
  442.4 4.1 copy.45
  (73 shorter events, 40.3 us)
Async XLA Ops:
  2.4 41.8 %all-to-all-start = ((bf16[16,128,256]{2,1,0:T(8,128)(2,1)}), bf16[16,128,256]{2,1,0:T(8,128)(2,1)S(1)}, u32[]{:S(2)}, u32[]{:S(2)}) async-start(bf16[16,128,256]{2,1,0:T(8,128)(2,1)} %bitcast.36), calls=%async_computation | async-start | bytes 2097152 | tf_op jit(solution)/shard_map/all_to_all | solution.py:143
  44.2 10.4 %copy-start = (bf16[16,128,256]{2,1,0:T(8,128)(2,1)}, bf16[16,128,256]{2,1,0:T(8,128)(2,1)S(1)}, u32[]{:S(2)}) copy-start(bf16[16,128,256]{2,1,0:T(8,128)(2,1)S(1)} %all-to-all-done.own_ref) | copy-start | bytes 3145732
  46.2 56.0 %all-to-all-start.1 = ((bf16[32,128,256]{2,1,0:T(8,128)(2,1)}), bf16[32,128,256]{2,1,0:T(8,128)(2,1)S(1)}, u32[]{:S(2)}, u32[]{:S(2)}) async-start(bf16[32,128,256]{2,1,0:T(8,128)(2,1)} %gather_fusion), calls=%async_computation.1 | async-start | bytes 4194304 | tf_op jit(solution)/shard_map/all_to_all | solution.py:155
  102.2 7.4 %copy-start.1 = (bf16[32,128,256]{2,1,0:T(8,128)(2,1)}, bf16[32,128,256]{2,1,0:T(8,128)(2,1)S(1)}, u32[]{:S(2)}) copy-start(bf16[32,128,256]{2,1,0:T(8,128)(2,1)S(1)} %all-to-all-done.1.mine0_ref) | copy-start | bytes 6291460
  102.2 99.4 %all-to-all-start.2 = ((bf16[32,128,256]{2,1,0:T(8,128)(2,1)}), bf16[32,128,256]{2,1,0:T(8,128)(2,1)}, u32[]{:S(2)}, u32[]{:S(2)}) async-start(bf16[32,128,256]{2,1,0:T(8,128)(2,1)} %gather_fusion.1), calls=%async_computation.2 | async-start | bytes 4194304 | tf_op jit(solution)/shard_map/all_to_all | solution.py:155
  117.6 232.4 %collective-permute-start.14 = (bf16[128,512]{1,0:T(8,128)(2,1)S(1)}, bf16[128,512]{1,0:T(8,128)(2,1)S(1)}, u32[]{:S(2)}, u32[]{:S(2)}) collective-permute-start(bf16[128,512]{1,0:T(8,128)(2,1)S(1)} %get-tuple-element.9), channel_id=1, source_target_pairs={{0,15},{1,0},{2,1},{3,2},{4,3},{5,4},{6,5},{7,6},{8,7},{9,8},{10,9... | collective-permute-start | bytes 393224 | tf_op jit(solution)/shard_map/ppermute | solution.py:165
  121.8 227.5 %collective-permute-start.13 = (bf16[128,512]{1,0:T(8,128)(2,1)S(1)}, bf16[128,512]{1,0:T(8,128)(2,1)S(1)}, u32[]{:S(2)}, u32[]{:S(2)}) collective-permute-start(bf16[128,512]{1,0:T(8,128)(2,1)S(1)} %get-tuple-element.10), channel_id=1, source_target_pairs={{0,14},{1,15},{2,0},{3,1},{4,2},{5,3},{6,4},{7,5},{8,6},{9,7},{10,... | collective-permute-start | bytes 393224 | tf_op jit(solution)/shard_map/ppermute | solution.py:165
  126.3 79.9 %collective-permute-start.6 = (bf16[128,512]{1,0:T(8,128)(2,1)S(1)}, bf16[128,512]{1,0:T(8,128)(2,1)S(1)}, u32[]{:S(2)}, u32[]{:S(2)}) collective-permute-start(bf16[128,512]{1,0:T(8,128)(2,1)S(1)} %get-tuple-element.17), channel_id=1, source_target_pairs={{0,7},{1,8},{2,9},{3,10},{4,11},{5,12},{6,13},{7,14},{8,15},{9,0},... | collective-permute-start | bytes 393224 | tf_op jit(solution)/shard_map/ppermute | solution.py:165
  128.6 73.0 %collective-permute-start.5 = (bf16[128,512]{1,0:T(8,128)(2,1)S(1)}, bf16[128,512]{1,0:T(8,128)(2,1)S(1)}, u32[]{:S(2)}, u32[]{:S(2)}) collective-permute-start(bf16[128,512]{1,0:T(8,128)(2,1)S(1)} %get-tuple-element.18), channel_id=1, source_target_pairs={{0,6},{1,7},{2,8},{3,9},{4,10},{5,11},{6,12},{7,13},{8,14},{9,15},... | collective-permute-start | bytes 393224 | tf_op jit(solution)/shard_map/ppermute | solution.py:165
  134.4 12.7 %collective-permute-start = (bf16[128,512]{1,0:T(8,128)(2,1)}, bf16[128,512]{1,0:T(8,128)(2,1)S(1)}, u32[]{:S(2)}, u32[]{:S(2)}) collective-permute-start(bf16[128,512]{1,0:T(8,128)(2,1)} %get-tuple-element.23), channel_id=1, source_target_pairs={{0,1},{1,2},{2,3},{3,4},{4,5},{5,6},{6,7},{7,8},{8,9},{9,10},{10,1... | collective-permute-start | bytes 393224 | tf_op jit(solution)/shard_map/ppermute | solution.py:165
  147.0 20.8 %collective-permute-start.1 = (bf16[128,512]{1,0:T(8,128)(2,1)}, bf16[128,512]{1,0:T(8,128)(2,1)S(1)}, u32[]{:S(2)}, u32[]{:S(2)}) collective-permute-start(bf16[128,512]{1,0:T(8,128)(2,1)} %get-tuple-element.22), channel_id=1, source_target_pairs={{0,2},{1,3},{2,4},{3,5},{4,6},{5,7},{6,8},{7,9},{8,10},{9,11},{10,... | collective-permute-start | bytes 393224 | tf_op jit(solution)/shard_map/ppermute | solution.py:165
  167.9 10.6 %collective-permute-start.2 = (bf16[128,512]{1,0:T(8,128)(2,1)}, bf16[128,512]{1,0:T(8,128)(2,1)S(1)}, u32[]{:S(2)}, u32[]{:S(2)}) collective-permute-start(bf16[128,512]{1,0:T(8,128)(2,1)} %get-tuple-element.21), channel_id=1, source_target_pairs={{0,3},{1,4},{2,5},{3,6},{4,7},{5,8},{6,9},{7,10},{8,11},{9,12},{10... | collective-permute-start | bytes 393224 | tf_op jit(solution)/shard_map/ppermute | solution.py:165
  178.5 8.3 %collective-permute-start.3 = (bf16[128,512]{1,0:T(8,128)(2,1)}, bf16[128,512]{1,0:T(8,128)(2,1)S(1)}, u32[]{:S(2)}, u32[]{:S(2)}) collective-permute-start(bf16[128,512]{1,0:T(8,128)(2,1)} %get-tuple-element.20), channel_id=1, source_target_pairs={{0,4},{1,5},{2,6},{3,7},{4,8},{5,9},{6,10},{7,11},{8,12},{9,13},{1... | collective-permute-start | bytes 393224 | tf_op jit(solution)/shard_map/ppermute | solution.py:165
  186.7 12.2 %collective-permute-start.4 = (bf16[128,512]{1,0:T(8,128)(2,1)}, bf16[128,512]{1,0:T(8,128)(2,1)S(1)}, u32[]{:S(2)}, u32[]{:S(2)}) collective-permute-start(bf16[128,512]{1,0:T(8,128)(2,1)} %get-tuple-element.19), channel_id=1, source_target_pairs={{0,5},{1,6},{2,7},{3,8},{4,9},{5,10},{6,11},{7,12},{8,13},{9,14},{... | collective-permute-start | bytes 393224 | tf_op jit(solution)/shard_map/ppermute | solution.py:165
  199.6 151.0 %collective-permute-start.15 = (bf16[32,128,256]{2,1,0:T(8,128)(2,1)}, bf16[32,128,256]{2,1,0:T(8,128)(2,1)}, u32[]{:S(2)}, u32[]{:S(2)}) collective-permute-start(bf16[32,128,256]{2,1,0:T(8,128)(2,1)} %copy-done.1), channel_id=1, source_target_pairs={{0,4},{1,5},{2,6},{3,7},{4,0},{5,1},{6,2},{7,3},{8,12},{9,13},{10,... | collective-permute-start | bytes 6291464 | tf_op jit(solution)/shard_map/ppermute | solution.py:157
  201.6 149.1 %collective-permute-start.16 = (bf16[32,128,256]{2,1,0:T(8,128)(2,1)}, bf16[32,128,256]{2,1,0:T(8,128)(2,1)}, u32[]{:S(2)}, u32[]{:S(2)}) collective-permute-start(bf16[32,128,256]{2,1,0:T(8,128)(2,1)} %all-to-all-done.2.mine1_ref), channel_id=1, source_target_pairs={{0,4},{1,5},{2,6},{3,7},{4,0},{5,1},{6,2},{7,3},{8,12},{9,13},{10,... | collective-permute-start | bytes 6291464 | tf_op jit(solution)/shard_map/ppermute | solution.py:157
  206.2 86.5 %collective-permute-start.7 = (bf16[128,512]{1,0:T(8,128)(2,1)S(1)}, bf16[128,512]{1,0:T(8,128)(2,1)S(1)}, u32[]{:S(2)}, u32[]{:S(2)}) collective-permute-start(bf16[128,512]{1,0:T(8,128)(2,1)S(1)} %get-tuple-element.16), channel_id=1, source_target_pairs={{0,8},{1,9},{2,10},{3,11},{4,12},{5,13},{6,14},{7,15},{8,0},{9,1},... | collective-permute-start | bytes 393224 | tf_op jit(solution)/shard_map/ppermute | solution.py:165
  292.7 11.0 %collective-permute-start.8 = (bf16[128,512]{1,0:T(8,128)(2,1)S(1)}, bf16[128,512]{1,0:T(8,128)(2,1)S(1)}, u32[]{:S(2)}, u32[]{:S(2)}) collective-permute-start(bf16[128,512]{1,0:T(8,128)(2,1)S(1)} %get-tuple-element.15), channel_id=1, source_target_pairs={{0,9},{1,10},{2,11},{3,12},{4,13},{5,14},{6,15},{7,0},{8,1},{9,2},... | collective-permute-start | bytes 393224 | tf_op jit(solution)/shard_map/ppermute | solution.py:165
  303.7 14.4 %collective-permute-start.9 = (bf16[128,512]{1,0:T(8,128)(2,1)S(1)}, bf16[128,512]{1,0:T(8,128)(2,1)S(1)}, u32[]{:S(2)}, u32[]{:S(2)}) collective-permute-start(bf16[128,512]{1,0:T(8,128)(2,1)S(1)} %get-tuple-element.14), channel_id=1, source_target_pairs={{0,10},{1,11},{2,12},{3,13},{4,14},{5,15},{6,0},{7,1},{8,2},{9,3},... | collective-permute-start | bytes 393224 | tf_op jit(solution)/shard_map/ppermute | solution.py:165
  318.0 8.8 %collective-permute-start.10 = (bf16[128,512]{1,0:T(8,128)(2,1)S(1)}, bf16[128,512]{1,0:T(8,128)(2,1)S(1)}, u32[]{:S(2)}, u32[]{:S(2)}) collective-permute-start(bf16[128,512]{1,0:T(8,128)(2,1)S(1)} %get-tuple-element.13), channel_id=1, source_target_pairs={{0,11},{1,12},{2,13},{3,14},{4,15},{5,0},{6,1},{7,2},{8,3},{9,4},{... | collective-permute-start | bytes 393224 | tf_op jit(solution)/shard_map/ppermute | solution.py:165
  326.8 9.0 %collective-permute-start.11 = (bf16[128,512]{1,0:T(8,128)(2,1)S(1)}, bf16[128,512]{1,0:T(8,128)(2,1)S(1)}, u32[]{:S(2)}, u32[]{:S(2)}) collective-permute-start(bf16[128,512]{1,0:T(8,128)(2,1)S(1)} %get-tuple-element.12), channel_id=1, source_target_pairs={{0,12},{1,13},{2,14},{3,15},{4,0},{5,1},{6,2},{7,3},{8,4},{9,5},{1... | collective-permute-start | bytes 393224 | tf_op jit(solution)/shard_map/ppermute | solution.py:165
  335.7 12.9 %collective-permute-start.12 = (bf16[128,512]{1,0:T(8,128)(2,1)S(1)}, bf16[128,512]{1,0:T(8,128)(2,1)S(1)}, u32[]{:S(2)}, u32[]{:S(2)}) collective-permute-start(bf16[128,512]{1,0:T(8,128)(2,1)S(1)} %get-tuple-element.11), channel_id=1, source_target_pairs={{0,13},{1,14},{2,15},{3,0},{4,1},{5,2},{6,3},{7,4},{8,5},{9,6},{10... | collective-permute-start | bytes 393224 | tf_op jit(solution)/shard_map/ppermute | solution.py:165

commit v9 on v6

--- a/solution.py
+++ b/solution.py
@@ -16,46 +16,34 @@
 def attend_kernel(slot_ref, which_ref, count_ref, query_ref, own_ref, mine0_ref, mine1_ref,
                   peer0_ref, peer1_ref, out_ref, block_buf, *, score_scale, slot_total, heads):
     row = pl.program_id(0)
-    head_dim = block_buf.shape[2] // 2
+    head_dim = block_buf.shape[1] // 2
     query = query_ref[...]
     query = jnp.concatenate(
         [query[:, h * head_dim:(h + 1) * head_dim] for h in range(heads)], axis=0
     )
     row_count = count_ref[row]
     sources = (mine0_ref, mine1_ref, peer0_ref, peer1_ref)
+    block_buf[0:BLK] = own_ref[row]
     for slot in range(1, slot_total):
         index = slot_ref[row, slot]
         which = which_ref[row, slot]
         for code, source in enumerate(sources):
             @pl.when(which == code)
             def _(source=source, slot=slot, index=index):
-                block_buf[slot - 1] = source[index]
-    scores = []
-    values = []
-    for slot in range(slot_total):
-        block = own_ref[row] if slot == 0 else block_buf[slot - 1]
-        key = block[:, :head_dim]
-        value = block[:, head_dim:]
-        part = lax.dot_general(
-            query, key, (((1,), (1,)), ((), ())), preferred_element_type=jnp.float32
-        ) * score_scale
-        if slot > 0:
-            part = jnp.where(slot < row_count, part, NEG_FILL)
-        scores.append(part)
-        values.append(value)
-    row_max = jnp.max(scores[0], axis=1, keepdims=True)
-    for part in scores[1:]:
-        row_max = jnp.maximum(row_max, jnp.max(part, axis=1, keepdims=True))
-    weights = [jnp.exp(part - row_max) for part in scores]
-    total = jnp.sum(weights[0], axis=1, keepdims=True)
-    for part in weights[1:]:
-        total = total + jnp.sum(part, axis=1, keepdims=True)
-    inverse = 1.0 / total
-    acc = None
-    for part, value in zip(weights, values):
-        probs = (part * inverse).astype(jnp.bfloat16)
-        term = jnp.dot(probs, value, preferred_element_type=jnp.float32)
-        acc = term if acc is None else acc + term
+                block_buf[slot * BLK:(slot + 1) * BLK] = source[index]
+    blocks = block_buf[...]
+    keys = blocks[:, :head_dim]
+    values = blocks[:, head_dim:]
+    scores = lax.dot_general(
+        query, keys, (((1,), (1,)), ((), ())), preferred_element_type=jnp.float32
+    ) * score_scale
+    key_slot = lax.broadcasted_iota(jnp.int32, (1, slot_total * BLK), 1) // BLK
+    scores = jnp.where(key_slot < row_count, scores, NEG_FILL)
+    row_max = jnp.max(scores, axis=1, keepdims=True)
+    weights = jnp.exp(scores - row_max)
+    inverse = 1.0 / jnp.sum(weights, axis=1, keepdims=True)
+    probs = (weights * inverse).astype(jnp.bfloat16)
+    acc = jnp.dot(probs, values, preferred_element_type=jnp.float32)
     tokens = query_ref.shape[0]
     for h in range(heads):
         out_ref[:, h * head_dim:(h + 1) * head_dim] = acc[h * tokens:(h + 1) * tokens].astype(
@@ -85,7 +73,7 @@
             ]
             + [whole(part.shape) for part in received],
             out_specs=pl.BlockSpec((BLK, width), lambda r, s, w, c: (r, 0)),
-            scratch_shapes=[pltpu.VMEM((slot_total - 1, BLK, pair_dim), own_blocks.dtype)],
+            scratch_shapes=[pltpu.VMEM((slot_total * BLK, pair_dim), own_blocks.dtype)],
         ),
         compiler_params=pltpu.CompilerParams(vmem_limit_bytes=100 * 1024 * 1024),
     )(slot_index, slot_which, row_counts, local_queries, own_blocks, *received)

time: 342 us -> 338 us (0.988)
  Pallas kernels: 39.6 us -> 35.3 us
    pallas_call x1, Pallas kernels: 39.6 us -> 35.3 us  [attend_all(): pl.pallas_call(kernel, out_shape=jax.ShapeDtypeStruct((seq_rows, width),...]
where the time goes in v9:
time: 338 us; the launch traced here: 337 us
  waiting for transfers between devices  171 us (51%)
  blocking collectives  61 us (18%)
  starting transfers between devices  42.6 us (13%)
  Pallas kernels  35.3 us (10%)
  local copies, waits for them, and re-layouts  21.7 us (6%)
  other arithmetic  5.5 us (2%)
    ppermute x2, waiting for transfers between devices, on_device(): peer.append(lax.ppermute(got, 'head', partner))  106 us
    all_to_all x1, blocking collectives, on_device(): lax.all_to_all(attended.reshape(head_count, tokens, width), 'head', split...  61 us
    all_to_all x2, waiting for transfers between devices, on_device(): got = lax.all_to_all(picked, 'seq', split_axis=0, concat_axis=0, tiled=True)  47.4 us
    pallas_call x1, Pallas kernels, attend_all(): pl.pallas_call(kernel, out_shape=jax.ShapeDtypeStruct((seq_rows, width),...  35.3 us
    all_to_all x2, starting transfers between devices, on_device(): got = lax.all_to_all(picked, 'seq', split_axis=0, concat_axis=0, tiled=True)  19.7 us
    all_to_all x1, waiting for transfers between devices, on_device(): lax.all_to_all(kv, 'head', split_axis=0, concat_axis=0, tiled=True)  17.6 us
    all_to_all x1, starting transfers between devices, on_device(): lax.all_to_all(kv, 'head', split_axis=0, concat_axis=0, tiled=True)  12.9 us
  transfers between devices with their start and end apart: 6, of which 4 were waited for; matrix products, arithmetic and copies ran while one was open for 5% of the time, Pallas kernels for 0%

profile of v9, /device:TPU:16, one launch (start us, length us, event | category | flops | bytes accessed | tf_op | source)
XLA Modules:
  0.0 337.0 jit_solution(14914149562529589996)
XLA Ops:
  0.0 1.1 pad_maximum_fusion
  1.1 0.1 reshape.153
  1.3 1.1 broadcast_in_dim.12
  2.4 12.9 %all-to-all-start = ((bf16[16,128,256]{2,1,0:T(8,128)(2,1)}), bf16[16,128,256]{2,1,0:T(8,128)(2,1)S(1)}, u32[]{:S(2)}, u32[]{:S(2)}) async-start(bf16[16,128,256]{2,1,0:T(8,128)(2,1)} %bitcast.6), calls=%async_computation | async-start | bytes 2097152 | tf_op jit(solution)/shard_map/all_to_all | solution.py:130
  15.3 0.7 dynamic-slice_bitcast_fusion
  16.1 0.1 copy.35
  16.2 0.2 reshape.150
  16.5 0.7 dynamic-slice_reduce_fusion.2
  17.7 3.9 %fusion.3 = s32[32,112]{0,1:T(8,128)S(1)} fusion(s32[32,112]{0,1:T(8,128)S(1)} %get-tuple-element.12, pred[32,112]{0,1:T(8,128)(4,1)S(1)} %get-tuple-element.10), kind=kOutput, calls=%fused_computation.6 | output fusion | flops 13758976 | bytes 32256 | tf_op jit(solution)/shard_map/jit(cumsum)/reduce_window_sum | solution.py:96
  21.7 0.2 multiply_reduce_fusion
  21.9 17.6 %all-to-all-done.own_ref = bf16[16,128,256]{2,1,0:T(8,128)(2,1)S(1)} async-done(((bf16[16,128,256]{2,1,0:T(8,128)(2,1)}), bf16[16,128,256]{2,1,0:T(8,128)(2,1)S(1)}, u32[]{:S(2)}, u32[]{:S(2)}) %all-to-all-start) | async-done | bytes 1048608 | tf_op jit(solution)/shard_map/all_to_all | solution.py:130
  39.5 2.0 gather_fusion.1
  41.5 14.2 %all-to-all-start.1 = ((bf16[32,128,256]{2,1,0:T(8,128)(2,1)}), bf16[32,128,256]{2,1,0:T(8,128)(2,1)}, u32[]{:S(2)}, u32[]{:S(2)}) async-start(bf16[32,128,256]{2,1,0:T(8,128)(2,1)} %gather_fusion.1), calls=%async_computation.1 | async-start | bytes 4194304 | tf_op jit(solution)/shard_map/all_to_all | solution.py:142
  55.7 2.0 gather_fusion
  57.7 47.4 %all-to-all-done.1.mine0_ref = bf16[32,128,256]{2,1,0:T(8,128)(2,1)} async-done(((bf16[32,128,256]{2,1,0:T(8,128)(2,1)}), bf16[32,128,256]{2,1,0:T(8,128)(2,1)}, u32[]{:S(2)}, u32[]{:S(2)}) %all-to-all-start.1) | async-done | bytes 2097184 | tf_op jit(solution)/shard_map/all_to_all | solution.py:142
  105.2 5.5 %all-to-all-start.2 = ((bf16[32,128,256]{2,1,0:T(8,128)(2,1)}), bf16[32,128,256]{2,1,0:T(8,128)(2,1)}, u32[]{:S(2)}, u32[]{:S(2)}) async-start(bf16[32,128,256]{2,1,0:T(8,128)(2,1)} %gather_fusion), calls=%async_computation.2 | async-start | bytes 4194304 | tf_op jit(solution)/shard_map/all_to_all | solution.py:142
  110.7 1.9 collective-permute-start
  112.7 2.6 copy.40
  115.2 2.2 reshape.152
  117.4 43.2 %collective-permute-done.peer0_ref = bf16[32,128,256]{2,1,0:T(8,128)(2,1)} collective-permute-done((bf16[32,128,256]{2,1,0:T(8,128)(2,1)}, bf16[32,128,256]{2,1,0:T(8,128)(2,1)}, u32[]{:S(2)}, u32[]{:S(2)}) %collective-permute-start) | collective-permute-done | bytes 2097184 | tf_op jit(solution)/shard_map/ppermute | solution.py:144
  160.6 4.4 %all-to-all-start.3 = ((bf16[16,128,512]{2,1,0:T(8,128)(2,1)}), bf16[16,128,512]{2,1,0:T(8,128)(2,1)}, u32[]{:S(2)}, u32[]{:S(2)}) async-start(bf16[16,128,512]{2,1,0:T(8,128)(2,1)} %reshape.152), calls=%async_computation.3 | async-start | bytes 4194304 | tf_op jit(solution)/shard_map/all_to_all | solution.py:149
  165.1 3.7 %collective-permute-start.1 = (bf16[32,128,256]{2,1,0:T(8,128)(2,1)}, bf16[32,128,256]{2,1,0:T(8,128)(2,1)}, u32[]{:S(2)}, u32[]{:S(2)}) collective-permute-start(bf16[32,128,256]{2,1,0:T(8,128)(2,1)} %all-to-all-done.2.mine1_ref), channel_id=1, source_target_pairs={{0,4},{1,5},{2,6},{3,7},{4,0},{5,1},{6,2},{7,3},{8,12},{9,13},{10,... | collective-permute-start | bytes 6291464 | tf_op jit(solution)/shard_map/ppermute | solution.py:144
  168.7 0.2 minimum_reduce_fusion
  169.1 0.2 dynamic-slice_reduce_fusion.1
  169.4 0.7 concatenate.10.which_ref
  170.1 0.7 concatenate.9.slot_ref
  170.8 1.3 dynamic-slice_bitcast_fusion.1.count_ref
  172.1 62.4 %collective-permute-done.1.peer1_ref = bf16[32,128,256]{2,1,0:T(8,128)(2,1)} collective-permute-done((bf16[32,128,256]{2,1,0:T(8,128)(2,1)}, bf16[32,128,256]{2,1,0:T(8,128)(2,1)}, u32[]{:S(2)}, u32[]{:S(2)}) %collective-permute-start.1) | collective-permute-done | bytes 2097184 | tf_op jit(solution)/shard_map/ppermute | solution.py:144
  234.5 35.3 %shard_map.55 = bf16[2048,512]{1,0:T(8,128)(2,1)} custom-call(s32[16,8]{1,0:T(8,128)} %concatenate.9.slot_ref, s32[16,8]{1,0:T(8,128)} %concatenate.10.which_ref, s32[16]{0:T(128)} %dynamic-slice_bitcast_fusion.1.count_ref, bf16[2048,512]{1,0:T(8,128)(2,1)} %bitcast.9.query_ref, bf16[16,128,256]{2,1,0:T(8,128)(2,1)} %copy-done, ...), custom_call_target="tpu_custom_call" | custom-call | tf_op jit(solution)/shard_map/pallas_call | solution.py:64
  269.8 61.0 %all_to_all.25 = bf16[16,128,512]{2,1,0:T(8,128)(2,1)S(1)} all-to-all(bf16[16,128,512]{2,1,0:T(8,128)(2,1)} %bitcast.22), channel_id=1, replica_groups=mesh['seq'=32,'head'=16] {'head'}, dimensions={0} | all-to-all | bytes 4194304 | tf_op jit(solution)/shard_map/all_to_all | solution.py:163
  330.9 2.1 reshape.157
  332.9 4.1 %copy.45 = bf16[2,2,4,128,4,128]{5,4,1,2,0,3:T(4,128)(2,1)} copy(bf16[2,2,4,128,4,128]{5,4,3,2,1,0:T(4,128)(2,1)} %reshape.157) | data formatting | bytes 4194304 | tf_op jit(solution)/shard_map/reshape | solution.py:167
  (26 shorter events, 1.1 us)
Async XLA Ops:
  2.4 37.1 %all-to-all-start = ((bf16[16,128,256]{2,1,0:T(8,128)(2,1)}), bf16[16,128,256]{2,1,0:T(8,128)(2,1)S(1)}, u32[]{:S(2)}, u32[]{:S(2)}) async-start(bf16[16,128,256]{2,1,0:T(8,128)(2,1)} %bitcast.6), calls=%async_computation | async-start | bytes 2097152 | tf_op jit(solution)/shard_map/all_to_all | solution.py:130
  39.5 16.2 %copy-start = (bf16[16,128,256]{2,1,0:T(8,128)(2,1)}, bf16[16,128,256]{2,1,0:T(8,128)(2,1)S(1)}, u32[]{:S(2)}) copy-start(bf16[16,128,256]{2,1,0:T(8,128)(2,1)S(1)} %all-to-all-done.own_ref) | copy-start | bytes 3145732
  41.5 63.7 %all-to-all-start.1 = ((bf16[32,128,256]{2,1,0:T(8,128)(2,1)}), bf16[32,128,256]{2,1,0:T(8,128)(2,1)}, u32[]{:S(2)}, u32[]{:S(2)}) async-start(bf16[32,128,256]{2,1,0:T(8,128)(2,1)} %gather_fusion.1), calls=%async_computation.1 | async-start | bytes 4194304 | tf_op jit(solution)/shard_map/all_to_all | solution.py:142
  105.2 55.5 %all-to-all-start.2 = ((bf16[32,128,256]{2,1,0:T(8,128)(2,1)}), bf16[32,128,256]{2,1,0:T(8,128)(2,1)}, u32[]{:S(2)}, u32[]{:S(2)}) async-start(bf16[32,128,256]{2,1,0:T(8,128)(2,1)} %gather_fusion), calls=%async_computation.2 | async-start | bytes 4194304 | tf_op jit(solution)/shard_map/all_to_all | solution.py:142
  110.7 49.9 %collective-permute-start = (bf16[32,128,256]{2,1,0:T(8,128)(2,1)}, bf16[32,128,256]{2,1,0:T(8,128)(2,1)}, u32[]{:S(2)}, u32[]{:S(2)}) collective-permute-start(bf16[32,128,256]{2,1,0:T(8,128)(2,1)} %all-to-all-done.1.mine0_ref), channel_id=1, source_target_pairs={{0,4},{1,5},{2,6},{3,7},{4,0},{5,1},{6,2},{7,3},{8,12},{9,13},{10,... | collective-permute-start | bytes 6291464 | tf_op jit(solution)/shard_map/ppermute | solution.py:144
  160.6 73.9 %all-to-all-start.3 = ((bf16[16,128,512]{2,1,0:T(8,128)(2,1)}), bf16[16,128,512]{2,1,0:T(8,128)(2,1)}, u32[]{:S(2)}, u32[]{:S(2)}) async-start(bf16[16,128,512]{2,1,0:T(8,128)(2,1)} %reshape.152), calls=%async_computation.3 | async-start | bytes 4194304 | tf_op jit(solution)/shard_map/all_to_all | solution.py:149
  165.1 69.4 %collective-permute-start.1 = (bf16[32,128,256]{2,1,0:T(8,128)(2,1)}, bf16[32,128,256]{2,1,0:T(8,128)(2,1)}, u32[]{:S(2)}, u32[]{:S(2)}) collective-permute-start(bf16[32,128,256]{2,1,0:T(8,128)(2,1)} %all-to-all-done.2.mine1_ref), channel_id=1, source_target_pairs={{0,4},{1,5},{2,6},{3,7},{4,0},{5,1},{6,2},{7,3},{8,12},{9,13},{10,... | collective-permute-start | bytes 6291464 | tf_op jit(solution)/shard_map/ppermute | solution.py:144

commit v10 on v9

--- a/solution.py
+++ b/solution.py
@@ -11,6 +11,7 @@
 
 
 NEG_FILL = -1e30
+LOG2_E = 1.4426950408889634
 
 
 def attend_kernel(slot_ref, which_ref, count_ref, query_ref, own_ref, mine0_ref, mine1_ref,
@@ -36,14 +37,14 @@
     values = blocks[:, head_dim:]
     scores = lax.dot_general(
         query, keys, (((1,), (1,)), ((), ())), preferred_element_type=jnp.float32
-    ) * score_scale
+    )
     key_slot = lax.broadcasted_iota(jnp.int32, (1, slot_total * BLK), 1) // BLK
     scores = jnp.where(key_slot < row_count, scores, NEG_FILL)
     row_max = jnp.max(scores, axis=1, keepdims=True)
-    weights = jnp.exp(scores - row_max)
+    weights = jnp.exp2((scores - row_max) * (score_scale * LOG2_E))
     inverse = 1.0 / jnp.sum(weights, axis=1, keepdims=True)
-    probs = (weights * inverse).astype(jnp.bfloat16)
-    acc = jnp.dot(probs, values, preferred_element_type=jnp.float32)
+    acc = jnp.dot(weights.astype(jnp.bfloat16), values, preferred_element_type=jnp.float32)
+    acc = acc * inverse
     tokens = query_ref.shape[0]
     for h in range(heads):
         out_ref[:, h * head_dim:(h + 1) * head_dim] = acc[h * tokens:(h + 1) * tokens].astype(

time: 338 us -> 336 us (level)
  no operation moved by 1% of the time
where the time goes in v10:
time: 336 us; the launch traced here: 335 us
  waiting for transfers between devices  171 us (51%)
  blocking collectives  61 us (18%)
  starting transfers between devices  42.6 us (13%)
  Pallas kernels  33.2 us (10%)
  local copies, waits for them, and re-layouts  21.7 us (6%)
  other arithmetic  5.5 us (2%)
    ppermute x2, waiting for transfers between devices, on_device(): peer.append(lax.ppermute(got, 'head', partner))  106 us
    all_to_all x1, blocking collectives, on_device(): lax.all_to_all(attended.reshape(head_count, tokens, width), 'head', split...  61 us
    all_to_all x2, waiting for transfers between devices, on_device(): got = lax.all_to_all(picked, 'seq', split_axis=0, concat_axis=0, tiled=True)  47.4 us
    pallas_call x1, Pallas kernels, attend_all(): pl.pallas_call(kernel, out_shape=jax.ShapeDtypeStruct((seq_rows, width),...  33.2 us
    all_to_all x2, starting transfers between devices, on_device(): got = lax.all_to_all(picked, 'seq', split_axis=0, concat_axis=0, tiled=True)  19.7 us
    all_to_all x1, waiting for transfers between devices, on_device(): lax.all_to_all(kv, 'head', split_axis=0, concat_axis=0, tiled=True)  17.6 us
    all_to_all x1, starting transfers between devices, on_device(): lax.all_to_all(kv, 'head', split_axis=0, concat_axis=0, tiled=True)  12.9 us
  transfers between devices with their start and end apart: 6, of which 4 were waited for; matrix products, arithmetic and copies ran while one was open for 5% of the time, Pallas kernels for 0%

profile of v10, /device:TPU:16, one launch (start us, length us, event | category | flops | bytes accessed | tf_op | source)
XLA Modules:
  0.0 334.9 jit_solution(6454295565707871355)
XLA Ops:
  0.0 1.1 pad_maximum_fusion
  1.1 0.1 reshape.153
  1.3 1.1 broadcast_in_dim.12
  2.4 12.9 %all-to-all-start = ((bf16[16,128,256]{2,1,0:T(8,128)(2,1)}), bf16[16,128,256]{2,1,0:T(8,128)(2,1)S(1)}, u32[]{:S(2)}, u32[]{:S(2)}) async-start(bf16[16,128,256]{2,1,0:T(8,128)(2,1)} %bitcast.6), calls=%async_computation | async-start | bytes 2097152 | tf_op jit(solution)/shard_map/all_to_all | solution.py:131
  15.3 0.7 dynamic-slice_bitcast_fusion
  16.1 0.1 copy.35
  16.2 0.2 reshape.150
  16.5 0.7 dynamic-slice_reduce_fusion.2
  17.7 3.9 %fusion.3 = s32[32,112]{0,1:T(8,128)S(1)} fusion(s32[32,112]{0,1:T(8,128)S(1)} %get-tuple-element.12, pred[32,112]{0,1:T(8,128)(4,1)S(1)} %get-tuple-element.10), kind=kOutput, calls=%fused_computation.6 | output fusion | flops 13758976 | bytes 32256 | tf_op jit(solution)/shard_map/jit(cumsum)/reduce_window_sum | solution.py:97
  21.7 0.2 multiply_reduce_fusion
  21.9 17.6 %all-to-all-done.own_ref = bf16[16,128,256]{2,1,0:T(8,128)(2,1)S(1)} async-done(((bf16[16,128,256]{2,1,0:T(8,128)(2,1)}), bf16[16,128,256]{2,1,0:T(8,128)(2,1)S(1)}, u32[]{:S(2)}, u32[]{:S(2)}) %all-to-all-start) | async-done | bytes 1048608 | tf_op jit(solution)/shard_map/all_to_all | solution.py:131
  39.5 2.0 gather_fusion.1
  41.5 14.2 %all-to-all-start.1 = ((bf16[32,128,256]{2,1,0:T(8,128)(2,1)}), bf16[32,128,256]{2,1,0:T(8,128)(2,1)}, u32[]{:S(2)}, u32[]{:S(2)}) async-start(bf16[32,128,256]{2,1,0:T(8,128)(2,1)} %gather_fusion.1), calls=%async_computation.1 | async-start | bytes 4194304 | tf_op jit(solution)/shard_map/all_to_all | solution.py:143
  55.7 2.0 gather_fusion
  57.7 47.4 %all-to-all-done.1.mine0_ref = bf16[32,128,256]{2,1,0:T(8,128)(2,1)} async-done(((bf16[32,128,256]{2,1,0:T(8,128)(2,1)}), bf16[32,128,256]{2,1,0:T(8,128)(2,1)}, u32[]{:S(2)}, u32[]{:S(2)}) %all-to-all-start.1) | async-done | bytes 2097184 | tf_op jit(solution)/shard_map/all_to_all | solution.py:143
  105.2 5.5 %all-to-all-start.2 = ((bf16[32,128,256]{2,1,0:T(8,128)(2,1)}), bf16[32,128,256]{2,1,0:T(8,128)(2,1)}, u32[]{:S(2)}, u32[]{:S(2)}) async-start(bf16[32,128,256]{2,1,0:T(8,128)(2,1)} %gather_fusion), calls=%async_computation.2 | async-start | bytes 4194304 | tf_op jit(solution)/shard_map/all_to_all | solution.py:143
  110.7 1.9 collective-permute-start
  112.7 2.6 copy.40
  115.2 2.2 reshape.152
  117.4 43.2 %collective-permute-done.peer0_ref = bf16[32,128,256]{2,1,0:T(8,128)(2,1)} collective-permute-done((bf16[32,128,256]{2,1,0:T(8,128)(2,1)}, bf16[32,128,256]{2,1,0:T(8,128)(2,1)}, u32[]{:S(2)}, u32[]{:S(2)}) %collective-permute-start) | collective-permute-done | bytes 2097184 | tf_op jit(solution)/shard_map/ppermute | solution.py:145
  160.6 4.4 %all-to-all-start.3 = ((bf16[16,128,512]{2,1,0:T(8,128)(2,1)}), bf16[16,128,512]{2,1,0:T(8,128)(2,1)}, u32[]{:S(2)}, u32[]{:S(2)}) async-start(bf16[16,128,512]{2,1,0:T(8,128)(2,1)} %reshape.152), calls=%async_computation.3 | async-start | bytes 4194304 | tf_op jit(solution)/shard_map/all_to_all | solution.py:150
  165.1 3.7 %collective-permute-start.1 = (bf16[32,128,256]{2,1,0:T(8,128)(2,1)}, bf16[32,128,256]{2,1,0:T(8,128)(2,1)}, u32[]{:S(2)}, u32[]{:S(2)}) collective-permute-start(bf16[32,128,256]{2,1,0:T(8,128)(2,1)} %all-to-all-done.2.mine1_ref), channel_id=1, source_target_pairs={{0,4},{1,5},{2,6},{3,7},{4,0},{5,1},{6,2},{7,3},{8,12},{9,13},{10,... | collective-permute-start | bytes 6291464 | tf_op jit(solution)/shard_map/ppermute | solution.py:145
  168.7 0.2 minimum_reduce_fusion
  169.1 0.2 dynamic-slice_reduce_fusion.1
  169.4 0.7 concatenate.10.which_ref
  170.1 0.7 concatenate.9.slot_ref
  170.8 1.3 dynamic-slice_bitcast_fusion.1.count_ref
  172.1 62.4 %collective-permute-done.1.peer1_ref = bf16[32,128,256]{2,1,0:T(8,128)(2,1)} collective-permute-done((bf16[32,128,256]{2,1,0:T(8,128)(2,1)}, bf16[32,128,256]{2,1,0:T(8,128)(2,1)}, u32[]{:S(2)}, u32[]{:S(2)}) %collective-permute-start.1) | collective-permute-done | bytes 2097184 | tf_op jit(solution)/shard_map/ppermute | solution.py:145
  234.5 33.2 %shard_map.55 = bf16[2048,512]{1,0:T(8,128)(2,1)} custom-call(s32[16,8]{1,0:T(8,128)} %concatenate.9.slot_ref, s32[16,8]{1,0:T(8,128)} %concatenate.10.which_ref, s32[16]{0:T(128)} %dynamic-slice_bitcast_fusion.1.count_ref, bf16[2048,512]{1,0:T(8,128)(2,1)} %bitcast.9.query_ref, bf16[16,128,256]{2,1,0:T(8,128)(2,1)} %copy-done, ...), custom_call_target="tpu_custom_call" | custom-call | tf_op jit(solution)/shard_map/pallas_call | solution.py:65
  267.7 61.0 %all_to_all.25 = bf16[16,128,512]{2,1,0:T(8,128)(2,1)S(1)} all-to-all(bf16[16,128,512]{2,1,0:T(8,128)(2,1)} %bitcast.22), channel_id=1, replica_groups=mesh['seq'=32,'head'=16] {'head'}, dimensions={0} | all-to-all | bytes 4194304 | tf_op jit(solution)/shard_map/all_to_all | solution.py:164
  328.7 2.1 reshape.157
  330.8 4.1 %copy.45 = bf16[2,2,4,128,4,128]{5,4,1,2,0,3:T(4,128)(2,1)} copy(bf16[2,2,4,128,4,128]{5,4,3,2,1,0:T(4,128)(2,1)} %reshape.157) | data formatting | bytes 4194304 | tf_op jit(solution)/shard_map/reshape | solution.py:168
  (26 shorter events, 1.1 us)
Async XLA Ops:
  2.4 37.1 %all-to-all-start = ((bf16[16,128,256]{2,1,0:T(8,128)(2,1)}), bf16[16,128,256]{2,1,0:T(8,128)(2,1)S(1)}, u32[]{:S(2)}, u32[]{:S(2)}) async-start(bf16[16,128,256]{2,1,0:T(8,128)(2,1)} %bitcast.6), calls=%async_computation | async-start | bytes 2097152 | tf_op jit(solution)/shard_map/all_to_all | solution.py:131
  39.5 16.2 %copy-start = (bf16[16,128,256]{2,1,0:T(8,128)(2,1)}, bf16[16,128,256]{2,1,0:T(8,128)(2,1)S(1)}, u32[]{:S(2)}) copy-start(bf16[16,128,256]{2,1,0:T(8,128)(2,1)S(1)} %all-to-all-done.own_ref) | copy-start | bytes 3145732
  41.5 63.7 %all-to-all-start.1 = ((bf16[32,128,256]{2,1,0:T(8,128)(2,1)}), bf16[32,128,256]{2,1,0:T(8,128)(2,1)}, u32[]{:S(2)}, u32[]{:S(2)}) async-start(bf16[32,128,256]{2,1,0:T(8,128)(2,1)} %gather_fusion.1), calls=%async_computation.1 | async-start | bytes 4194304 | tf_op jit(solution)/shard_map/all_to_all | solution.py:143
  105.2 55.5 %all-to-all-start.2 = ((bf16[32,128,256]{2,1,0:T(8,128)(2,1)}), bf16[32,128,256]{2,1,0:T(8,128)(2,1)}, u32[]{:S(2)}, u32[]{:S(2)}) async-start(bf16[32,128,256]{2,1,0:T(8,128)(2,1)} %gather_fusion), calls=%async_computation.2 | async-start | bytes 4194304 | tf_op jit(solution)/shard_map/all_to_all | solution.py:143
  110.7 49.9 %collective-permute-start = (bf16[32,128,256]{2,1,0:T(8,128)(2,1)}, bf16[32,128,256]{2,1,0:T(8,128)(2,1)}, u32[]{:S(2)}, u32[]{:S(2)}) collective-permute-start(bf16[32,128,256]{2,1,0:T(8,128)(2,1)} %all-to-all-done.1.mine0_ref), channel_id=1, source_target_pairs={{0,4},{1,5},{2,6},{3,7},{4,0},{5,1},{6,2},{7,3},{8,12},{9,13},{10,... | collective-permute-start | bytes 6291464 | tf_op jit(solution)/shard_map/ppermute | solution.py:145
  160.6 73.9 %all-to-all-start.3 = ((bf16[16,128,512]{2,1,0:T(8,128)(2,1)}), bf16[16,128,512]{2,1,0:T(8,128)(2,1)}, u32[]{:S(2)}, u32[]{:S(2)}) async-start(bf16[16,128,512]{2,1,0:T(8,128)(2,1)} %reshape.152), calls=%async_computation.3 | async-start | bytes 4194304 | tf_op jit(solution)/shard_map/all_to_all | solution.py:150
  165.1 69.4 %collective-permute-start.1 = (bf16[32,128,256]{2,1,0:T(8,128)(2,1)}, bf16[32,128,256]{2,1,0:T(8,128)(2,1)}, u32[]{:S(2)}, u32[]{:S(2)}) collective-permute-start(bf16[32,128,256]{2,1,0:T(8,128)(2,1)} %all-to-all-done.2.mine1_ref), channel_id=1, source_target_pairs={{0,4},{1,5},{2,6},{3,7},{4,0},{5,1},{6,2},{7,3},{8,12},{9,13},{10,... | collective-permute-start | bytes 6291464 | tf_op jit(solution)/shard_map/ppermute | solution.py:145

commit v11 on v10

--- a/solution.py
+++ b/solution.py
@@ -43,8 +43,8 @@
     row_max = jnp.max(scores, axis=1, keepdims=True)
     weights = jnp.exp2((scores - row_max) * (score_scale * LOG2_E))
     inverse = 1.0 / jnp.sum(weights, axis=1, keepdims=True)
-    acc = jnp.dot(weights.astype(jnp.bfloat16), values, preferred_element_type=jnp.float32)
-    acc = acc * inverse
+    probs = (weights * inverse).astype(jnp.bfloat16)
+    acc = jnp.dot(probs, values, preferred_element_type=jnp.float32)
     tokens = query_ref.shape[0]
     for h in range(heads):
         out_ref[:, h * head_dim:(h + 1) * head_dim] = acc[h * tokens:(h + 1) * tokens].astype(
@@ -156,15 +156,18 @@
     slot_index = jnp.concatenate([zero_col, slot_index], axis=1)
     slot_which = jnp.concatenate([zero_col, slot_which], axis=1)
     score_scale = head_dim ** (-0.5)
-    width = group_size * head_dim
-    attended = attend_all(
-        local_queries, 0, width, own_blocks, mine + peer, slot_index, slot_which,
-        my_counts, score_scale
-    )
-    back = lax.all_to_all(
-        attended.reshape(head_count, tokens, width), "head", split_axis=0, concat_axis=0,
-        tiled=True
-    )
+    width = group_size * head_dim // 2
+    pieces = []
+    for column in range(2):
+        attended = attend_all(
+            local_queries, column, width, own_blocks, mine + peer, slot_index, slot_which,
+            my_counts, score_scale
+        )
+        pieces.append(lax.all_to_all(
+            attended.reshape(head_count, tokens, width), "head", split_axis=0, concat_axis=0,
+            tiled=True
+        ))
+    back = jnp.stack(pieces, axis=2)
     back = jnp.transpose(back.reshape(2, 2, 4, tokens, group_size, head_dim), (3, 0, 2, 1, 4, 5))
     return back.reshape(tokens, query_heads, head_dim)
 

time: 336 us -> 337 us (level)
  the two profiles are of different devices: /device:TPU:16 before, /device:TPU:73 now
where the time goes in v11:
time: 337 us; the launch traced here: 336 us
  waiting for transfers between devices  178 us (53%)
  starting transfers between devices  45.8 us (14%)
  Pallas kernels  42 us (12%)
  blocking collectives  33.4 us (10%)
  local copies, waits for them, and re-layouts  29.2 us (9%)
  other arithmetic  6.97 us (2%)
    ppermute x2, waiting for transfers between devices, on_device(): peer.append(lax.ppermute(got, 'head', partner))  102 us
    all_to_all x2, waiting for transfers between devices, on_device(): got = lax.all_to_all(picked, 'seq', split_axis=0, concat_axis=0, tiled=True)  50.1 us
    pallas_call x2, Pallas kernels, attend_all(): pl.pallas_call(kernel, out_shape=jax.ShapeDtypeStruct((seq_rows, width),...  42 us
    all_to_all x1, blocking collectives, on_device(): lax.all_to_all(attended.reshape(head_count, tokens, width), 'head', split...  33.4 us
    all_to_all x1, waiting for transfers between devices, on_device(): lax.all_to_all(kv, 'head', split_axis=0, concat_axis=0, tiled=True)  21 us
    all_to_all x2, starting transfers between devices, on_device(): got = lax.all_to_all(picked, 'seq', split_axis=0, concat_axis=0, tiled=True)  16 us
    all_to_all x1, starting transfers between devices, on_device(): lax.all_to_all(kv, 'head', split_axis=0, concat_axis=0, tiled=True)  11.7 us
    all_to_all x1, starting transfers between devices, on_device(): lax.all_to_all(attended.reshape(head_count, tokens, width), 'head', split...  8.7 us
  transfers between devices with their start and end apart: 7, of which 6 were waited for; matrix products, arithmetic and copies ran while one was open for 6% of the time, Pallas kernels for 6%

profile of v11, /device:TPU:73, one launch (start us, length us, event | category | flops | bytes accessed | tf_op | source)
XLA Modules:
  0.0 335.9 jit_solution(13324462297783032288)
XLA Ops:
  0.0 1.1 pad_maximum_fusion.1
  1.3 1.1 broadcast_in_dim.12
  2.4 11.7 %all-to-all-start = ((bf16[16,128,256]{2,1,0:T(8,128)(2,1)}), bf16[16,128,256]{2,1,0:T(8,128)(2,1)S(1)}, u32[]{:S(2)}, u32[]{:S(2)}) async-start(bf16[16,128,256]{2,1,0:T(8,128)(2,1)} %bitcast.6), calls=%async_computation | async-start | bytes 2097152 | tf_op jit(solution)/shard_map/all_to_all | solution.py:131
  14.3 0.7 dynamic-slice_reduce_fusion.2
  15.2 0.7 dynamic-slice_bitcast_fusion
  16.6 3.9 %fusion.3 = s32[32,112]{0,1:T(8,128)S(1)} fusion(s32[32,112]{0,1:T(8,128)S(1)} %get-tuple-element.12, pred[32,112]{0,1:T(8,128)(4,1)S(1)} %get-tuple-element.10), kind=kOutput, calls=%fused_computation.7 | output fusion | flops 13758976 | bytes 32256 | tf_op jit(solution)/shard_map/jit(cumsum)/reduce_window_sum | solution.py:97
  20.8 21.0 %all-to-all-done.own_ref = bf16[16,128,256]{2,1,0:T(8,128)(2,1)S(1)} async-done(((bf16[16,128,256]{2,1,0:T(8,128)(2,1)}), bf16[16,128,256]{2,1,0:T(8,128)(2,1)S(1)}, u32[]{:S(2)}, u32[]{:S(2)}) %all-to-all-start) | async-done | bytes 1048608 | tf_op jit(solution)/shard_map/all_to_all | solution.py:131
  41.8 2.0 gather_fusion.1
  43.8 11.4 %all-to-all-start.1 = ((bf16[32,128,256]{2,1,0:T(8,128)(2,1)}), bf16[32,128,256]{2,1,0:T(8,128)(2,1)S(1)}, u32[]{:S(2)}, u32[]{:S(2)}) async-start(bf16[32,128,256]{2,1,0:T(8,128)(2,1)} %gather_fusion.1), calls=%async_computation.1 | async-start | bytes 4194304 | tf_op jit(solution)/shard_map/all_to_all | solution.py:143
  55.2 2.0 gather_fusion
  57.2 48.3 %all-to-all-done.1.mine0_ref = bf16[32,128,256]{2,1,0:T(8,128)(2,1)S(1)} async-done(((bf16[32,128,256]{2,1,0:T(8,128)(2,1)}), bf16[32,128,256]{2,1,0:T(8,128)(2,1)S(1)}, u32[]{:S(2)}, u32[]{:S(2)}) %all-to-all-start.1) | async-done | bytes 2097184 | tf_op jit(solution)/shard_map/all_to_all | solution.py:143
  105.5 4.6 %all-to-all-start.2 = ((bf16[32,128,256]{2,1,0:T(8,128)(2,1)}), bf16[32,128,256]{2,1,0:T(8,128)(2,1)}, u32[]{:S(2)}, u32[]{:S(2)}) async-start(bf16[32,128,256]{2,1,0:T(8,128)(2,1)} %gather_fusion), calls=%async_computation.2 | async-start | bytes 4194304 | tf_op jit(solution)/shard_map/all_to_all | solution.py:143
  110.1 1.9 collective-permute-start
  112.1 3.9 %copy.57 = bf16[2,2,4,128,4,128]{5,4,3,2,1,0:T(4,128)(2,1)} copy(bf16[2,2,4,128,4,128]{5,4,1,2,0,3:T(4,128)(2,1)} %bitcast.31) | data formatting | bytes 4194304 | tf_op jit(solution)/shard_map/transpose | solution.py:146
  116.0 4.1 %reshape.155 = bf16[16,128,512]{2,1,0:T(8,128)(2,1)} reshape(bf16[2,2,4,128,4,128]{5,4,3,2,1,0:T(4,128)(2,1)} %copy.57) | data formatting | bytes 4194304 | tf_op jit(solution)/shard_map/reshape | solution.py:148
  120.1 38.8 %collective-permute-done.peer0_ref = bf16[32,128,256]{2,1,0:T(8,128)(2,1)} collective-permute-done((bf16[32,128,256]{2,1,0:T(8,128)(2,1)S(1)}, bf16[32,128,256]{2,1,0:T(8,128)(2,1)}, u32[]{:S(2)}, u32[]{:S(2)}) %collective-permute-start) | collective-permute-done | bytes 2097184 | tf_op jit(solution)/shard_map/ppermute | solution.py:145
  158.9 1.7 all-to-all-done.2.mine1_ref
  160.6 4.4 %all-to-all-start.3 = ((bf16[16,128,512]{2,1,0:T(8,128)(2,1)}), bf16[16,128,512]{2,1,0:T(8,128)(2,1)}, u32[]{:S(2)}, u32[]{:S(2)}) async-start(bf16[16,128,512]{2,1,0:T(8,128)(2,1)} %reshape.155), calls=%async_computation.3 | async-start | bytes 4194304 | tf_op jit(solution)/shard_map/all_to_all | solution.py:150
  165.0 3.1 collective-permute-start.1
  169.5 0.7 concatenate.9.slot_ref
  170.2 1.3 dynamic-slice_bitcast_fusion.1.count_ref
  171.5 62.8 %collective-permute-done.1.peer1_ref = bf16[32,128,256]{2,1,0:T(8,128)(2,1)} collective-permute-done((bf16[32,128,256]{2,1,0:T(8,128)(2,1)}, bf16[32,128,256]{2,1,0:T(8,128)(2,1)}, u32[]{:S(2)}, u32[]{:S(2)}) %collective-permute-start.1) | collective-permute-done | bytes 2097184 | tf_op jit(solution)/shard_map/ppermute | solution.py:145
  234.3 21.0 %shard_map.56 = bf16[2048,256]{1,0:T(8,128)(2,1)} custom-call(s32[16,8]{1,0:T(8,128)} %concatenate.9.slot_ref, s32[16,8]{1,0:T(8,128)} %concatenate.10.which_ref, s32[16]{0:T(128)} %dynamic-slice_bitcast_fusion.1.count_ref, bf16[2048,512]{1,0:T(8,128)(2,1)} %bitcast.9.query_ref, bf16[16,128,256]{2,1,0:T(8,128)(2,1)} %copy-done, ...), custom_call_target="tpu_custom_call" | custom-call | tf_op jit(solution)/shard_map/pallas_call | solution.py:65
  255.3 2.3 copy.63
  257.6 8.7 %all-to-all-start.5 = ((bf16[16,128,256]{1,2,0:T(8,128)(2,1)}), bf16[16,128,256]{1,2,0:T(8,128)(2,1)}, u32[]{:S(2)}, u32[]{:S(2)}) async-start(bf16[16,128,256]{1,2,0:T(8,128)(2,1)} %copy.63), calls=%async_computation.5 | async-start | bytes 2097152 | tf_op jit(solution)/shard_map/all_to_all | solution.py:166
  266.3 21.0 %shard_map.55 = bf16[2048,256]{1,0:T(8,128)(2,1)} custom-call(s32[16,8]{1,0:T(8,128)} %concatenate.9.slot_ref, s32[16,8]{1,0:T(8,128)} %concatenate.10.which_ref, s32[16]{0:T(128)} %dynamic-slice_bitcast_fusion.1.count_ref, bf16[2048,512]{1,0:T(8,128)(2,1)} %bitcast.9.query_ref, bf16[16,128,256]{2,1,0:T(8,128)(2,1)} %copy-done, ...), custom_call_target="tpu_custom_call" | custom-call | tf_op jit(solution)/shard_map/pallas_call | solution.py:65
  287.3 1.6 copy.62
  288.9 5.6 %all-to-all-done.5 = bf16[16,128,256]{1,2,0:T(8,128)(2,1)} async-done(((bf16[16,128,256]{1,2,0:T(8,128)(2,1)}), bf16[16,128,256]{1,2,0:T(8,128)(2,1)}, u32[]{:S(2)}, u32[]{:S(2)}) %all-to-all-start.5) | async-done | bytes 1048608 | tf_op jit(solution)/shard_map/all_to_all | solution.py:166
  294.4 33.4 %all_to_all.30 = bf16[16,128,256]{1,2,0:T(8,128)(2,1)S(1)} all-to-all(bf16[16,128,256]{1,2,0:T(8,128)(2,1)S(1)} %copy.62), channel_id=1, replica_groups=mesh['seq'=32,'head'=16] {'head'}, dimensions={0} | all-to-all | bytes 2097152 | tf_op jit(solution)/shard_map/all_to_all | solution.py:166
  327.8 1.4 pad_maximum_fusion
  329.3 2.4 copy.64
  331.6 4.3 %copy.65 = bf16[128,64,128]{2,1,0:T(8,128)(2,1)} copy(bf16[128,64,128]{2,0,1:T(8,128)(2,1)} %bitcast.27) | data formatting | bytes 4194304 | tf_op jit(solution)/shard_map/reshape | solution.py:172
  (34 shorter events, 2.7 us)
Async XLA Ops:
  2.4 39.4 %all-to-all-start = ((bf16[16,128,256]{2,1,0:T(8,128)(2,1)}), bf16[16,128,256]{2,1,0:T(8,128)(2,1)S(1)}, u32[]{:S(2)}, u32[]{:S(2)}) async-start(bf16[16,128,256]{2,1,0:T(8,128)(2,1)} %bitcast.6), calls=%async_computation | async-start | bytes 2097152 | tf_op jit(solution)/shard_map/all_to_all | solution.py:131
  41.8 13.4 %copy-start = (bf16[16,128,256]{2,1,0:T(8,128)(2,1)}, bf16[16,128,256]{2,1,0:T(8,128)(2,1)S(1)}, u32[]{:S(2)}) copy-start(bf16[16,128,256]{2,1,0:T(8,128)(2,1)S(1)} %all-to-all-done.own_ref) | copy-start | bytes 3145732
  43.8 61.7 %all-to-all-start.1 = ((bf16[32,128,256]{2,1,0:T(8,128)(2,1)}), bf16[32,128,256]{2,1,0:T(8,128)(2,1)S(1)}, u32[]{:S(2)}, u32[]{:S(2)}) async-start(bf16[32,128,256]{2,1,0:T(8,128)(2,1)} %gather_fusion.1), calls=%async_computation.1 | async-start | bytes 4194304 | tf_op jit(solution)/shard_map/all_to_all | solution.py:143
  105.5 6.5 %copy-start.1 = (bf16[32,128,256]{2,1,0:T(8,128)(2,1)}, bf16[32,128,256]{2,1,0:T(8,128)(2,1)S(1)}, u32[]{:S(2)}) copy-start(bf16[32,128,256]{2,1,0:T(8,128)(2,1)S(1)} %all-to-all-done.1.mine0_ref) | copy-start | bytes 6291460
  105.5 55.1 %all-to-all-start.2 = ((bf16[32,128,256]{2,1,0:T(8,128)(2,1)}), bf16[32,128,256]{2,1,0:T(8,128)(2,1)}, u32[]{:S(2)}, u32[]{:S(2)}) async-start(bf16[32,128,256]{2,1,0:T(8,128)(2,1)} %gather_fusion), calls=%async_computation.2 | async-start | bytes 4194304 | tf_op jit(solution)/shard_map/all_to_all | solution.py:143
  110.1 48.7 %collective-permute-start = (bf16[32,128,256]{2,1,0:T(8,128)(2,1)S(1)}, bf16[32,128,256]{2,1,0:T(8,128)(2,1)}, u32[]{:S(2)}, u32[]{:S(2)}) collective-permute-start(bf16[32,128,256]{2,1,0:T(8,128)(2,1)S(1)} %all-to-all-done.1.mine0_ref), channel_id=1, source_target_pairs={{0,4},{1,5},{2,6},{3,7},{4,0},{5,1},{6,2},{7,3},{8,12},{9,13},{10,... | collective-permute-start | bytes 6291464 | tf_op jit(solution)/shard_map/ppermute | solution.py:145
  160.6 73.7 %all-to-all-start.3 = ((bf16[16,128,512]{2,1,0:T(8,128)(2,1)}), bf16[16,128,512]{2,1,0:T(8,128)(2,1)}, u32[]{:S(2)}, u32[]{:S(2)}) async-start(bf16[16,128,512]{2,1,0:T(8,128)(2,1)} %reshape.155), calls=%async_computation.3 | async-start | bytes 4194304 | tf_op jit(solution)/shard_map/all_to_all | solution.py:150
  165.0 69.3 %collective-permute-start.1 = (bf16[32,128,256]{2,1,0:T(8,128)(2,1)}, bf16[32,128,256]{2,1,0:T(8,128)(2,1)}, u32[]{:S(2)}, u32[]{:S(2)}) collective-permute-start(bf16[32,128,256]{2,1,0:T(8,128)(2,1)} %all-to-all-done.2.mine1_ref), channel_id=1, source_target_pairs={{0,4},{1,5},{2,6},{3,7},{4,0},{5,1},{6,2},{7,3},{8,12},{9,13},{10,... | collective-permute-start | bytes 6291464 | tf_op jit(solution)/shard_map/ppermute | solution.py:145
  257.6 36.9 %all-to-all-start.5 = ((bf16[16,128,256]{1,2,0:T(8,128)(2,1)}), bf16[16,128,256]{1,2,0:T(8,128)(2,1)}, u32[]{:S(2)}, u32[]{:S(2)}) async-start(bf16[16,128,256]{1,2,0:T(8,128)(2,1)} %copy.63), calls=%async_computation.5 | async-start | bytes 2097152 | tf_op jit(solution)/shard_map/all_to_all | solution.py:166

commit v12 on v10

--- a/solution.py
+++ b/solution.py
@@ -43,8 +43,8 @@
     row_max = jnp.max(scores, axis=1, keepdims=True)
     weights = jnp.exp2((scores - row_max) * (score_scale * LOG2_E))
     inverse = 1.0 / jnp.sum(weights, axis=1, keepdims=True)
-    acc = jnp.dot(weights.astype(jnp.bfloat16), values, preferred_element_type=jnp.float32)
-    acc = acc * inverse
+    probs = (weights * inverse).astype(jnp.bfloat16)
+    acc = jnp.dot(probs, values, preferred_element_type=jnp.float32)
     tokens = query_ref.shape[0]
     for h in range(heads):
         out_ref[:, h * head_dim:(h + 1) * head_dim] = acc[h * tokens:(h + 1) * tokens].astype(

time: 336 us -> 337 us (level)
  the two profiles are of different devices: /device:TPU:16 before, /device:TPU:72 now
where the time goes in v12:
time: 337 us
  waiting for transfers between devices  179 us (53%)
  blocking collectives  60.3 us (18%)
  starting transfers between devices  35.2 us (10%)
  Pallas kernels  35.1 us (10%)
  local copies, waits for them, and re-layouts  21.7 us (6%)
  other arithmetic  5.5 us (2%)
    ppermute x2, waiting for transfers between devices, on_device(): peer.append(lax.ppermute(got, 'head', partner))  106 us
    all_to_all x1, blocking collectives, on_device(): lax.all_to_all(attended.reshape(head_count, tokens, width), 'head', split...  60.3 us
    all_to_all x2, waiting for transfers between devices, on_device(): got = lax.all_to_all(picked, 'seq', split_axis=0, concat_axis=0, tiled=True)  49.3 us
    pallas_call x1, Pallas kernels, attend_all(): pl.pallas_call(kernel, out_shape=jax.ShapeDtypeStruct((seq_rows, width),...  35.1 us
    all_to_all x1, waiting for transfers between devices, on_device(): lax.all_to_all(kv, 'head', split_axis=0, concat_axis=0, tiled=True)  23.2 us
    all_to_all x2, starting transfers between devices, on_device(): got = lax.all_to_all(picked, 'seq', split_axis=0, concat_axis=0, tiled=True)  13.2 us
    all_to_all x1, starting transfers between devices, on_device(): lax.all_to_all(kv, 'head', split_axis=0, concat_axis=0, tiled=True)  12 us
  transfers between devices with their start and end apart: 6, of which 5 were waited for; matrix products, arithmetic and copies ran while one was open for 5% of the time, Pallas kernels for 0%

profile of v12, /device:TPU:72, one launch (start us, length us, event | category | flops | bytes accessed | tf_op | source)
XLA Modules:
  0.0 336.7 jit_solution(2770277654836544805)
XLA Ops:
  0.0 1.1 pad_maximum_fusion
  1.3 1.1 broadcast_in_dim.12
  2.4 12.0 %all-to-all-start = ((bf16[16,128,256]{2,1,0:T(8,128)(2,1)}), bf16[16,128,256]{2,1,0:T(8,128)(2,1)S(1)}, u32[]{:S(2)}, u32[]{:S(2)}) async-start(bf16[16,128,256]{2,1,0:T(8,128)(2,1)} %bitcast.6), calls=%async_computation | async-start | bytes 2097152 | tf_op jit(solution)/shard_map/all_to_all | solution.py:131
  14.4 0.7 dynamic-slice_bitcast_fusion
  15.2 0.1 copy.35
  15.3 0.2 reshape.150
  15.6 0.7 dynamic-slice_reduce_fusion.2
  16.8 3.9 %fusion.3 = s32[32,112]{0,1:T(8,128)S(1)} fusion(s32[32,112]{0,1:T(8,128)S(1)} %get-tuple-element.12, pred[32,112]{0,1:T(8,128)(4,1)S(1)} %get-tuple-element.10), kind=kOutput, calls=%fused_computation.6 | output fusion | flops 13758976 | bytes 32256 | tf_op jit(solution)/shard_map/jit(cumsum)/reduce_window_sum | solution.py:97
  20.8 0.2 multiply_reduce_fusion
  21.0 23.2 %all-to-all-done.own_ref = bf16[16,128,256]{2,1,0:T(8,128)(2,1)S(1)} async-done(((bf16[16,128,256]{2,1,0:T(8,128)(2,1)}), bf16[16,128,256]{2,1,0:T(8,128)(2,1)S(1)}, u32[]{:S(2)}, u32[]{:S(2)}) %all-to-all-start) | async-done | bytes 1048608 | tf_op jit(solution)/shard_map/all_to_all | solution.py:131
  44.2 2.0 gather_fusion.1
  46.2 8.7 %all-to-all-start.1 = ((bf16[32,128,256]{2,1,0:T(8,128)(2,1)}), bf16[32,128,256]{2,1,0:T(8,128)(2,1)}, u32[]{:S(2)}, u32[]{:S(2)}) async-start(bf16[32,128,256]{2,1,0:T(8,128)(2,1)} %gather_fusion.1), calls=%async_computation.1 | async-start | bytes 4194304 | tf_op jit(solution)/shard_map/all_to_all | solution.py:143
  54.9 2.0 gather_fusion
  56.9 48.5 %all-to-all-done.1.mine0_ref = bf16[32,128,256]{2,1,0:T(8,128)(2,1)} async-done(((bf16[32,128,256]{2,1,0:T(8,128)(2,1)}), bf16[32,128,256]{2,1,0:T(8,128)(2,1)}, u32[]{:S(2)}, u32[]{:S(2)}) %all-to-all-start.1) | async-done | bytes 2097184 | tf_op jit(solution)/shard_map/all_to_all | solution.py:143
  105.5 4.5 %all-to-all-start.2 = ((bf16[32,128,256]{2,1,0:T(8,128)(2,1)}), bf16[32,128,256]{2,1,0:T(8,128)(2,1)}, u32[]{:S(2)}, u32[]{:S(2)}) async-start(bf16[32,128,256]{2,1,0:T(8,128)(2,1)} %gather_fusion), calls=%async_computation.2 | async-start | bytes 4194304 | tf_op jit(solution)/shard_map/all_to_all | solution.py:143
  110.0 1.9 collective-permute-start
  112.0 2.6 copy.40
  114.5 2.2 reshape.152
  116.7 43.1 %collective-permute-done.peer0_ref = bf16[32,128,256]{2,1,0:T(8,128)(2,1)} collective-permute-done((bf16[32,128,256]{2,1,0:T(8,128)(2,1)}, bf16[32,128,256]{2,1,0:T(8,128)(2,1)}, u32[]{:S(2)}, u32[]{:S(2)}) %collective-permute-start) | collective-permute-done | bytes 2097184 | tf_op jit(solution)/shard_map/ppermute | solution.py:145
  159.8 0.7 all-to-all-done.2.mine1_ref
  160.6 4.4 %all-to-all-start.3 = ((bf16[16,128,512]{2,1,0:T(8,128)(2,1)}), bf16[16,128,512]{2,1,0:T(8,128)(2,1)}, u32[]{:S(2)}, u32[]{:S(2)}) async-start(bf16[16,128,512]{2,1,0:T(8,128)(2,1)} %reshape.152), calls=%async_computation.3 | async-start | bytes 4194304 | tf_op jit(solution)/shard_map/all_to_all | solution.py:150
  165.0 3.7 %collective-permute-start.1 = (bf16[32,128,256]{2,1,0:T(8,128)(2,1)}, bf16[32,128,256]{2,1,0:T(8,128)(2,1)}, u32[]{:S(2)}, u32[]{:S(2)}) collective-permute-start(bf16[32,128,256]{2,1,0:T(8,128)(2,1)} %all-to-all-done.2.mine1_ref), channel_id=1, source_target_pairs={{0,4},{1,5},{2,6},{3,7},{4,0},{5,1},{6,2},{7,3},{8,12},{9,13},{10,... | collective-permute-start | bytes 6291464 | tf_op jit(solution)/shard_map/ppermute | solution.py:145
  168.7 0.2 minimum_reduce_fusion
  169.0 0.2 dynamic-slice_reduce_fusion.1
  169.4 0.7 concatenate.10.which_ref
  170.0 0.7 concatenate.9.slot_ref
  170.7 1.3 dynamic-slice_bitcast_fusion.1.count_ref
  172.0 63.1 %collective-permute-done.1.peer1_ref = bf16[32,128,256]{2,1,0:T(8,128)(2,1)} collective-permute-done((bf16[32,128,256]{2,1,0:T(8,128)(2,1)}, bf16[32,128,256]{2,1,0:T(8,128)(2,1)}, u32[]{:S(2)}, u32[]{:S(2)}) %collective-permute-start.1) | collective-permute-done | bytes 2097184 | tf_op jit(solution)/shard_map/ppermute | solution.py:145
  235.1 35.1 %shard_map.55 = bf16[2048,512]{1,0:T(8,128)(2,1)} custom-call(s32[16,8]{1,0:T(8,128)} %concatenate.9.slot_ref, s32[16,8]{1,0:T(8,128)} %concatenate.10.which_ref, s32[16]{0:T(128)} %dynamic-slice_bitcast_fusion.1.count_ref, bf16[2048,512]{1,0:T(8,128)(2,1)} %bitcast.9.query_ref, bf16[16,128,256]{2,1,0:T(8,128)(2,1)} %copy-done, ...), custom_call_target="tpu_custom_call" | custom-call | tf_op jit(solution)/shard_map/pallas_call | solution.py:65
  270.2 60.3 %all_to_all.25 = bf16[16,128,512]{2,1,0:T(8,128)(2,1)S(1)} all-to-all(bf16[16,128,512]{2,1,0:T(8,128)(2,1)} %bitcast.22), channel_id=1, replica_groups=mesh['seq'=32,'head'=16] {'head'}, dimensions={0} | all-to-all | bytes 4194304 | tf_op jit(solution)/shard_map/all_to_all | solution.py:164
  330.5 2.1 reshape.157
  332.6 4.1 %copy.45 = bf16[2,2,4,128,4,128]{5,4,1,2,0,3:T(4,128)(2,1)} copy(bf16[2,2,4,128,4,128]{5,4,3,2,1,0:T(4,128)(2,1)} %reshape.157) | data formatting | bytes 4194304 | tf_op jit(solution)/shard_map/reshape | solution.py:168
  (26 shorter events, 1.2 us)
Async XLA Ops:
  2.4 41.8 %all-to-all-start = ((bf16[16,128,256]{2,1,0:T(8,128)(2,1)}), bf16[16,128,256]{2,1,0:T(8,128)(2,1)S(1)}, u32[]{:S(2)}, u32[]{:S(2)}) async-start(bf16[16,128,256]{2,1,0:T(8,128)(2,1)} %bitcast.6), calls=%async_computation | async-start | bytes 2097152 | tf_op jit(solution)/shard_map/all_to_all | solution.py:131
  44.2 10.7 %copy-start = (bf16[16,128,256]{2,1,0:T(8,128)(2,1)}, bf16[16,128,256]{2,1,0:T(8,128)(2,1)S(1)}, u32[]{:S(2)}) copy-start(bf16[16,128,256]{2,1,0:T(8,128)(2,1)S(1)} %all-to-all-done.own_ref) | copy-start | bytes 3145732
  46.2 59.3 %all-to-all-start.1 = ((bf16[32,128,256]{2,1,0:T(8,128)(2,1)}), bf16[32,128,256]{2,1,0:T(8,128)(2,1)}, u32[]{:S(2)}, u32[]{:S(2)}) async-start(bf16[32,128,256]{2,1,0:T(8,128)(2,1)} %gather_fusion.1), calls=%async_computation.1 | async-start | bytes 4194304 | tf_op jit(solution)/shard_map/all_to_all | solution.py:143
  105.5 55.1 %all-to-all-start.2 = ((bf16[32,128,256]{2,1,0:T(8,128)(2,1)}), bf16[32,128,256]{2,1,0:T(8,128)(2,1)}, u32[]{:S(2)}, u32[]{:S(2)}) async-start(bf16[32,128,256]{2,1,0:T(8,128)(2,1)} %gather_fusion), calls=%async_computation.2 | async-start | bytes 4194304 | tf_op jit(solution)/shard_map/all_to_all | solution.py:143
  110.0 49.8 %collective-permute-start = (bf16[32,128,256]{2,1,0:T(8,128)(2,1)}, bf16[32,128,256]{2,1,0:T(8,128)(2,1)}, u32[]{:S(2)}, u32[]{:S(2)}) collective-permute-start(bf16[32,128,256]{2,1,0:T(8,128)(2,1)} %all-to-all-done.1.mine0_ref), channel_id=1, source_target_pairs={{0,4},{1,5},{2,6},{3,7},{4,0},{5,1},{6,2},{7,3},{8,12},{9,13},{10,... | collective-permute-start | bytes 6291464 | tf_op jit(solution)/shard_map/ppermute | solution.py:145
  160.6 74.5 %all-to-all-start.3 = ((bf16[16,128,512]{2,1,0:T(8,128)(2,1)}), bf16[16,128,512]{2,1,0:T(8,128)(2,1)}, u32[]{:S(2)}, u32[]{:S(2)}) async-start(bf16[16,128,512]{2,1,0:T(8,128)(2,1)} %reshape.152), calls=%async_computation.3 | async-start | bytes 4194304 | tf_op jit(solution)/shard_map/all_to_all | solution.py:150
  165.0 70.1 %collective-permute-start.1 = (bf16[32,128,256]{2,1,0:T(8,128)(2,1)}, bf16[32,128,256]{2,1,0:T(8,128)(2,1)}, u32[]{:S(2)}, u32[]{:S(2)}) collective-permute-start(bf16[32,128,256]{2,1,0:T(8,128)(2,1)} %all-to-all-done.2.mine1_ref), channel_id=1, source_target_pairs={{0,4},{1,5},{2,6},{3,7},{4,0},{5,1},{6,2},{7,3},{8,12},{9,13},{10,... | collective-permute-start | bytes 6291464 | tf_op jit(solution)/shard_map/ppermute | solution.py:145

commit v13 on v9

--- a/solution.py
+++ b/solution.py
@@ -31,24 +31,29 @@
             @pl.when(which == code)
             def _(source=source, slot=slot, index=index):
                 block_buf[slot * BLK:(slot + 1) * BLK] = source[index]
-    blocks = block_buf[...]
-    keys = blocks[:, :head_dim]
-    values = blocks[:, head_dim:]
-    scores = lax.dot_general(
-        query, keys, (((1,), (1,)), ((), ())), preferred_element_type=jnp.float32
-    ) * score_scale
-    key_slot = lax.broadcasted_iota(jnp.int32, (1, slot_total * BLK), 1) // BLK
-    scores = jnp.where(key_slot < row_count, scores, NEG_FILL)
-    row_max = jnp.max(scores, axis=1, keepdims=True)
-    weights = jnp.exp(scores - row_max)
-    inverse = 1.0 / jnp.sum(weights, axis=1, keepdims=True)
-    probs = (weights * inverse).astype(jnp.bfloat16)
-    acc = jnp.dot(probs, values, preferred_element_type=jnp.float32)
-    tokens = query_ref.shape[0]
-    for h in range(heads):
-        out_ref[:, h * head_dim:(h + 1) * head_dim] = acc[h * tokens:(h + 1) * tokens].astype(
-            out_ref.dtype
-        )
+    def attend(masked):
+        blocks = block_buf[...]
+        keys = blocks[:, :head_dim]
+        values = blocks[:, head_dim:]
+        scores = lax.dot_general(
+            query, keys, (((1,), (1,)), ((), ())), preferred_element_type=jnp.float32
+        ) * score_scale
+        if masked:
+            key_slot = lax.broadcasted_iota(jnp.int32, (1, slot_total * BLK), 1) // BLK
+            scores = jnp.where(key_slot < row_count, scores, NEG_FILL)
+        row_max = jnp.max(scores, axis=1, keepdims=True)
+        weights = jnp.exp(scores - row_max)
+        inverse = 1.0 / jnp.sum(weights, axis=1, keepdims=True)
+        probs = (weights * inverse).astype(jnp.bfloat16)
+        acc = jnp.dot(probs, values, preferred_element_type=jnp.float32)
+        tokens = query_ref.shape[0]
+        for h in range(heads):
+            out_ref[:, h * head_dim:(h + 1) * head_dim] = acc[
+                h * tokens:(h + 1) * tokens
+            ].astype(out_ref.dtype)
+
+    pl.when(row_count >= slot_total)(lambda: attend(False))
+    pl.when(row_count < slot_total)(lambda: attend(True))
 
 
 def attend_all(local_queries, column, width, own_blocks, received, slot_index, slot_which,

time: 338 us -> 338 us (level)
  no operation moved by 1% of the time
where the time goes in v13:
time: 338 us; the launch traced here: 337 us
  waiting for transfers between devices  171 us (51%)
  blocking collectives  60.4 us (18%)
  starting transfers between devices  42.6 us (13%)
  Pallas kernels  36 us (11%)
  local copies, waits for them, and re-layouts  21.7 us (6%)
  other arithmetic  5.5 us (2%)
    ppermute x2, waiting for transfers between devices, on_device(): peer.append(lax.ppermute(got, 'head', partner))  106 us
    all_to_all x1, blocking collectives, on_device(): lax.all_to_all(attended.reshape(head_count, tokens, width), 'head', split...  60.4 us
    all_to_all x2, waiting for transfers between devices, on_device(): got = lax.all_to_all(picked, 'seq', split_axis=0, concat_axis=0, tiled=True)  47.4 us
    pallas_call x1, Pallas kernels, attend_all(): pl.pallas_call(kernel, out_shape=jax.ShapeDtypeStruct((seq_rows, width),...  36 us
    all_to_all x2, starting transfers between devices, on_device(): got = lax.all_to_all(picked, 'seq', split_axis=0, concat_axis=0, tiled=True)  19.7 us
    all_to_all x1, waiting for transfers between devices, on_device(): lax.all_to_all(kv, 'head', split_axis=0, concat_axis=0, tiled=True)  17.6 us
    all_to_all x1, starting transfers between devices, on_device(): lax.all_to_all(kv, 'head', split_axis=0, concat_axis=0, tiled=True)  12.9 us
  transfers between devices with their start and end apart: 6, of which 4 were waited for; matrix products, arithmetic and copies ran while one was open for 5% of the time, Pallas kernels for 0%

profile of v13, /device:TPU:16, one launch (start us, length us, event | category | flops | bytes accessed | tf_op | source)
XLA Modules:
  0.0 337.1 jit_solution(4324268866947056175)
XLA Ops:
  0.0 1.1 pad_maximum_fusion
  1.1 0.1 reshape.153
  1.3 1.1 broadcast_in_dim.12
  2.4 12.9 %all-to-all-start = ((bf16[16,128,256]{2,1,0:T(8,128)(2,1)}), bf16[16,128,256]{2,1,0:T(8,128)(2,1)S(1)}, u32[]{:S(2)}, u32[]{:S(2)}) async-start(bf16[16,128,256]{2,1,0:T(8,128)(2,1)} %bitcast.6), calls=%async_computation | async-start | bytes 2097152 | tf_op jit(solution)/shard_map/all_to_all | solution.py:135
  15.3 0.7 dynamic-slice_bitcast_fusion
  16.1 0.1 copy.35
  16.2 0.2 reshape.150
  16.5 0.7 dynamic-slice_reduce_fusion.2
  17.7 3.9 %fusion.3 = s32[32,112]{0,1:T(8,128)S(1)} fusion(s32[32,112]{0,1:T(8,128)S(1)} %get-tuple-element.12, pred[32,112]{0,1:T(8,128)(4,1)S(1)} %get-tuple-element.10), kind=kOutput, calls=%fused_computation.6 | output fusion | flops 13758976 | bytes 32256 | tf_op jit(solution)/shard_map/jit(cumsum)/reduce_window_sum | solution.py:101
  21.7 0.2 multiply_reduce_fusion
  21.9 17.6 %all-to-all-done.own_ref = bf16[16,128,256]{2,1,0:T(8,128)(2,1)S(1)} async-done(((bf16[16,128,256]{2,1,0:T(8,128)(2,1)}), bf16[16,128,256]{2,1,0:T(8,128)(2,1)S(1)}, u32[]{:S(2)}, u32[]{:S(2)}) %all-to-all-start) | async-done | bytes 1048608 | tf_op jit(solution)/shard_map/all_to_all | solution.py:135
  39.5 2.0 gather_fusion.1
  41.5 14.2 %all-to-all-start.1 = ((bf16[32,128,256]{2,1,0:T(8,128)(2,1)}), bf16[32,128,256]{2,1,0:T(8,128)(2,1)}, u32[]{:S(2)}, u32[]{:S(2)}) async-start(bf16[32,128,256]{2,1,0:T(8,128)(2,1)} %gather_fusion.1), calls=%async_computation.1 | async-start | bytes 4194304 | tf_op jit(solution)/shard_map/all_to_all | solution.py:147
  55.7 2.0 gather_fusion
  57.7 47.4 %all-to-all-done.1.mine0_ref = bf16[32,128,256]{2,1,0:T(8,128)(2,1)} async-done(((bf16[32,128,256]{2,1,0:T(8,128)(2,1)}), bf16[32,128,256]{2,1,0:T(8,128)(2,1)}, u32[]{:S(2)}, u32[]{:S(2)}) %all-to-all-start.1) | async-done | bytes 2097184 | tf_op jit(solution)/shard_map/all_to_all | solution.py:147
  105.2 5.5 %all-to-all-start.2 = ((bf16[32,128,256]{2,1,0:T(8,128)(2,1)}), bf16[32,128,256]{2,1,0:T(8,128)(2,1)}, u32[]{:S(2)}, u32[]{:S(2)}) async-start(bf16[32,128,256]{2,1,0:T(8,128)(2,1)} %gather_fusion), calls=%async_computation.2 | async-start | bytes 4194304 | tf_op jit(solution)/shard_map/all_to_all | solution.py:147
  110.7 1.9 collective-permute-start
  112.7 2.6 copy.40
  115.2 2.2 reshape.152
  117.4 43.2 %collective-permute-done.peer0_ref = bf16[32,128,256]{2,1,0:T(8,128)(2,1)} collective-permute-done((bf16[32,128,256]{2,1,0:T(8,128)(2,1)}, bf16[32,128,256]{2,1,0:T(8,128)(2,1)}, u32[]{:S(2)}, u32[]{:S(2)}) %collective-permute-start) | collective-permute-done | bytes 2097184 | tf_op jit(solution)/shard_map/ppermute | solution.py:149
  160.6 4.4 %all-to-all-start.3 = ((bf16[16,128,512]{2,1,0:T(8,128)(2,1)}), bf16[16,128,512]{2,1,0:T(8,128)(2,1)}, u32[]{:S(2)}, u32[]{:S(2)}) async-start(bf16[16,128,512]{2,1,0:T(8,128)(2,1)} %reshape.152), calls=%async_computation.3 | async-start | bytes 4194304 | tf_op jit(solution)/shard_map/all_to_all | solution.py:154
  165.1 3.7 %collective-permute-start.1 = (bf16[32,128,256]{2,1,0:T(8,128)(2,1)}, bf16[32,128,256]{2,1,0:T(8,128)(2,1)}, u32[]{:S(2)}, u32[]{:S(2)}) collective-permute-start(bf16[32,128,256]{2,1,0:T(8,128)(2,1)} %all-to-all-done.2.mine1_ref), channel_id=1, source_target_pairs={{0,4},{1,5},{2,6},{3,7},{4,0},{5,1},{6,2},{7,3},{8,12},{9,13},{10,... | collective-permute-start | bytes 6291464 | tf_op jit(solution)/shard_map/ppermute | solution.py:149
  168.7 0.2 minimum_reduce_fusion
  169.1 0.2 dynamic-slice_reduce_fusion.1
  169.4 0.7 concatenate.10.which_ref
  170.1 0.7 concatenate.9.slot_ref
  170.8 1.3 dynamic-slice_bitcast_fusion.1.count_ref
  172.1 62.4 %collective-permute-done.1.peer1_ref = bf16[32,128,256]{2,1,0:T(8,128)(2,1)} collective-permute-done((bf16[32,128,256]{2,1,0:T(8,128)(2,1)}, bf16[32,128,256]{2,1,0:T(8,128)(2,1)}, u32[]{:S(2)}, u32[]{:S(2)}) %collective-permute-start.1) | collective-permute-done | bytes 2097184 | tf_op jit(solution)/shard_map/ppermute | solution.py:149
  234.5 36.0 %shard_map.55 = bf16[2048,512]{1,0:T(8,128)(2,1)} custom-call(s32[16,8]{1,0:T(8,128)} %concatenate.9.slot_ref, s32[16,8]{1,0:T(8,128)} %concatenate.10.which_ref, s32[16]{0:T(128)} %dynamic-slice_bitcast_fusion.1.count_ref, bf16[2048,512]{1,0:T(8,128)(2,1)} %bitcast.9.query_ref, bf16[16,128,256]{2,1,0:T(8,128)(2,1)} %copy-done, ...), custom_call_target="tpu_custom_call" | custom-call | tf_op jit(solution)/shard_map/pallas_call | solution.py:69
  270.5 60.4 %all_to_all.25 = bf16[16,128,512]{2,1,0:T(8,128)(2,1)S(1)} all-to-all(bf16[16,128,512]{2,1,0:T(8,128)(2,1)} %bitcast.22), channel_id=1, replica_groups=mesh['seq'=32,'head'=16] {'head'}, dimensions={0} | all-to-all | bytes 4194304 | tf_op jit(solution)/shard_map/all_to_all | solution.py:168
  330.9 2.1 reshape.157
  333.0 4.1 %copy.45 = bf16[2,2,4,128,4,128]{5,4,1,2,0,3:T(4,128)(2,1)} copy(bf16[2,2,4,128,4,128]{5,4,3,2,1,0:T(4,128)(2,1)} %reshape.157) | data formatting | bytes 4194304 | tf_op jit(solution)/shard_map/reshape | solution.py:172
  (26 shorter events, 1.1 us)
Async XLA Ops:
  2.4 37.1 %all-to-all-start = ((bf16[16,128,256]{2,1,0:T(8,128)(2,1)}), bf16[16,128,256]{2,1,0:T(8,128)(2,1)S(1)}, u32[]{:S(2)}, u32[]{:S(2)}) async-start(bf16[16,128,256]{2,1,0:T(8,128)(2,1)} %bitcast.6), calls=%async_computation | async-start | bytes 2097152 | tf_op jit(solution)/shard_map/all_to_all | solution.py:135
  39.5 16.2 %copy-start = (bf16[16,128,256]{2,1,0:T(8,128)(2,1)}, bf16[16,128,256]{2,1,0:T(8,128)(2,1)S(1)}, u32[]{:S(2)}) copy-start(bf16[16,128,256]{2,1,0:T(8,128)(2,1)S(1)} %all-to-all-done.own_ref) | copy-start | bytes 3145732
  41.5 63.7 %all-to-all-start.1 = ((bf16[32,128,256]{2,1,0:T(8,128)(2,1)}), bf16[32,128,256]{2,1,0:T(8,128)(2,1)}, u32[]{:S(2)}, u32[]{:S(2)}) async-start(bf16[32,128,256]{2,1,0:T(8,128)(2,1)} %gather_fusion.1), calls=%async_computation.1 | async-start | bytes 4194304 | tf_op jit(solution)/shard_map/all_to_all | solution.py:147
  105.2 55.5 %all-to-all-start.2 = ((bf16[32,128,256]{2,1,0:T(8,128)(2,1)}), bf16[32,128,256]{2,1,0:T(8,128)(2,1)}, u32[]{:S(2)}, u32[]{:S(2)}) async-start(bf16[32,128,256]{2,1,0:T(8,128)(2,1)} %gather_fusion), calls=%async_computation.2 | async-start | bytes 4194304 | tf_op jit(solution)/shard_map/all_to_all | solution.py:147
  110.7 49.9 %collective-permute-start = (bf16[32,128,256]{2,1,0:T(8,128)(2,1)}, bf16[32,128,256]{2,1,0:T(8,128)(2,1)}, u32[]{:S(2)}, u32[]{:S(2)}) collective-permute-start(bf16[32,128,256]{2,1,0:T(8,128)(2,1)} %all-to-all-done.1.mine0_ref), channel_id=1, source_target_pairs={{0,4},{1,5},{2,6},{3,7},{4,0},{5,1},{6,2},{7,3},{8,12},{9,13},{10,... | collective-permute-start | bytes 6291464 | tf_op jit(solution)/shard_map/ppermute | solution.py:149
  160.6 73.9 %all-to-all-start.3 = ((bf16[16,128,512]{2,1,0:T(8,128)(2,1)}), bf16[16,128,512]{2,1,0:T(8,128)(2,1)}, u32[]{:S(2)}, u32[]{:S(2)}) async-start(bf16[16,128,512]{2,1,0:T(8,128)(2,1)} %reshape.152), calls=%async_computation.3 | async-start | bytes 4194304 | tf_op jit(solution)/shard_map/all_to_all | solution.py:154
  165.1 69.4 %collective-permute-start.1 = (bf16[32,128,256]{2,1,0:T(8,128)(2,1)}, bf16[32,128,256]{2,1,0:T(8,128)(2,1)}, u32[]{:S(2)}, u32[]{:S(2)}) collective-permute-start(bf16[32,128,256]{2,1,0:T(8,128)(2,1)} %all-to-all-done.2.mine1_ref), channel_id=1, source_target_pairs={{0,4},{1,5},{2,6},{3,7},{4,0},{5,1},{6,2},{7,3},{8,12},{9,13},{10,... | collective-permute-start | bytes 6291464 | tf_op jit(solution)/shard_map/ppermute | solution.py:149

commit v14 on v9

--- a/solution.py
+++ b/solution.py
@@ -164,7 +164,7 @@
         attended.reshape(head_count, tokens, width), "head", split_axis=0, concat_axis=0,
         tiled=True
     )
-    back = jnp.transpose(back.reshape(2, 2, 4, tokens, group_size, head_dim), (3, 0, 2, 1, 4, 5))
+    back = jnp.transpose(back.reshape(2, 2, 4, tokens, group_size * head_dim), (3, 0, 2, 1, 4))
     return back.reshape(tokens, query_heads, head_dim)
 
 

time: 338 us -> 336 us (level)
  no operation moved by 1% of the time
where the time goes in v14:
time: 336 us
  waiting for transfers between devices  171 us (51%)
  blocking collectives  61 us (18%)
  starting transfers between devices  42.6 us (13%)
  Pallas kernels  35.3 us (11%)
  local copies, waits for them, and re-layouts  20.3 us (6%)
  other arithmetic  5.5 us (2%)
    ppermute x2, waiting for transfers between devices, on_device(): peer.append(lax.ppermute(got, 'head', partner))  106 us
    all_to_all x1, blocking collectives, on_device(): lax.all_to_all(attended.reshape(head_count, tokens, width), 'head', split...  61 us
    all_to_all x2, waiting for transfers between devices, on_device(): got = lax.all_to_all(picked, 'seq', split_axis=0, concat_axis=0, tiled=True)  47.4 us
    pallas_call x1, Pallas kernels, attend_all(): pl.pallas_call(kernel, out_shape=jax.ShapeDtypeStruct((seq_rows, width),...  35.3 us
    all_to_all x2, starting transfers between devices, on_device(): got = lax.all_to_all(picked, 'seq', split_axis=0, concat_axis=0, tiled=True)  19.7 us
    all_to_all x1, waiting for transfers between devices, on_device(): lax.all_to_all(kv, 'head', split_axis=0, concat_axis=0, tiled=True)  17.6 us
    all_to_all x1, starting transfers between devices, on_device(): lax.all_to_all(kv, 'head', split_axis=0, concat_axis=0, tiled=True)  12.9 us
  transfers between devices with their start and end apart: 6, of which 4 were waited for; matrix products, arithmetic and copies ran while one was open for 5% of the time, Pallas kernels for 0%

profile of v14, /device:TPU:16, one launch (start us, length us, event | category | flops | bytes accessed | tf_op | source)
XLA Modules:
  0.0 335.7 jit_solution(17204073668642591203)
XLA Ops:
  0.0 1.1 pad_maximum_fusion
  1.1 0.1 reshape.153
  1.3 1.1 broadcast_in_dim.12
  2.4 12.9 %all-to-all-start = ((bf16[16,128,256]{2,1,0:T(8,128)(2,1)}), bf16[16,128,256]{2,1,0:T(8,128)(2,1)S(1)}, u32[]{:S(2)}, u32[]{:S(2)}) async-start(bf16[16,128,256]{2,1,0:T(8,128)(2,1)} %bitcast.6), calls=%async_computation | async-start | bytes 2097152 | tf_op jit(solution)/shard_map/all_to_all | solution.py:130
  15.3 0.7 dynamic-slice_bitcast_fusion
  16.1 0.1 copy.35
  16.2 0.2 reshape.150
  16.5 0.7 dynamic-slice_reduce_fusion.2
  17.7 3.9 %fusion.3 = s32[32,112]{0,1:T(8,128)S(1)} fusion(s32[32,112]{0,1:T(8,128)S(1)} %get-tuple-element.12, pred[32,112]{0,1:T(8,128)(4,1)S(1)} %get-tuple-element.10), kind=kOutput, calls=%fused_computation.7 | output fusion | flops 13758976 | bytes 32256 | tf_op jit(solution)/shard_map/jit(cumsum)/reduce_window_sum | solution.py:96
  21.7 0.2 multiply_reduce_fusion
  21.9 17.6 %all-to-all-done.own_ref = bf16[16,128,256]{2,1,0:T(8,128)(2,1)S(1)} async-done(((bf16[16,128,256]{2,1,0:T(8,128)(2,1)}), bf16[16,128,256]{2,1,0:T(8,128)(2,1)S(1)}, u32[]{:S(2)}, u32[]{:S(2)}) %all-to-all-start) | async-done | bytes 1048608 | tf_op jit(solution)/shard_map/all_to_all | solution.py:130
  39.5 2.0 gather_fusion.1
  41.5 14.2 %all-to-all-start.1 = ((bf16[32,128,256]{2,1,0:T(8,128)(2,1)}), bf16[32,128,256]{2,1,0:T(8,128)(2,1)}, u32[]{:S(2)}, u32[]{:S(2)}) async-start(bf16[32,128,256]{2,1,0:T(8,128)(2,1)} %gather_fusion.1), calls=%async_computation.1 | async-start | bytes 4194304 | tf_op jit(solution)/shard_map/all_to_all | solution.py:142
  55.7 2.0 gather_fusion
  57.7 47.4 %all-to-all-done.1.mine0_ref = bf16[32,128,256]{2,1,0:T(8,128)(2,1)} async-done(((bf16[32,128,256]{2,1,0:T(8,128)(2,1)}), bf16[32,128,256]{2,1,0:T(8,128)(2,1)}, u32[]{:S(2)}, u32[]{:S(2)}) %all-to-all-start.1) | async-done | bytes 2097184 | tf_op jit(solution)/shard_map/all_to_all | solution.py:142
  105.2 5.5 %all-to-all-start.2 = ((bf16[32,128,256]{2,1,0:T(8,128)(2,1)}), bf16[32,128,256]{2,1,0:T(8,128)(2,1)}, u32[]{:S(2)}, u32[]{:S(2)}) async-start(bf16[32,128,256]{2,1,0:T(8,128)(2,1)} %gather_fusion), calls=%async_computation.2 | async-start | bytes 4194304 | tf_op jit(solution)/shard_map/all_to_all | solution.py:142
  110.7 1.9 collective-permute-start
  112.7 2.6 copy.40
  115.2 2.2 reshape.152
  117.4 43.2 %collective-permute-done.peer0_ref = bf16[32,128,256]{2,1,0:T(8,128)(2,1)} collective-permute-done((bf16[32,128,256]{2,1,0:T(8,128)(2,1)}, bf16[32,128,256]{2,1,0:T(8,128)(2,1)}, u32[]{:S(2)}, u32[]{:S(2)}) %collective-permute-start) | collective-permute-done | bytes 2097184 | tf_op jit(solution)/shard_map/ppermute | solution.py:144
  160.6 4.4 %all-to-all-start.3 = ((bf16[16,128,512]{2,1,0:T(8,128)(2,1)}), bf16[16,128,512]{2,1,0:T(8,128)(2,1)}, u32[]{:S(2)}, u32[]{:S(2)}) async-start(bf16[16,128,512]{2,1,0:T(8,128)(2,1)} %reshape.152), calls=%async_computation.3 | async-start | bytes 4194304 | tf_op jit(solution)/shard_map/all_to_all | solution.py:149
  165.1 3.7 %collective-permute-start.1 = (bf16[32,128,256]{2,1,0:T(8,128)(2,1)}, bf16[32,128,256]{2,1,0:T(8,128)(2,1)}, u32[]{:S(2)}, u32[]{:S(2)}) collective-permute-start(bf16[32,128,256]{2,1,0:T(8,128)(2,1)} %all-to-all-done.2.mine1_ref), channel_id=1, source_target_pairs={{0,4},{1,5},{2,6},{3,7},{4,0},{5,1},{6,2},{7,3},{8,12},{9,13},{10,... | collective-permute-start | bytes 6291464 | tf_op jit(solution)/shard_map/ppermute | solution.py:144
  168.7 0.2 minimum_reduce_fusion
  169.1 0.2 dynamic-slice_reduce_fusion.1
  169.4 0.7 concatenate.10.which_ref
  170.1 0.7 concatenate.9.slot_ref
  170.8 1.3 dynamic-slice_bitcast_fusion.1.count_ref
  172.1 62.4 %collective-permute-done.1.peer1_ref = bf16[32,128,256]{2,1,0:T(8,128)(2,1)} collective-permute-done((bf16[32,128,256]{2,1,0:T(8,128)(2,1)}, bf16[32,128,256]{2,1,0:T(8,128)(2,1)}, u32[]{:S(2)}, u32[]{:S(2)}) %collective-permute-start.1) | collective-permute-done | bytes 2097184 | tf_op jit(solution)/shard_map/ppermute | solution.py:144
  234.5 35.3 %shard_map.55 = bf16[2048,512]{1,0:T(8,128)(2,1)} custom-call(s32[16,8]{1,0:T(8,128)} %concatenate.9.slot_ref, s32[16,8]{1,0:T(8,128)} %concatenate.10.which_ref, s32[16]{0:T(128)} %dynamic-slice_bitcast_fusion.1.count_ref, bf16[2048,512]{1,0:T(8,128)(2,1)} %bitcast.9.query_ref, bf16[16,128,256]{2,1,0:T(8,128)(2,1)} %copy-done, ...), custom_call_target="tpu_custom_call" | custom-call | tf_op jit(solution)/shard_map/pallas_call | solution.py:64
  269.8 61.0 %all_to_all.25 = bf16[16,128,512]{2,1,0:T(8,128)(2,1)S(1)} all-to-all(bf16[16,128,512]{2,1,0:T(8,128)(2,1)} %bitcast.25), channel_id=1, replica_groups=mesh['seq'=32,'head'=16] {'head'}, dimensions={0} | all-to-all | bytes 4194304 | tf_op jit(solution)/shard_map/all_to_all | solution.py:163
  330.9 2.2 copy.47
  333.0 2.6 reshape.158
  (26 shorter events, 1.1 us)
Async XLA Ops:
  2.4 37.1 %all-to-all-start = ((bf16[16,128,256]{2,1,0:T(8,128)(2,1)}), bf16[16,128,256]{2,1,0:T(8,128)(2,1)S(1)}, u32[]{:S(2)}, u32[]{:S(2)}) async-start(bf16[16,128,256]{2,1,0:T(8,128)(2,1)} %bitcast.6), calls=%async_computation | async-start | bytes 2097152 | tf_op jit(solution)/shard_map/all_to_all | solution.py:130
  39.5 16.2 %copy-start = (bf16[16,128,256]{2,1,0:T(8,128)(2,1)}, bf16[16,128,256]{2,1,0:T(8,128)(2,1)S(1)}, u32[]{:S(2)}) copy-start(bf16[16,128,256]{2,1,0:T(8,128)(2,1)S(1)} %all-to-all-done.own_ref) | copy-start | bytes 3145732
  41.5 63.7 %all-to-all-start.1 = ((bf16[32,128,256]{2,1,0:T(8,128)(2,1)}), bf16[32,128,256]{2,1,0:T(8,128)(2,1)}, u32[]{:S(2)}, u32[]{:S(2)}) async-start(bf16[32,128,256]{2,1,0:T(8,128)(2,1)} %gather_fusion.1), calls=%async_computation.1 | async-start | bytes 4194304 | tf_op jit(solution)/shard_map/all_to_all | solution.py:142
  105.2 55.5 %all-to-all-start.2 = ((bf16[32,128,256]{2,1,0:T(8,128)(2,1)}), bf16[32,128,256]{2,1,0:T(8,128)(2,1)}, u32[]{:S(2)}, u32[]{:S(2)}) async-start(bf16[32,128,256]{2,1,0:T(8,128)(2,1)} %gather_fusion), calls=%async_computation.2 | async-start | bytes 4194304 | tf_op jit(solution)/shard_map/all_to_all | solution.py:142
  110.7 49.9 %collective-permute-start = (bf16[32,128,256]{2,1,0:T(8,128)(2,1)}, bf16[32,128,256]{2,1,0:T(8,128)(2,1)}, u32[]{:S(2)}, u32[]{:S(2)}) collective-permute-start(bf16[32,128,256]{2,1,0:T(8,128)(2,1)} %all-to-all-done.1.mine0_ref), channel_id=1, source_target_pairs={{0,4},{1,5},{2,6},{3,7},{4,0},{5,1},{6,2},{7,3},{8,12},{9,13},{10,... | collective-permute-start | bytes 6291464 | tf_op jit(solution)/shard_map/ppermute | solution.py:144
  160.6 73.9 %all-to-all-start.3 = ((bf16[16,128,512]{2,1,0:T(8,128)(2,1)}), bf16[16,128,512]{2,1,0:T(8,128)(2,1)}, u32[]{:S(2)}, u32[]{:S(2)}) async-start(bf16[16,128,512]{2,1,0:T(8,128)(2,1)} %reshape.152), calls=%async_computation.3 | async-start | bytes 4194304 | tf_op jit(solution)/shard_map/all_to_all | solution.py:149
  165.1 69.4 %collective-permute-start.1 = (bf16[32,128,256]{2,1,0:T(8,128)(2,1)}, bf16[32,128,256]{2,1,0:T(8,128)(2,1)}, u32[]{:S(2)}, u32[]{:S(2)}) collective-permute-start(bf16[32,128,256]{2,1,0:T(8,128)(2,1)} %all-to-all-done.2.mine1_ref), channel_id=1, source_target_pairs={{0,4},{1,5},{2,6},{3,7},{4,0},{5,1},{6,2},{7,3},{8,12},{9,13},{10,... | collective-permute-start | bytes 6291464 | tf_op jit(solution)/shard_map/ppermute | solution.py:144

commit v15 on v13

--- a/solution.py
+++ b/solution.py
@@ -14,46 +14,43 @@
 
 
 def attend_kernel(slot_ref, which_ref, count_ref, query_ref, own_ref, mine0_ref, mine1_ref,
-                  peer0_ref, peer1_ref, out_ref, block_buf, *, score_scale, slot_total, heads):
-    row = pl.program_id(0)
+                  peer0_ref, peer1_ref, out_ref, block_buf, *, score_scale, slot_total, heads,
+                  rows_per_step):
     head_dim = block_buf.shape[1] // 2
-    query = query_ref[...]
-    query = jnp.concatenate(
-        [query[:, h * head_dim:(h + 1) * head_dim] for h in range(heads)], axis=0
-    )
-    row_count = count_ref[row]
     sources = (mine0_ref, mine1_ref, peer0_ref, peer1_ref)
-    block_buf[0:BLK] = own_ref[row]
-    for slot in range(1, slot_total):
-        index = slot_ref[row, slot]
-        which = which_ref[row, slot]
-        for code, source in enumerate(sources):
-            @pl.when(which == code)
-            def _(source=source, slot=slot, index=index):
-                block_buf[slot * BLK:(slot + 1) * BLK] = source[index]
-    def attend(masked):
+    for sub in range(rows_per_step):
+        row = pl.program_id(0) * rows_per_step + sub
+        lines = pl.ds(sub * BLK, BLK)
+        query = query_ref[lines, :]
+        query = jnp.concatenate(
+            [query[:, h * head_dim:(h + 1) * head_dim] for h in range(heads)], axis=0
+        )
+        row_count = count_ref[row]
+        block_buf[0:BLK] = own_ref[row]
+        for slot in range(1, slot_total):
+            index = slot_ref[row, slot]
+            which = which_ref[row, slot]
+            for code, source in enumerate(sources):
+                @pl.when(which == code)
+                def _(source=source, slot=slot, index=index):
+                    block_buf[slot * BLK:(slot + 1) * BLK] = source[index]
         blocks = block_buf[...]
         keys = blocks[:, :head_dim]
         values = blocks[:, head_dim:]
         scores = lax.dot_general(
             query, keys, (((1,), (1,)), ((), ())), preferred_element_type=jnp.float32
         ) * score_scale
-        if masked:
-            key_slot = lax.broadcasted_iota(jnp.int32, (1, slot_total * BLK), 1) // BLK
-            scores = jnp.where(key_slot < row_count, scores, NEG_FILL)
+        key_slot = lax.broadcasted_iota(jnp.int32, (1, slot_total * BLK), 1) // BLK
+        scores = jnp.where(key_slot < row_count, scores, NEG_FILL)
         row_max = jnp.max(scores, axis=1, keepdims=True)
         weights = jnp.exp(scores - row_max)
         inverse = 1.0 / jnp.sum(weights, axis=1, keepdims=True)
         probs = (weights * inverse).astype(jnp.bfloat16)
         acc = jnp.dot(probs, values, preferred_element_type=jnp.float32)
-        tokens = query_ref.shape[0]
         for h in range(heads):
-            out_ref[:, h * head_dim:(h + 1) * head_dim] = acc[
-                h * tokens:(h + 1) * tokens
+            out_ref[lines, h * head_dim:(h + 1) * head_dim] = acc[
+                h * BLK:(h + 1) * BLK
             ].astype(out_ref.dtype)
-
-    pl.when(row_count >= slot_total)(lambda: attend(False))
-    pl.when(row_count < slot_total)(lambda: attend(True))
 
 
 def attend_all(local_queries, column, width, own_blocks, received, slot_index, slot_which,
@@ -62,8 +59,10 @@
     qblocks, _, pair_dim = own_blocks.shape
     head_dim = pair_dim // 2
     slot_total = slot_index.shape[1]
+    rows_per_step = 2
     kernel = partial(
-        attend_kernel, score_scale=score_scale, slot_total=slot_total, heads=width // head_dim
+        attend_kernel, score_scale=score_scale, slot_total=slot_total, heads=width // head_dim,
+        rows_per_step=rows_per_step
     )
     whole = lambda shape: pl.BlockSpec(shape, lambda r, s, w, c: (0,) * len(shape))
     return pl.pallas_call(
@@ -71,13 +70,13 @@
         out_shape=jax.ShapeDtypeStruct((seq_rows, width), local_queries.dtype),
         grid_spec=pltpu.PrefetchScalarGridSpec(
             num_scalar_prefetch=3,
-            grid=(qblocks,),
+            grid=(qblocks // rows_per_step,),
             in_specs=[
-                pl.BlockSpec((BLK, width), lambda r, s, w, c: (r, column)),
+                pl.BlockSpec((rows_per_step * BLK, width), lambda r, s, w, c: (r, column)),
                 whole(own_blocks.shape),
             ]
             + [whole(part.shape) for part in received],
-            out_specs=pl.BlockSpec((BLK, width), lambda r, s, w, c: (r, 0)),
+            out_specs=pl.BlockSpec((rows_per_step * BLK, width), lambda r, s, w, c: (r, 0)),
             scratch_shapes=[pltpu.VMEM((slot_total * BLK, pair_dim), own_blocks.dtype)],
         ),
         compiler_params=pltpu.CompilerParams(vmem_limit_bytes=100 * 1024 * 1024),
@@ -169,7 +168,7 @@
         attended.reshape(head_count, tokens, width), "head", split_axis=0, concat_axis=0,
         tiled=True
     )
-    back = jnp.transpose(back.reshape(2, 2, 4, tokens, group_size, head_dim), (3, 0, 2, 1, 4, 5))
+    back = jnp.transpose(back.reshape(2, 2, 4, tokens, group_size * head_dim), (3, 0, 2, 1, 4))
     return back.reshape(tokens, query_heads, head_dim)
 
 

time: 338 us -> 336 us (level)
  no operation moved by 1% of the time
where the time goes in v15:
time: 336 us; the launch traced here: 335 us
  waiting for transfers between devices  171 us (51%)
  blocking collectives  60.9 us (18%)
  starting transfers between devices  42.6 us (13%)
  Pallas kernels  35 us (10%)
  local copies, waits for them, and re-layouts  20.3 us (6%)
  other arithmetic  5.5 us (2%)
    ppermute x2, waiting for transfers between devices, on_device(): peer.append(lax.ppermute(got, 'head', partner))  106 us
    all_to_all x1, blocking collectives, on_device(): lax.all_to_all(attended.reshape(head_count, tokens, width), 'head', split...  60.9 us
    all_to_all x2, waiting for transfers between devices, on_device(): got = lax.all_to_all(picked, 'seq', split_axis=0, concat_axis=0, tiled=True)  47.4 us
    pallas_call x1, Pallas kernels, attend_all(): pl.pallas_call(kernel, out_shape=jax.ShapeDtypeStruct((seq_rows, width),...  35 us
    all_to_all x2, starting transfers between devices, on_device(): got = lax.all_to_all(picked, 'seq', split_axis=0, concat_axis=0, tiled=True)  19.7 us
    all_to_all x1, waiting for transfers between devices, on_device(): lax.all_to_all(kv, 'head', split_axis=0, concat_axis=0, tiled=True)  17.6 us
    all_to_all x1, starting transfers between devices, on_device(): lax.all_to_all(kv, 'head', split_axis=0, concat_axis=0, tiled=True)  12.9 us
  transfers between devices with their start and end apart: 6, of which 4 were waited for; matrix products, arithmetic and copies ran while one was open for 5% of the time, Pallas kernels for 0%

profile of v15, /device:TPU:16, one launch (start us, length us, event | category | flops | bytes accessed | tf_op | source)
XLA Modules:
  0.0 335.3 jit_solution(10346526705715935734)
XLA Ops:
  0.0 1.1 pad_maximum_fusion
  1.1 0.1 reshape.153
  1.3 1.1 broadcast_in_dim.12
  2.4 12.9 %all-to-all-start = ((bf16[16,128,256]{2,1,0:T(8,128)(2,1)}), bf16[16,128,256]{2,1,0:T(8,128)(2,1)S(1)}, u32[]{:S(2)}, u32[]{:S(2)}) async-start(bf16[16,128,256]{2,1,0:T(8,128)(2,1)} %bitcast.6), calls=%async_computation | async-start | bytes 2097152 | tf_op jit(solution)/shard_map/all_to_all | solution.py:134
  15.3 0.7 dynamic-slice_bitcast_fusion
  16.1 0.1 copy.35
  16.2 0.2 reshape.150
  16.5 0.7 dynamic-slice_reduce_fusion.2
  17.7 3.9 %fusion.3 = s32[32,112]{0,1:T(8,128)S(1)} fusion(s32[32,112]{0,1:T(8,128)S(1)} %get-tuple-element.12, pred[32,112]{0,1:T(8,128)(4,1)S(1)} %get-tuple-element.10), kind=kOutput, calls=%fused_computation.7 | output fusion | flops 13758976 | bytes 32256 | tf_op jit(solution)/shard_map/jit(cumsum)/reduce_window_sum | solution.py:100
  21.7 0.2 multiply_reduce_fusion
  21.9 17.6 %all-to-all-done.own_ref = bf16[16,128,256]{2,1,0:T(8,128)(2,1)S(1)} async-done(((bf16[16,128,256]{2,1,0:T(8,128)(2,1)}), bf16[16,128,256]{2,1,0:T(8,128)(2,1)S(1)}, u32[]{:S(2)}, u32[]{:S(2)}) %all-to-all-start) | async-done | bytes 1048608 | tf_op jit(solution)/shard_map/all_to_all | solution.py:134
  39.5 2.0 gather_fusion.1
  41.5 14.2 %all-to-all-start.1 = ((bf16[32,128,256]{2,1,0:T(8,128)(2,1)}), bf16[32,128,256]{2,1,0:T(8,128)(2,1)}, u32[]{:S(2)}, u32[]{:S(2)}) async-start(bf16[32,128,256]{2,1,0:T(8,128)(2,1)} %gather_fusion.1), calls=%async_computation.1 | async-start | bytes 4194304 | tf_op jit(solution)/shard_map/all_to_all | solution.py:146
  55.7 2.0 gather_fusion
  57.7 47.4 %all-to-all-done.1.mine0_ref = bf16[32,128,256]{2,1,0:T(8,128)(2,1)} async-done(((bf16[32,128,256]{2,1,0:T(8,128)(2,1)}), bf16[32,128,256]{2,1,0:T(8,128)(2,1)}, u32[]{:S(2)}, u32[]{:S(2)}) %all-to-all-start.1) | async-done | bytes 2097184 | tf_op jit(solution)/shard_map/all_to_all | solution.py:146
  105.2 5.5 %all-to-all-start.2 = ((bf16[32,128,256]{2,1,0:T(8,128)(2,1)}), bf16[32,128,256]{2,1,0:T(8,128)(2,1)}, u32[]{:S(2)}, u32[]{:S(2)}) async-start(bf16[32,128,256]{2,1,0:T(8,128)(2,1)} %gather_fusion), calls=%async_computation.2 | async-start | bytes 4194304 | tf_op jit(solution)/shard_map/all_to_all | solution.py:146
  110.7 1.9 collective-permute-start
  112.7 2.6 copy.40
  115.2 2.2 reshape.152
  117.4 43.2 %collective-permute-done.peer0_ref = bf16[32,128,256]{2,1,0:T(8,128)(2,1)} collective-permute-done((bf16[32,128,256]{2,1,0:T(8,128)(2,1)}, bf16[32,128,256]{2,1,0:T(8,128)(2,1)}, u32[]{:S(2)}, u32[]{:S(2)}) %collective-permute-start) | collective-permute-done | bytes 2097184 | tf_op jit(solution)/shard_map/ppermute | solution.py:148
  160.6 4.4 %all-to-all-start.3 = ((bf16[16,128,512]{2,1,0:T(8,128)(2,1)}), bf16[16,128,512]{2,1,0:T(8,128)(2,1)}, u32[]{:S(2)}, u32[]{:S(2)}) async-start(bf16[16,128,512]{2,1,0:T(8,128)(2,1)} %reshape.152), calls=%async_computation.3 | async-start | bytes 4194304 | tf_op jit(solution)/shard_map/all_to_all | solution.py:153
  165.1 3.7 %collective-permute-start.1 = (bf16[32,128,256]{2,1,0:T(8,128)(2,1)}, bf16[32,128,256]{2,1,0:T(8,128)(2,1)}, u32[]{:S(2)}, u32[]{:S(2)}) collective-permute-start(bf16[32,128,256]{2,1,0:T(8,128)(2,1)} %all-to-all-done.2.mine1_ref), channel_id=1, source_target_pairs={{0,4},{1,5},{2,6},{3,7},{4,0},{5,1},{6,2},{7,3},{8,12},{9,13},{10,... | collective-permute-start | bytes 6291464 | tf_op jit(solution)/shard_map/ppermute | solution.py:148
  168.7 0.2 minimum_reduce_fusion
  169.1 0.2 dynamic-slice_reduce_fusion.1
  169.4 0.7 concatenate.10.which_ref
  170.1 0.7 concatenate.9.slot_ref
  170.8 1.3 dynamic-slice_bitcast_fusion.1.count_ref
  172.1 62.4 %collective-permute-done.1.peer1_ref = bf16[32,128,256]{2,1,0:T(8,128)(2,1)} collective-permute-done((bf16[32,128,256]{2,1,0:T(8,128)(2,1)}, bf16[32,128,256]{2,1,0:T(8,128)(2,1)}, u32[]{:S(2)}, u32[]{:S(2)}) %collective-permute-start.1) | collective-permute-done | bytes 2097184 | tf_op jit(solution)/shard_map/ppermute | solution.py:148
  234.5 35.0 %shard_map.55 = bf16[2048,512]{1,0:T(8,128)(2,1)} custom-call(s32[16,8]{1,0:T(8,128)} %concatenate.9.slot_ref, s32[16,8]{1,0:T(8,128)} %concatenate.10.which_ref, s32[16]{0:T(128)} %dynamic-slice_bitcast_fusion.1.count_ref, bf16[2048,512]{1,0:T(8,128)(2,1)} %bitcast.9.query_ref, bf16[16,128,256]{2,1,0:T(8,128)(2,1)} %copy-done, ...), custom_call_target="tpu_custom_call" | custom-call | tf_op jit(solution)/shard_map/pallas_call | solution.py:68
  269.5 60.9 %all_to_all.25 = bf16[16,128,512]{2,1,0:T(8,128)(2,1)S(1)} all-to-all(bf16[16,128,512]{2,1,0:T(8,128)(2,1)} %bitcast.25), channel_id=1, replica_groups=mesh['seq'=32,'head'=16] {'head'}, dimensions={0} | all-to-all | bytes 4194304 | tf_op jit(solution)/shard_map/all_to_all | solution.py:167
  330.5 2.2 copy.47
  332.6 2.6 reshape.158
  (26 shorter events, 1.1 us)
Async XLA Ops:
  2.4 37.1 %all-to-all-start = ((bf16[16,128,256]{2,1,0:T(8,128)(2,1)}), bf16[16,128,256]{2,1,0:T(8,128)(2,1)S(1)}, u32[]{:S(2)}, u32[]{:S(2)}) async-start(bf16[16,128,256]{2,1,0:T(8,128)(2,1)} %bitcast.6), calls=%async_computation | async-start | bytes 2097152 | tf_op jit(solution)/shard_map/all_to_all | solution.py:134
  39.5 16.2 %copy-start = (bf16[16,128,256]{2,1,0:T(8,128)(2,1)}, bf16[16,128,256]{2,1,0:T(8,128)(2,1)S(1)}, u32[]{:S(2)}) copy-start(bf16[16,128,256]{2,1,0:T(8,128)(2,1)S(1)} %all-to-all-done.own_ref) | copy-start | bytes 3145732
  41.5 63.7 %all-to-all-start.1 = ((bf16[32,128,256]{2,1,0:T(8,128)(2,1)}), bf16[32,128,256]{2,1,0:T(8,128)(2,1)}, u32[]{:S(2)}, u32[]{:S(2)}) async-start(bf16[32,128,256]{2,1,0:T(8,128)(2,1)} %gather_fusion.1), calls=%async_computation.1 | async-start | bytes 4194304 | tf_op jit(solution)/shard_map/all_to_all | solution.py:146
  105.2 55.5 %all-to-all-start.2 = ((bf16[32,128,256]{2,1,0:T(8,128)(2,1)}), bf16[32,128,256]{2,1,0:T(8,128)(2,1)}, u32[]{:S(2)}, u32[]{:S(2)}) async-start(bf16[32,128,256]{2,1,0:T(8,128)(2,1)} %gather_fusion), calls=%async_computation.2 | async-start | bytes 4194304 | tf_op jit(solution)/shard_map/all_to_all | solution.py:146
  110.7 49.9 %collective-permute-start = (bf16[32,128,256]{2,1,0:T(8,128)(2,1)}, bf16[32,128,256]{2,1,0:T(8,128)(2,1)}, u32[]{:S(2)}, u32[]{:S(2)}) collective-permute-start(bf16[32,128,256]{2,1,0:T(8,128)(2,1)} %all-to-all-done.1.mine0_ref), channel_id=1, source_target_pairs={{0,4},{1,5},{2,6},{3,7},{4,0},{5,1},{6,2},{7,3},{8,12},{9,13},{10,... | collective-permute-start | bytes 6291464 | tf_op jit(solution)/shard_map/ppermute | solution.py:148
  160.6 73.9 %all-to-all-start.3 = ((bf16[16,128,512]{2,1,0:T(8,128)(2,1)}), bf16[16,128,512]{2,1,0:T(8,128)(2,1)}, u32[]{:S(2)}, u32[]{:S(2)}) async-start(bf16[16,128,512]{2,1,0:T(8,128)(2,1)} %reshape.152), calls=%async_computation.3 | async-start | bytes 4194304 | tf_op jit(solution)/shard_map/all_to_all | solution.py:153
  165.1 69.4 %collective-permute-start.1 = (bf16[32,128,256]{2,1,0:T(8,128)(2,1)}, bf16[32,128,256]{2,1,0:T(8,128)(2,1)}, u32[]{:S(2)}, u32[]{:S(2)}) collective-permute-start(bf16[32,128,256]{2,1,0:T(8,128)(2,1)} %all-to-all-done.2.mine1_ref), channel_id=1, source_target_pairs={{0,4},{1,5},{2,6},{3,7},{4,0},{5,1},{6,2},{7,3},{8,12},{9,13},{10,... | collective-permute-start | bytes 6291464 | tf_op jit(solution)/shard_map/ppermute | solution.py:148

commit v16 on v15

--- a/solution.py
+++ b/solution.py
@@ -59,7 +59,7 @@
     qblocks, _, pair_dim = own_blocks.shape
     head_dim = pair_dim // 2
     slot_total = slot_index.shape[1]
-    rows_per_step = 2
+    rows_per_step = 4
     kernel = partial(
         attend_kernel, score_scale=score_scale, slot_total=slot_total, heads=width // head_dim,
         rows_per_step=rows_per_step

time: 336 us -> 336 us (level)
  no operation moved by 1% of the time
where the time goes in v16:
time: 336 us; the launch traced here: 335 us
  waiting for transfers between devices  170 us (51%)
  blocking collectives  61 us (18%)
  starting transfers between devices  42.8 us (13%)
  Pallas kernels  35.1 us (10%)
  local copies, waits for them, and re-layouts  20.3 us (6%)
  other arithmetic  5.5 us (2%)
    ppermute x2, waiting for transfers between devices, on_device(): peer.append(lax.ppermute(got, 'head', partner))  105 us
    all_to_all x1, blocking collectives, on_device(): lax.all_to_all(attended.reshape(head_count, tokens, width), 'head', split...  61 us
    all_to_all x2, waiting for transfers between devices, on_device(): got = lax.all_to_all(picked, 'seq', split_axis=0, concat_axis=0, tiled=True)  47.4 us
    pallas_call x1, Pallas kernels, attend_all(): pl.pallas_call(kernel, out_shape=jax.ShapeDtypeStruct((seq_rows, width),...  35.1 us
    all_to_all x2, starting transfers between devices, on_device(): got = lax.all_to_all(picked, 'seq', split_axis=0, concat_axis=0, tiled=True)  19.7 us
    all_to_all x1, waiting for transfers between devices, on_device(): lax.all_to_all(kv, 'head', split_axis=0, concat_axis=0, tiled=True)  17.6 us
    all_to_all x1, starting transfers between devices, on_device(): lax.all_to_all(kv, 'head', split_axis=0, concat_axis=0, tiled=True)  12.9 us
  transfers between devices with their start and end apart: 6, of which 4 were waited for; matrix products, arithmetic and copies ran while one was open for 5% of the time, Pallas kernels for 0%

profile of v16, /device:TPU:16, one launch (start us, length us, event | category | flops | bytes accessed | tf_op | source)
XLA Modules:
  0.0 335.4 jit_solution(2193640335777411827)
XLA Ops:
  0.0 1.1 pad_maximum_fusion
  1.1 0.1 reshape.153
  1.3 1.1 broadcast_in_dim.12
  2.4 12.9 %all-to-all-start = ((bf16[16,128,256]{2,1,0:T(8,128)(2,1)}), bf16[16,128,256]{2,1,0:T(8,128)(2,1)S(1)}, u32[]{:S(2)}, u32[]{:S(2)}) async-start(bf16[16,128,256]{2,1,0:T(8,128)(2,1)} %bitcast.6), calls=%async_computation | async-start | bytes 2097152 | tf_op jit(solution)/shard_map/all_to_all | solution.py:134
  15.3 0.7 dynamic-slice_bitcast_fusion
  16.1 0.1 copy.35
  16.2 0.2 reshape.150
  16.5 0.7 dynamic-slice_reduce_fusion.2
  17.7 3.9 %fusion.3 = s32[32,112]{0,1:T(8,128)S(1)} fusion(s32[32,112]{0,1:T(8,128)S(1)} %get-tuple-element.12, pred[32,112]{0,1:T(8,128)(4,1)S(1)} %get-tuple-element.10), kind=kOutput, calls=%fused_computation.7 | output fusion | flops 13758976 | bytes 32256 | tf_op jit(solution)/shard_map/jit(cumsum)/reduce_window_sum | solution.py:100
  21.7 0.2 multiply_reduce_fusion
  21.9 17.6 %all-to-all-done.own_ref = bf16[16,128,256]{2,1,0:T(8,128)(2,1)S(1)} async-done(((bf16[16,128,256]{2,1,0:T(8,128)(2,1)}), bf16[16,128,256]{2,1,0:T(8,128)(2,1)S(1)}, u32[]{:S(2)}, u32[]{:S(2)}) %all-to-all-start) | async-done | bytes 1048608 | tf_op jit(solution)/shard_map/all_to_all | solution.py:134
  39.5 2.0 gather_fusion.1
  41.5 14.2 %all-to-all-start.1 = ((bf16[32,128,256]{2,1,0:T(8,128)(2,1)}), bf16[32,128,256]{2,1,0:T(8,128)(2,1)}, u32[]{:S(2)}, u32[]{:S(2)}) async-start(bf16[32,128,256]{2,1,0:T(8,128)(2,1)} %gather_fusion.1), calls=%async_computation.1 | async-start | bytes 4194304 | tf_op jit(solution)/shard_map/all_to_all | solution.py:146
  55.7 2.0 gather_fusion
  57.7 47.4 %all-to-all-done.1.mine0_ref = bf16[32,128,256]{2,1,0:T(8,128)(2,1)} async-done(((bf16[32,128,256]{2,1,0:T(8,128)(2,1)}), bf16[32,128,256]{2,1,0:T(8,128)(2,1)}, u32[]{:S(2)}, u32[]{:S(2)}) %all-to-all-start.1) | async-done | bytes 2097184 | tf_op jit(solution)/shard_map/all_to_all | solution.py:146
  105.2 5.5 %all-to-all-start.2 = ((bf16[32,128,256]{2,1,0:T(8,128)(2,1)}), bf16[32,128,256]{2,1,0:T(8,128)(2,1)}, u32[]{:S(2)}, u32[]{:S(2)}) async-start(bf16[32,128,256]{2,1,0:T(8,128)(2,1)} %gather_fusion), calls=%async_computation.2 | async-start | bytes 4194304 | tf_op jit(solution)/shard_map/all_to_all | solution.py:146
  110.7 1.9 collective-permute-start
  112.7 2.6 copy.40
  115.2 2.2 reshape.152
  117.4 43.2 %collective-permute-done.peer0_ref = bf16[32,128,256]{2,1,0:T(8,128)(2,1)} collective-permute-done((bf16[32,128,256]{2,1,0:T(8,128)(2,1)}, bf16[32,128,256]{2,1,0:T(8,128)(2,1)}, u32[]{:S(2)}, u32[]{:S(2)}) %collective-permute-start) | collective-permute-done | bytes 2097184 | tf_op jit(solution)/shard_map/ppermute | solution.py:148
  160.6 4.4 %all-to-all-start.3 = ((bf16[16,128,512]{2,1,0:T(8,128)(2,1)}), bf16[16,128,512]{2,1,0:T(8,128)(2,1)}, u32[]{:S(2)}, u32[]{:S(2)}) async-start(bf16[16,128,512]{2,1,0:T(8,128)(2,1)} %reshape.152), calls=%async_computation.3 | async-start | bytes 4194304 | tf_op jit(solution)/shard_map/all_to_all | solution.py:153
  165.1 3.8 %collective-permute-start.1 = (bf16[32,128,256]{2,1,0:T(8,128)(2,1)}, bf16[32,128,256]{2,1,0:T(8,128)(2,1)}, u32[]{:S(2)}, u32[]{:S(2)}) collective-permute-start(bf16[32,128,256]{2,1,0:T(8,128)(2,1)} %all-to-all-done.2.mine1_ref), channel_id=1, source_target_pairs={{0,4},{1,5},{2,6},{3,7},{4,0},{5,1},{6,2},{7,3},{8,12},{9,13},{10,... | collective-permute-start | bytes 6291464 | tf_op jit(solution)/shard_map/ppermute | solution.py:148
  168.9 0.2 minimum_reduce_fusion
  169.3 0.2 dynamic-slice_reduce_fusion.1
  169.6 0.7 concatenate.10.which_ref
  170.3 0.7 concatenate.9.slot_ref
  171.0 1.3 dynamic-slice_bitcast_fusion.1.count_ref
  172.3 62.2 %collective-permute-done.1.peer1_ref = bf16[32,128,256]{2,1,0:T(8,128)(2,1)} collective-permute-done((bf16[32,128,256]{2,1,0:T(8,128)(2,1)}, bf16[32,128,256]{2,1,0:T(8,128)(2,1)}, u32[]{:S(2)}, u32[]{:S(2)}) %collective-permute-start.1) | collective-permute-done | bytes 2097184 | tf_op jit(solution)/shard_map/ppermute | solution.py:148
  234.5 35.1 %shard_map.55 = bf16[2048,512]{1,0:T(8,128)(2,1)} custom-call(s32[16,8]{1,0:T(8,128)} %concatenate.9.slot_ref, s32[16,8]{1,0:T(8,128)} %concatenate.10.which_ref, s32[16]{0:T(128)} %dynamic-slice_bitcast_fusion.1.count_ref, bf16[2048,512]{1,0:T(8,128)(2,1)} %bitcast.9.query_ref, bf16[16,128,256]{2,1,0:T(8,128)(2,1)} %copy-done, ...), custom_call_target="tpu_custom_call" | custom-call | tf_op jit(solution)/shard_map/pallas_call | solution.py:68
  269.6 61.0 %all_to_all.25 = bf16[16,128,512]{2,1,0:T(8,128)(2,1)S(1)} all-to-all(bf16[16,128,512]{2,1,0:T(8,128)(2,1)} %bitcast.25), channel_id=1, replica_groups=mesh['seq'=32,'head'=16] {'head'}, dimensions={0} | all-to-all | bytes 4194304 | tf_op jit(solution)/shard_map/all_to_all | solution.py:167
  330.6 2.2 copy.47
  332.8 2.6 reshape.158
  (26 shorter events, 1.1 us)
Async XLA Ops:
  2.4 37.1 %all-to-all-start = ((bf16[16,128,256]{2,1,0:T(8,128)(2,1)}), bf16[16,128,256]{2,1,0:T(8,128)(2,1)S(1)}, u32[]{:S(2)}, u32[]{:S(2)}) async-start(bf16[16,128,256]{2,1,0:T(8,128)(2,1)} %bitcast.6), calls=%async_computation | async-start | bytes 2097152 | tf_op jit(solution)/shard_map/all_to_all | solution.py:134
  39.5 16.2 %copy-start = (bf16[16,128,256]{2,1,0:T(8,128)(2,1)}, bf16[16,128,256]{2,1,0:T(8,128)(2,1)S(1)}, u32[]{:S(2)}) copy-start(bf16[16,128,256]{2,1,0:T(8,128)(2,1)S(1)} %all-to-all-done.own_ref) | copy-start | bytes 3145732
  41.5 63.7 %all-to-all-start.1 = ((bf16[32,128,256]{2,1,0:T(8,128)(2,1)}), bf16[32,128,256]{2,1,0:T(8,128)(2,1)}, u32[]{:S(2)}, u32[]{:S(2)}) async-start(bf16[32,128,256]{2,1,0:T(8,128)(2,1)} %gather_fusion.1), calls=%async_computation.1 | async-start | bytes 4194304 | tf_op jit(solution)/shard_map/all_to_all | solution.py:146
  105.2 55.5 %all-to-all-start.2 = ((bf16[32,128,256]{2,1,0:T(8,128)(2,1)}), bf16[32,128,256]{2,1,0:T(8,128)(2,1)}, u32[]{:S(2)}, u32[]{:S(2)}) async-start(bf16[32,128,256]{2,1,0:T(8,128)(2,1)} %gather_fusion), calls=%async_computation.2 | async-start | bytes 4194304 | tf_op jit(solution)/shard_map/all_to_all | solution.py:146
  110.7 49.9 %collective-permute-start = (bf16[32,128,256]{2,1,0:T(8,128)(2,1)}, bf16[32,128,256]{2,1,0:T(8,128)(2,1)}, u32[]{:S(2)}, u32[]{:S(2)}) collective-permute-start(bf16[32,128,256]{2,1,0:T(8,128)(2,1)} %all-to-all-done.1.mine0_ref), channel_id=1, source_target_pairs={{0,4},{1,5},{2,6},{3,7},{4,0},{5,1},{6,2},{7,3},{8,12},{9,13},{10,... | collective-permute-start | bytes 6291464 | tf_op jit(solution)/shard_map/ppermute | solution.py:148
  160.6 73.9 %all-to-all-start.3 = ((bf16[16,128,512]{2,1,0:T(8,128)(2,1)}), bf16[16,128,512]{2,1,0:T(8,128)(2,1)}, u32[]{:S(2)}, u32[]{:S(2)}) async-start(bf16[16,128,512]{2,1,0:T(8,128)(2,1)} %reshape.152), calls=%async_computation.3 | async-start | bytes 4194304 | tf_op jit(solution)/shard_map/all_to_all | solution.py:153
  165.1 69.4 %collective-permute-start.1 = (bf16[32,128,256]{2,1,0:T(8,128)(2,1)}, bf16[32,128,256]{2,1,0:T(8,128)(2,1)}, u32[]{:S(2)}, u32[]{:S(2)}) collective-permute-start(bf16[32,128,256]{2,1,0:T(8,128)(2,1)} %all-to-all-done.2.mine1_ref), channel_id=1, source_target_pairs={{0,4},{1,5},{2,6},{3,7},{4,0},{5,1},{6,2},{7,3},{8,12},{9,13},{10,... | collective-permute-start | bytes 6291464 | tf_op jit(solution)/shard_map/ppermute | solution.py:148
